TPU v7x, 128 devices: a whole 4x4x4 slice. The times are simulated.
128 devices in a mesh: dp: 32 (over x, z_hi, y), tensor: 4 (over z_lo, core).
Axes of the slice: x: 4, y: 4, z: 4 (z_hi: 2, z_lo: 2; z = z_hi * 2 + z_lo), core: 2. Of those that a mesh axis runs over, the one named last changes fastest.
Arguments:
- tokens: bfloat16 [65536, 1024], P(('dp', 'tensor')), may hold values from -16 to 16
- prompts: bfloat16 [32, 64, 1024], P('dp'), may hold values from -6 to 6
- w_attn: bfloat16 [3, 1024, 1024], P(None, None, 'tensor'), may hold values from -0.1875 to 0.1875
- w_out: bfloat16 [1024, 1024], P('tensor'), may hold values from -0.1875 to 0.1875
- norm_gain: float32 [2, 1024], replicated, may hold values from 0.1 to 1.9
- norm_bias: float32 [2, 1024], replicated, may hold values from -3 to 3
- w_in: bfloat16 [1024, 4096], P(None, 'tensor'), may hold values from -0.1875 to 0.1875
- b_in: float32 [4096], P('tensor'), may hold values from -3 to 3
- w_down: bfloat16 [4096, 1024], P('tensor'), may hold values from -0.09375 to 0.09375
- index_rows: bfloat16 [65536, 1024], P('dp'), may hold values from -6 to 6
- lengths: int32 [32, 32], P('dp'), may hold values from 1 to 512, 2048 in all within a row
- groups: int32 [1024], P('dp'), may hold values from 0 to 31
- candidates: int32 [1024, 64], P(('dp', 'tensor')), may hold values from 0 to 65535
Outputs:
- scores: float32 [1024, 64], P(('dp', 'tensor'))
All inputs are finite; a program needn't handle non-finite values.
Results may differ from a plain program's by a relative error of at most 0.01.
Values may be sent and summed in bfloat16 or wider, within the bound.
No kernel may reach another device: no remote copies, remote signals or barrier semaphores. Data moves between devices by JAX's collectives and lax.ppermute only.
A program may use at most 128 MiB of HBM per device.

v0:
```python
import jax
import jax.numpy as jnp
from jax import lax
from jax.sharding import PartitionSpec as P

D = 1024
HEAD_DIM = 64


def layer_norm(values, gain, bias):
    mean = jnp.mean(values, axis=-1, keepdims=True)
    centred = values - mean
    var = jnp.mean(centred * centred, axis=-1, keepdims=True)
    return centred * lax.rsqrt(var + 1e-05) * gain + bias


def project(block, weight):
    return jnp.dot(block, weight, preferred_element_type=jnp.float32).astype(jnp.bfloat16)


def shards(
    tokens,
    prompts,
    w_attn,
    w_out,
    norm_gain,
    norm_bias,
    w_in,
    b_in,
    w_down,
    index_rows,
    lengths,
    groups,
    candidates,
):
    shard_rows = tokens.shape[0]
    tok_dev = shard_rows * lax.axis_size("tensor")
    columns = w_attn.shape[2]
    heads_here = columns // HEAD_DIM
    scale = HEAD_DIM ** (-0.5)
    whole = lax.all_gather(tokens, "tensor", axis=0, tiled=True)
    query = (jnp.dot(whole, w_attn[0], preferred_element_type=jnp.float32) * scale).astype(
        jnp.bfloat16
    )
    keys = project(whole, w_attn[1])
    values = project(whole, w_attn[2])
    every_prompt = lax.all_gather(prompts, "dp", axis=0, tiled=True)
    flat = every_prompt.reshape(-1, every_prompt.shape[2])
    prompt_key = project(flat, w_attn[1])
    prompt_value = project(flat, w_attn[2])
    prompt_len = prompts.shape[1]
    prompt_rows = prompt_key.shape[0]
    lens = lengths[0]
    texts_here = lens.shape[0]
    text_ids = jnp.arange(texts_here, dtype=jnp.int32)
    ends = jnp.cumsum(lens)
    position = jnp.arange(tok_dev, dtype=jnp.int32)
    seg = jnp.sum((position[:, None] >= ends[None, :]).astype(jnp.int32), axis=1)
    tok_group = jnp.sum(jnp.where(seg[:, None] == text_ids[None, :], groups[None, :], 0), axis=1)
    key_group = jnp.arange(prompt_rows, dtype=jnp.int32) // prompt_len
    all_keys = jnp.concatenate([keys, prompt_key], axis=0).reshape(-1, heads_here, HEAD_DIM)
    all_values = jnp.concatenate([values, prompt_value], axis=0).reshape(-1, heads_here, HEAD_DIM)
    block = min(512, tok_dev)

    def attend(number):
        start = number * block
        q_block = lax.dynamic_slice_in_dim(query, start, block, 0).reshape(
            block, heads_here, HEAD_DIM
        )
        seg_block = lax.dynamic_slice_in_dim(seg, start, block, 0)
        group_block = lax.dynamic_slice_in_dim(tok_group, start, block, 0)
        allowed = jnp.concatenate(
            [seg_block[:, None] == seg[None, :], group_block[:, None] == key_group[None, :]], axis=1
        )
        logits = jnp.einsum("qhe,khe->hqk", q_block, all_keys, preferred_element_type=jnp.float32)
        logits = jnp.where(allowed[None], logits, jnp.float32(-1e30))
        top = jnp.max(logits, axis=2, keepdims=True)
        weights = jnp.exp(logits - top)
        total = jnp.sum(weights, axis=2, keepdims=True)
        probs = (weights / total).astype(jnp.bfloat16)
        mixed = jnp.einsum("hqk,khe->qhe", probs, all_values, preferred_element_type=jnp.float32)
        return mixed.astype(jnp.bfloat16).reshape(block, columns)

    context = lax.map(attend, jnp.arange(tok_dev // block, dtype=jnp.int32)).reshape(
        tok_dev, columns
    )
    my_start = lax.axis_index("tensor") * shard_rows
    attn_part = lax.psum_scatter(
        jnp.dot(context, w_out, preferred_element_type=jnp.float32),
        "tensor",
        scatter_dimension=0,
        tiled=True,
    )
    normed_rows = layer_norm(
        tokens.astype(jnp.float32) + attn_part, norm_gain[0], norm_bias[0]
    ).astype(jnp.bfloat16)
    expanded = jax.nn.gelu(
        jnp.dot(
            lax.all_gather(normed_rows, "tensor", axis=0, tiled=True),
            w_in,
            preferred_element_type=jnp.float32,
        )
        + b_in,
        approximate=False,
    ).astype(jnp.bfloat16)
    reduced = lax.psum_scatter(
        jnp.dot(expanded, w_down, preferred_element_type=jnp.float32).astype(jnp.bfloat16),
        "tensor",
        scatter_dimension=0,
        tiled=True,
    ).astype(jnp.float32)
    output = layer_norm(
        normed_rows.astype(jnp.float32) + reduced, norm_gain[1], norm_bias[1]
    ).astype(jnp.bfloat16)
    seg_rows = lax.dynamic_slice_in_dim(seg, my_start, shard_rows, 0)
    member = (text_ids[:, None] == seg_rows[None, :]).astype(jnp.bfloat16)
    partial_sums = jnp.dot(member, output, preferred_element_type=jnp.float32)
    pooled_sums = lax.psum_scatter(partial_sums, "tensor", scatter_dimension=0, tiled=True)
    mine = pooled_sums.shape[0]
    my_lens = lax.dynamic_slice_in_dim(lens, lax.axis_index("tensor") * mine, mine, 0)
    pooled = pooled_sums / my_lens[:, None].astype(jnp.float32)
    square = jnp.mean(pooled * pooled, axis=1, keepdims=True)
    embedding = (pooled * lax.rsqrt(square + 1e-06)).astype(jnp.bfloat16)
    asked_vectors, asked_rows = (
        lax.all_gather(embedding, "dp", axis=0, tiled=True),
        lax.all_gather(candidates, "dp", axis=0, tiled=True),
    )
    held = index_rows.shape[0]
    local_rows = asked_rows - lax.axis_index("dp") * held
    owned = (local_rows >= 0) & (local_rows < held)
    table = jnp.dot(asked_vectors, index_rows.T, preferred_element_type=jnp.float32) * D ** (-0.5)
    picked = jnp.take_along_axis(table, jnp.clip(local_rows, 0, held - 1), axis=1)
    picked = jnp.where(owned, picked, jnp.float32(0.0))
    return lax.psum_scatter(
        picked.astype(jnp.bfloat16), "dp", scatter_dimension=0, tiled=True
    ).astype(jnp.float32)


def solution(mesh):
    placed = (
        P(("dp", "tensor"), None),
        P("dp", None, None),
        P(None, None, "tensor"),
        P("tensor", None),
        P(),
        P(),
        P(None, "tensor"),
        P("tensor"),
        P("tensor", None),
        P("dp", None),
        P("dp", None),
        P("dp"),
        P(("dp", "tensor"), None),
    )
    return jax.shard_map(
        shards, mesh=mesh, in_specs=placed, out_specs=P(("dp", "tensor"), None), check_vma=False
    )
```

profile of v0, /device:TPU:0, one launch (start us, length us, event | category | flops | bytes accessed | tf_op | source)
XLA Modules:
  0.0 1021.1 jit_solution(8762261364968548644)
XLA Ops:
  9.9 47.5 %all-gather.4.cloned.1.call-done = bf16[2048,1024]{1,0:T(8,128)(2,1)} async-done(((bf16[512,1024]{1,0:T(8,128)(2,1)}), bf16[2048,1024]{1,0:T(8,128)(2,1)}) %all-gather.4.cloned.1.call-update) | async-done | bytes 4194320 | tf_op jit(solution)/shard_map/all_gather | solution.py:41
  57.4 3.7 convolution_convert_fusion.1
  61.5 2.3 convolution_convert_fusion.3
  63.7 2.3 fusion.48
  66.1 78.2 %all-gather.6.cloned.1.call-done = bf16[32,64,1024]{2,1,0:T(8,128)(2,1)} async-done(((bf16[1,64,1024]{2,1,0:T(8,128)(2,1)}), bf16[32,64,1024]{2,1,0:T(8,128)(2,1)}) %all-gather.6.cloned.1.call-update) | async-done | bytes 4194320 | tf_op jit(solution)/shard_map/all_gather | solution.py:47
  144.3 4.7 convolution_convert_fusion
  149.0 2.4 convolution_convert_fusion.2
  152.9 4.1 copy.29
  157.0 2.7 pad_maximum_fusion.1
  159.7 4.1 copy.30
  163.8 158.4 %while.11 = (s32[]{:T(128)}, bf16[4,512,256]{2,1,0:T(8,128)(2,1)}, s32[4]{0:T(128)S(1)}, s32[2048]{0:T(1024)S(1)}, s32[2048]{0:T(1024)S(1)}, /*index=5*/bf16[204...) while((s32[]{:T(128)}, bf16[4,512,256]{2,1,0:T(8,128)(2,1)}, ...), condition=%wide.region_6.7_spmd.clone, body=%wide.region_3.6_spmd.clone.sunk | while | flops 3284297728 | bytes 19714248 | solution.py:84
  169.6 14.5 %fusion.133 = f32[4,512]{1,0:T(4,128)S(1)} fusion(pred[512,4096]{1,0:T(8,128)(4,1)} %pad_add_fusion.2, bf16[512,4,64]{0,2,1:T(8,128)(2,1)S(1)} %bitcast.71, bf16[4096,4,64]{0,2,1:T(8,128)(2,1)} %get-tuple-element.208), kind=kOutput, calls=%fused_computation.127.clone.1 | convolution fusion | flops 1098911744 | bytes 4464640 | tf_op jit(solution)/shard_map/while/body/eval_jaxpr/sub | solution.py:78
  184.0 16.2 %fusion.134 = bf16[4,512,64]{1,2,0:T(8,128)(2,1)S(1)} fusion(bf16[4096,4,64]{0,2,1:T(8,128)(2,1)} %get-tuple-element.209, f32[4,512]{1,0:T(4,128)S(1)} %fusion.133, pred[512,4096]{1,0:T(8,128)(4,1)} %pad_add_fusion.2, bf16[512,4,64]{0,2,1:T(8,128)(2,1)S(1)} %bitcast.72, bf16[4096,4,64]{0,2,1:T(8,128)(2,1)} %get-tuple-element.208), kind=kOutput, calls=%fused_computation.14.clone.1 | convolution fusion | flops 2181175296 | bytes 6823936 | tf_op jit(solution)/shard_map/while/body/eval_jaxpr/hqk,khe->qhe/dot_general | solution.py:81
  206.5 14.5 %fusion.133 = f32[4,512]{1,0:T(4,128)S(1)} fusion(pred[512,4096]{1,0:T(8,128)(4,1)} %pad_add_fusion.2, bf16[512,4,64]{0,2,1:T(8,128)(2,1)S(1)} %bitcast.71, bf16[4096,4,64]{0,2,1:T(8,128)(2,1)} %get-tuple-element.208), kind=kOutput, calls=%fused_computation.127.clone.1 | convolution fusion | flops 1098911744 | bytes 4464640 | tf_op jit(solution)/shard_map/while/body/eval_jaxpr/sub | solution.py:78
  221.0 16.2 %fusion.134 = bf16[4,512,64]{1,2,0:T(8,128)(2,1)S(1)} fusion(bf16[4096,4,64]{0,2,1:T(8,128)(2,1)} %get-tuple-element.209, f32[4,512]{1,0:T(4,128)S(1)} %fusion.133, pred[512,4096]{1,0:T(8,128)(4,1)} %pad_add_fusion.2, bf16[512,4,64]{0,2,1:T(8,128)(2,1)S(1)} %bitcast.72, bf16[4096,4,64]{0,2,1:T(8,128)(2,1)} %get-tuple-element.208), kind=kOutput, calls=%fused_computation.14.clone.1 | convolution fusion | flops 2181175296 | bytes 6823936 | tf_op jit(solution)/shard_map/while/body/eval_jaxpr/hqk,khe->qhe/dot_general | solution.py:81
  243.5 14.5 %fusion.133 = f32[4,512]{1,0:T(4,128)S(1)} fusion(pred[512,4096]{1,0:T(8,128)(4,1)} %pad_add_fusion.2, bf16[512,4,64]{0,2,1:T(8,128)(2,1)S(1)} %bitcast.71, bf16[4096,4,64]{0,2,1:T(8,128)(2,1)} %get-tuple-element.208), kind=kOutput, calls=%fused_computation.127.clone.1 | convolution fusion | flops 1098911744 | bytes 4464640 | tf_op jit(solution)/shard_map/while/body/eval_jaxpr/sub | solution.py:78
  258.0 16.2 %fusion.134 = bf16[4,512,64]{1,2,0:T(8,128)(2,1)S(1)} fusion(bf16[4096,4,64]{0,2,1:T(8,128)(2,1)} %get-tuple-element.209, f32[4,512]{1,0:T(4,128)S(1)} %fusion.133, pred[512,4096]{1,0:T(8,128)(4,1)} %pad_add_fusion.2, bf16[512,4,64]{0,2,1:T(8,128)(2,1)S(1)} %bitcast.72, bf16[4096,4,64]{0,2,1:T(8,128)(2,1)} %get-tuple-element.208), kind=kOutput, calls=%fused_computation.14.clone.1 | convolution fusion | flops 2181175296 | bytes 6823936 | tf_op jit(solution)/shard_map/while/body/eval_jaxpr/hqk,khe->qhe/dot_general | solution.py:81
  280.5 14.5 %fusion.133 = f32[4,512]{1,0:T(4,128)S(1)} fusion(pred[512,4096]{1,0:T(8,128)(4,1)} %pad_add_fusion.2, bf16[512,4,64]{0,2,1:T(8,128)(2,1)S(1)} %bitcast.71, bf16[4096,4,64]{0,2,1:T(8,128)(2,1)} %get-tuple-element.208), kind=kOutput, calls=%fused_computation.127.clone.1 | convolution fusion | flops 1098911744 | bytes 4464640 | tf_op jit(solution)/shard_map/while/body/eval_jaxpr/sub | solution.py:78
  295.0 16.2 %fusion.134 = bf16[4,512,64]{1,2,0:T(8,128)(2,1)S(1)} fusion(bf16[4096,4,64]{0,2,1:T(8,128)(2,1)} %get-tuple-element.209, f32[4,512]{1,0:T(4,128)S(1)} %fusion.133, pred[512,4096]{1,0:T(8,128)(4,1)} %pad_add_fusion.2, bf16[512,4,64]{0,2,1:T(8,128)(2,1)S(1)} %bitcast.72, bf16[4096,4,64]{0,2,1:T(8,128)(2,1)} %get-tuple-element.208), kind=kOutput, calls=%fused_computation.14.clone.1 | convolution fusion | flops 2181175296 | bytes 6823936 | tf_op jit(solution)/shard_map/while/body/eval_jaxpr/hqk,khe->qhe/dot_general | solution.py:81
  322.1 5.8 fusion.97
  328.7 75.2 %reduce-scatter.4.cloned.1.call-done = f32[512,1024]{1,0:T(8,128)} async-done(((f32[2048,1024]{1,0:T(8,128)}), f32[512,1024]{1,0:T(8,128)}) %reduce-scatter.4.cloned.1.call-update) | async-done | bytes 2097168 | tf_op jit(solution)/shard_map/reduce_scatter | solution.py:88
  403.9 2.0 fusion.52
  408.3 46.9 %all-gather.8.cloned.1.call-done = bf16[2048,1024]{1,0:T(8,128)(2,1)} async-done(((bf16[512,1024]{1,0:T(8,128)(2,1)}), bf16[2048,1024]{1,0:T(8,128)(2,1)}) %all-gather.8.cloned.1.call-update) | async-done | bytes 4194320 | tf_op jit(solution)/shard_map/all_gather | solution.py:99
  455.3 28.5 %fusion.43 = bf16[2048,1024]{1,0:T(8,128)(2,1)} fusion(bf16[1024,1024]{1,0:T(8,128)(2,1)S(1)} %copy-done, f32[1024]{0:T(1024)S(1)} %copy-done.13, bf16[2048,1024]{1,0:T(8,128)(2,1)} %all-gather.8.cloned.1.call-done, bf16[1024,1024]{1,0:T(8,128)(2,1)} %param.21), kind=kOutput, calls=%fused_computation.47 | convolution fusion | flops 8730443776 | bytes 12587008 | tf_op jit(solution)/shard_map/dot_general | solution.py:107
  484.5 95.9 %all_gather.15 = s32[256,64]{1,0:T(8,128)S(1)} all-gather(s32[8,64]{1,0:T(8,128)S(1)} %copy-done.8), channel_id=1, replica_groups=mesh['dp'=32,'tensor'=4] {'dp'}, dimensions={0}, use_global_device_ids=true | all-gather | bytes 67584 | tf_op jit(solution)/shard_map/all_gather | solution.py:126
  580.4 1.7 fusion.50
  582.1 1.7 multiply_reduce_fusion
  586.7 9.1 reduce-scatter.8.cloned.1.call-done
  597.6 97.2 %all_gather.19 = bf16[256,1024]{1,0:T(8,128)(2,1)S(1)} all-gather(bf16[8,1024]{1,0:T(8,128)(2,1)S(1)} %multiply_convert_fusion), channel_id=1, replica_groups=mesh['dp'=32,'tensor'=4] {'dp'}, dimensions={0}, use_global_device_ids=true | all-gather | bytes 540672 | tf_op jit(solution)/shard_map/all_gather | solution.py:125
  694.8 3.5 convolution_multiply_fusion
  698.2 138.8 %gather_fusion = bf16[16384]{0:T(1024)(128)(2,1)S(1)} fusion(bf16[256,2048]{1,0:T(8,128)(2,1)S(1)} %convolution_multiply_fusion, s32[16384]{0:T(1024)S(1)} %reshape.112), kind=kCustom, calls=%fused_computation | custom fusion | bytes 196608 | tf_op jit(solution)/shard_map/jit(take_along_axis)/gather | solution.py:132
  837.3 176.2 %all-reduce = bf16[256,64]{1,0:T(8,128)(2,1)S(1)} all-reduce(bf16[256,64]{1,0:T(8,128)(2,1)S(1)} %select_convert_fusion), channel_id=5, replica_groups=mesh['dp'=32,'tensor'=4] {'dp'}, use_global_device_ids=true, to_apply=%region_15.16.clone | all-reduce | flops 16384 | bytes 65536
  (111 shorter events, 35.8 us)
Async XLA Ops:
  6.5 448.7 %copy-start = (bf16[1024,1024]{1,0:T(8,128)(2,1)S(1)}, bf16[1024,1024]{1,0:T(8,128)(2,1)}, u32[]{:S(2)}) copy-start(bf16[1024,1024]{1,0:T(8,128)(2,1)} %param.23) | copy-start | bytes 6291460
  6.5 50.9 %all-gather.4.cloned.1.call-start = ((), (), s32[]{:S(2)}) async-start(), calls=%async_computation.3 | async-start | bytes 5242880 | tf_op jit(solution)/shard_map/all_gather | solution.py:41
  7.3 137.0 %all-gather.6.cloned.1.call-start = ((), (), s32[]{:S(2)}) async-start(), calls=%async_computation.4 | async-start | bytes 4325376 | tf_op jit(solution)/shard_map/all_gather | solution.py:47
  8.0 395.9 %reduce-scatter.4.cloned.1.call-start = ((), (), s32[]{:S(2)}) async-start(), calls=%async_computation.5 | async-start | bytes 10485760 | tf_op jit(solution)/shard_map/reduce_scatter | solution.py:88
  57.4 3.7 copy-start.10
  57.4 4.1 copy-start.12
  144.3 4.7 copy-start.11
  149.0 2.4 copy-start.5
  328.0 0.7 copy-start.6
  328.0 0.7 copy-start.7
  328.0 75.9 %copy-start.3 = (bf16[512,1024]{1,0:T(8,128)(2,1)S(1)}, bf16[512,1024]{1,0:T(8,128)(2,1)}, u32[]{:S(2)}) copy-start(bf16[512,1024]{1,0:T(8,128)(2,1)} %param.15) | copy-start | bytes 3145732
  328.0 127.2 %all-gather.8.cloned.1.call-start = ((), (), s32[]{:S(2)}) async-start(), calls=%async_computation.6 | async-start | bytes 5242880 | tf_op jit(solution)/shard_map/all_gather | solution.py:99
  403.9 2.2 copy-start.1
  406.2 49.1 %copy-start.13 = (f32[1024]{0:T(1024)S(1)}, f32[1024]{0:T(1024)}, u32[]{:S(2)}) copy-start(f32[1024]{0:T(1024)} %param.22) | copy-start | bytes 12292
  408.3 172.1 %reduce-scatter.6.cloned.1.call-start = ((), (), s32[]{:S(2)}) async-start(), calls=%async_computation.7 | async-start | bytes 5242880 | tf_op jit(solution)/shard_map/reduce_scatter | solution.py:106
  483.8 0.7 copy-start.8
  483.8 96.6 %copy-start.2 = (bf16[512,1024]{1,0:T(8,128)(2,1)S(1)}, bf16[512,1024]{1,0:T(8,128)(2,1)}, u32[]{:S(2)}) copy-start(bf16[512,1024]{1,0:T(8,128)(2,1)} %add_convert_fusion.1) | copy-start | bytes 3145732
  483.8 112.0 %reduce-scatter.8.cloned.1.call-start = ((), (), s32[]{:S(2)}) async-start(), calls=%async_computation.8 | async-start | bytes 163840 | tf_op jit(solution)/shard_map/reduce_scatter | solution.py:118
  580.4 5.0 copy-start.14
  580.4 6.2 copy-start.9
  580.4 3.4 copy-start.4
Sparse Core Ops, SparseCore 0:
  9.0 48.3 all-gather.3
  60.5 83.7 all-gather.5
  328.1 75.7 reduce-scatter.3
  408.4 46.8 all-gather.7
  483.9 47.6 reduce-scatter.5
  585.3 10.4 reduce-scatter.7
where the time goes:
time: 1030 us; the launch traced here: 1020 us
  blocking collectives  369 us (36%)
  waiting for transfers between devices  258 us (25%)
  matrix products  177 us (17%)
  local copies, waits for them, and re-layouts  162 us (16%)
  other arithmetic  26.4 us (3%)
  between operations  14.5 us (1%)
  loops' own time  13.4 us (1%)
    unnamed x1, blocking collectives  176 us
    gather x3, local copies, waits for them, and re-layouts, shards(): jnp.take_along_axis(table, jnp.clip(local_rows, 0, held - 1), axis=1)  139 us
    all_gather x1, blocking collectives, shards(): lax.all_gather(embedding, 'dp', axis=0, tiled=True)  97.2 us
    all_gather x1, blocking collectives, shards(): lax.all_gather(candidates, 'dp', axis=0, tiled=True)  95.9 us
    all_gather x1, waiting for transfers between devices, shards(): every_prompt = lax.all_gather(prompts, 'dp', axis=0, tiled=True)  78.2 us
    reduce_scatter x1, waiting for transfers between devices, shards(): lax.psum_scatter(jnp.dot(context, w_out, preferred_element_type=jnp.float...  75.2 us
    dot_general x4, matrix products, attend(): jnp.einsum('hqk,khe->qhe', probs, all_values, preferred_element_type=jnp....  64.8 us
    sub x4, matrix products, attend(): weights = jnp.exp(logits - top)  57.9 us
  transfers between devices with their start and end apart: 6, of which 5 were waited for; matrix products, arithmetic and copies ran while one was open for 1% of the time, Pallas kernels for 0%

commit v1 on v0

--- a/solution.py
+++ b/solution.py
@@ -121,19 +121,23 @@
     pooled = pooled_sums / my_lens[:, None].astype(jnp.float32)
     square = jnp.mean(pooled * pooled, axis=1, keepdims=True)
     embedding = (pooled * lax.rsqrt(square + 1e-06)).astype(jnp.bfloat16)
-    asked_vectors, asked_rows = (
-        lax.all_gather(embedding, "dp", axis=0, tiled=True),
-        lax.all_gather(candidates, "dp", axis=0, tiled=True),
-    )
+    n_dp = lax.axis_size("dp")
+    asked_vectors = lax.all_to_all(
+        jnp.broadcast_to(embedding[None], (n_dp,) + embedding.shape), "dp", 0, 0, tiled=True
+    ).reshape(-1, embedding.shape[1])
+    asked_rows = lax.all_to_all(
+        jnp.broadcast_to(candidates[None], (n_dp,) + candidates.shape), "dp", 0, 0, tiled=True
+    ).reshape(-1, candidates.shape[1])
     held = index_rows.shape[0]
     local_rows = asked_rows - lax.axis_index("dp") * held
-    owned = (local_rows >= 0) & (local_rows < held)
     table = jnp.dot(asked_vectors, index_rows.T, preferred_element_type=jnp.float32) * D ** (-0.5)
-    picked = jnp.take_along_axis(table, jnp.clip(local_rows, 0, held - 1), axis=1)
-    picked = jnp.where(owned, picked, jnp.float32(0.0))
-    return lax.psum_scatter(
-        picked.astype(jnp.bfloat16), "dp", scatter_dimension=0, tiled=True
-    ).astype(jnp.float32)
+    row_ids = jnp.arange(held, dtype=jnp.int32)
+    picked = jnp.sum(
+        jnp.where(local_rows[:, :, None] == row_ids[None, None, :], table[:, None, :], jnp.float32(0.0)),
+        axis=2,
+    )
+    returned = lax.all_to_all(picked, "dp", 0, 0, tiled=True)
+    return jnp.sum(returned.reshape(n_dp, -1, returned.shape[1]), axis=0)
 
 
 def solution(mesh):

time: 1030 us -> 629 us (0.61)
  blocking collectives: 369 us -> 14.1 us
  local copies, waits for them, and re-layouts: 162 us -> 24.4 us
  waiting for transfers between devices: 258 us -> 316 us
  other arithmetic: 26.4 us -> 49.7 us
  starting transfers between devices: 0.2 us -> 19 us
    all_gather x2 -> x0, blocking collectives: 193 us -> none  [the longest x1 97.2 us: shards(): lax.all_gather(embedding, 'dp', axis=0, tiled=True)]
    unnamed x1 -> x0, blocking collectives: 176 us -> none
    gather x3 -> x0, local copies, waits for them, and re-layouts: 139 us -> none  [shards(): jnp.take_along_axis(table, jnp.clip(local_rows, 0, held - 1), axis=1)]
    reduce_scatter x1, waiting for transfers between devices: 0.01 us -> 46.7 us  [shards(): lax.psum_scatter(jnp.dot(expanded, w_down, preferred_element_type=jnp.flo...]
    reduce_sum x0 -> x2, other arithmetic: none -> 22.5 us  [the longest x1 21.8 us: shards(): jnp.sum(jnp.where(local_rows[:, :, None] == row_ids[None, None, :], table...]
    all_to_all x0 -> x2, starting transfers between devices: none -> 18.6 us  [the longest x1 9.39 us: shards(): lax.all_to_all(jnp.broadcast_to(candidates[None], (n_dp,) + candidates.sh...]
    all_to_all x0 -> x1, blocking collectives: none -> 14.1 us  [shards(): returned = lax.all_to_all(picked, 'dp', 0, 0, tiled=True)]
    all_to_all x0 -> x2, waiting for transfers between devices: none -> 12.2 us  [the longest x1 12.2 us: shards(): lax.all_to_all(jnp.broadcast_to(embedding[None], (n_dp,) + embedding.shap...]
  transfers between devices with their start and end apart: 6 -> 8, of which waited for: 5 -> 7; matrix products, arithmetic and copies ran while one was open for 1% -> 2% of each run, Pallas kernels for 0% -> 0%
where the time goes in v1:
time: 629 us; the launch traced here: 618 us
  waiting for transfers between devices  316 us (50%)
  matrix products  177 us (28%)
  other arithmetic  49.7 us (8%)
  local copies, waits for them, and re-layouts  24.4 us (4%)
  starting transfers between devices  19 us (3%)
  blocking collectives  14.1 us (2%)
  between operations  14.1 us (2%)
    all_gather x1, waiting for transfers between devices, shards(): every_prompt = lax.all_gather(prompts, 'dp', axis=0, tiled=True)  78.2 us
    reduce_scatter x1, waiting for transfers between devices, shards(): lax.psum_scatter(jnp.dot(context, w_out, preferred_element_type=jnp.float...  75.2 us
    dot_general x4, matrix products, attend(): jnp.einsum('hqk,khe->qhe', probs, all_values, preferred_element_type=jnp....  64.8 us
    sub x4, matrix products, attend(): weights = jnp.exp(logits - top)  57.9 us
    all_gather x1, waiting for transfers between devices, shards(): whole = lax.all_gather(tokens, 'tensor', axis=0, tiled=True)  47.5 us
    all_gather x1, waiting for transfers between devices, shards(): lax.all_gather(normed_rows, 'tensor', axis=0, tiled=True)  46.9 us
    reduce_scatter x1, waiting for transfers between devices, shards(): lax.psum_scatter(jnp.dot(expanded, w_down, preferred_element_type=jnp.flo...  46.7 us
    dot_general x1, matrix products, shards(): jnp.dot(expanded, w_down, preferred_element_type=jnp.float32)  28.5 us
  transfers between devices with their start and end apart: 8, of which 7 were waited for; matrix products, arithmetic and copies ran while one was open for 2% of the time, Pallas kernels for 0%

profile of v1, /device:TPU:0, one launch (start us, length us, event | category | flops | bytes accessed | tf_op | source)
XLA Modules:
  0.0 618.3 jit_solution(7409169466895268998)
XLA Ops:
  9.9 47.5 %all-gather.4.cloned.1.call-done = bf16[2048,1024]{1,0:T(8,128)(2,1)} async-done(((bf16[512,1024]{1,0:T(8,128)(2,1)}), bf16[2048,1024]{1,0:T(8,128)(2,1)}) %all-gather.4.cloned.1.call-update) | async-done | bytes 4194320 | tf_op jit(solution)/shard_map/all_gather | solution.py:41
  57.4 3.7 convolution_convert_fusion.1
  61.5 2.3 convolution_convert_fusion.3
  63.7 2.3 fusion.48
  66.1 78.2 %all-gather.6.cloned.1.call-done = bf16[32,64,1024]{2,1,0:T(8,128)(2,1)} async-done(((bf16[1,64,1024]{2,1,0:T(8,128)(2,1)}), bf16[32,64,1024]{2,1,0:T(8,128)(2,1)}) %all-gather.6.cloned.1.call-update) | async-done | bytes 4194320 | tf_op jit(solution)/shard_map/all_gather | solution.py:47
  144.3 4.7 convolution_convert_fusion
  149.0 2.4 convolution_convert_fusion.2
  152.9 4.1 copy.29
  157.0 2.7 pad_maximum_fusion.1
  159.7 4.1 copy.30
  163.8 148.3 %while.11 = (s32[]{:T(128)}, bf16[4,512,256]{2,1,0:T(8,128)(2,1)}, s32[4]{0:T(128)S(1)}, s32[2048]{0:T(1024)S(1)}, s32[2048]{0:T(1024)S(1)}, /*index=5*/bf16[204...) while((s32[]{:T(128)}, bf16[4,512,256]{2,1,0:T(8,128)(2,1)}, ...), condition=%wide.region_6.7_spmd.clone, body=%wide.region_3.6_spmd.clone.sunk | while | flops 3284297728 | bytes 19714248 | solution.py:84
  169.3 14.5 %fusion.133 = f32[4,512]{1,0:T(4,128)S(1)} fusion(pred[512,4096]{1,0:T(8,128)(4,1)} %pad_add_fusion.2, bf16[512,4,64]{0,2,1:T(8,128)(2,1)S(1)} %bitcast.71, bf16[4096,4,64]{0,2,1:T(8,128)(2,1)} %get-tuple-element.208), kind=kOutput, calls=%fused_computation.126.clone.1 | convolution fusion | flops 1098911744 | bytes 4464640 | tf_op jit(solution)/shard_map/while/body/eval_jaxpr/sub | solution.py:78
  183.8 16.2 %fusion.134 = bf16[4,512,64]{1,2,0:T(8,128)(2,1)S(1)} fusion(bf16[4096,4,64]{0,2,1:T(8,128)(2,1)} %get-tuple-element.209, f32[4,512]{1,0:T(4,128)S(1)} %fusion.133, pred[512,4096]{1,0:T(8,128)(4,1)} %pad_add_fusion.2, bf16[512,4,64]{0,2,1:T(8,128)(2,1)S(1)} %bitcast.72, bf16[4096,4,64]{0,2,1:T(8,128)(2,1)} %get-tuple-element.208), kind=kOutput, calls=%fused_computation.13.clone.1 | convolution fusion | flops 2181175296 | bytes 6823936 | tf_op jit(solution)/shard_map/while/body/eval_jaxpr/hqk,khe->qhe/dot_general | solution.py:81
  206.3 14.5 %fusion.133 = f32[4,512]{1,0:T(4,128)S(1)} fusion(pred[512,4096]{1,0:T(8,128)(4,1)} %pad_add_fusion.2, bf16[512,4,64]{0,2,1:T(8,128)(2,1)S(1)} %bitcast.71, bf16[4096,4,64]{0,2,1:T(8,128)(2,1)} %get-tuple-element.208), kind=kOutput, calls=%fused_computation.126.clone.1 | convolution fusion | flops 1098911744 | bytes 4464640 | tf_op jit(solution)/shard_map/while/body/eval_jaxpr/sub | solution.py:78
  220.8 16.2 %fusion.134 = bf16[4,512,64]{1,2,0:T(8,128)(2,1)S(1)} fusion(bf16[4096,4,64]{0,2,1:T(8,128)(2,1)} %get-tuple-element.209, f32[4,512]{1,0:T(4,128)S(1)} %fusion.133, pred[512,4096]{1,0:T(8,128)(4,1)} %pad_add_fusion.2, bf16[512,4,64]{0,2,1:T(8,128)(2,1)S(1)} %bitcast.72, bf16[4096,4,64]{0,2,1:T(8,128)(2,1)} %get-tuple-element.208), kind=kOutput, calls=%fused_computation.13.clone.1 | convolution fusion | flops 2181175296 | bytes 6823936 | tf_op jit(solution)/shard_map/while/body/eval_jaxpr/hqk,khe->qhe/dot_general | solution.py:81
  243.3 14.5 %fusion.133 = f32[4,512]{1,0:T(4,128)S(1)} fusion(pred[512,4096]{1,0:T(8,128)(4,1)} %pad_add_fusion.2, bf16[512,4,64]{0,2,1:T(8,128)(2,1)S(1)} %bitcast.71, bf16[4096,4,64]{0,2,1:T(8,128)(2,1)} %get-tuple-element.208), kind=kOutput, calls=%fused_computation.126.clone.1 | convolution fusion | flops 1098911744 | bytes 4464640 | tf_op jit(solution)/shard_map/while/body/eval_jaxpr/sub | solution.py:78
  257.8 16.2 %fusion.134 = bf16[4,512,64]{1,2,0:T(8,128)(2,1)S(1)} fusion(bf16[4096,4,64]{0,2,1:T(8,128)(2,1)} %get-tuple-element.209, f32[4,512]{1,0:T(4,128)S(1)} %fusion.133, pred[512,4096]{1,0:T(8,128)(4,1)} %pad_add_fusion.2, bf16[512,4,64]{0,2,1:T(8,128)(2,1)S(1)} %bitcast.72, bf16[4096,4,64]{0,2,1:T(8,128)(2,1)} %get-tuple-element.208), kind=kOutput, calls=%fused_computation.13.clone.1 | convolution fusion | flops 2181175296 | bytes 6823936 | tf_op jit(solution)/shard_map/while/body/eval_jaxpr/hqk,khe->qhe/dot_general | solution.py:81
  280.3 14.5 %fusion.133 = f32[4,512]{1,0:T(4,128)S(1)} fusion(pred[512,4096]{1,0:T(8,128)(4,1)} %pad_add_fusion.2, bf16[512,4,64]{0,2,1:T(8,128)(2,1)S(1)} %bitcast.71, bf16[4096,4,64]{0,2,1:T(8,128)(2,1)} %get-tuple-element.208), kind=kOutput, calls=%fused_computation.126.clone.1 | convolution fusion | flops 1098911744 | bytes 4464640 | tf_op jit(solution)/shard_map/while/body/eval_jaxpr/sub | solution.py:78
  294.8 16.2 %fusion.134 = bf16[4,512,64]{1,2,0:T(8,128)(2,1)S(1)} fusion(bf16[4096,4,64]{0,2,1:T(8,128)(2,1)} %get-tuple-element.209, f32[4,512]{1,0:T(4,128)S(1)} %fusion.133, pred[512,4096]{1,0:T(8,128)(4,1)} %pad_add_fusion.2, bf16[512,4,64]{0,2,1:T(8,128)(2,1)S(1)} %bitcast.72, bf16[4096,4,64]{0,2,1:T(8,128)(2,1)} %get-tuple-element.208), kind=kOutput, calls=%fused_computation.13.clone.1 | convolution fusion | flops 2181175296 | bytes 6823936 | tf_op jit(solution)/shard_map/while/body/eval_jaxpr/hqk,khe->qhe/dot_general | solution.py:81
  312.1 5.8 fusion.98
  318.6 75.2 %reduce-scatter.4.cloned.1.call-done = f32[512,1024]{1,0:T(8,128)} async-done(((f32[2048,1024]{1,0:T(8,128)}), f32[512,1024]{1,0:T(8,128)}) %reduce-scatter.4.cloned.1.call-update) | async-done | bytes 2097168 | tf_op jit(solution)/shard_map/reduce_scatter | solution.py:88
  393.9 2.0 fusion.52
  398.2 46.9 %all-gather.8.cloned.1.call-done = bf16[2048,1024]{1,0:T(8,128)(2,1)} async-done(((bf16[512,1024]{1,0:T(8,128)(2,1)}), bf16[2048,1024]{1,0:T(8,128)(2,1)}) %all-gather.8.cloned.1.call-update) | async-done | bytes 4194320 | tf_op jit(solution)/shard_map/all_gather | solution.py:99
  445.2 28.5 %fusion.43 = bf16[2048,1024]{1,0:T(8,128)(2,1)} fusion(bf16[1024,1024]{1,0:T(8,128)(2,1)S(1)} %copy-done, f32[1024]{0:T(1024)S(1)} %copy-done.13, bf16[2048,1024]{1,0:T(8,128)(2,1)} %all-gather.8.cloned.1.call-done, bf16[1024,1024]{1,0:T(8,128)(2,1)} %param.21), kind=kOutput, calls=%fused_computation.48 | convolution fusion | flops 8730443776 | bytes 12587008 | tf_op jit(solution)/shard_map/dot_general | solution.py:107
  474.1 46.7 %reduce-scatter.6.cloned.1.call-done = bf16[512,1024]{1,0:T(8,128)(2,1)} async-done(((bf16[2048,1024]{1,0:T(8,128)(2,1)}), bf16[512,1024]{1,0:T(8,128)(2,1)}) %reduce-scatter.6.cloned.1.call-update) | async-done | bytes 1048592 | tf_op jit(solution)/shard_map/reduce_scatter | solution.py:106
  526.3 9.4 %all-to-all-start = ((s32[32,1,512]{2,1,0:T(1,128)}), s32[32,1,512]{2,1,0:T(1,128)S(1)}, u32[]{:S(2)}, u32[]{:S(2)}) async-start(s32[32,1,512]{2,1,0:T(1,128)} %reshape.123), calls=%async_computation | async-start | bytes 131072 | tf_op jit(solution)/shard_map/all_to_all | solution.py:128
  535.8 8.1 %reduce-scatter.8.cloned.1.call-done = f32[8,1024]{1,0:T(8,128)} async-done(((f32[32,1024]{1,0:T(8,128)}), f32[8,1024]{1,0:T(8,128)}) %reduce-scatter.8.cloned.1.call-update) | async-done | bytes 32784 | tf_op jit(solution)/shard_map/reduce_scatter | solution.py:118
  546.6 9.2 %all-to-all-start.1 = ((bf16[32,8,1024]{2,1,0:T(8,128)(2,1)}), bf16[32,8,1024]{2,1,0:T(8,128)(2,1)S(1)}, u32[]{:S(2)}, u32[]{:S(2)}) async-start(bf16[32,8,1024]{2,1,0:T(8,128)(2,1)} %broadcast_in_dim.53), calls=%async_computation.4 | async-start | bytes 1048576 | tf_op jit(solution)/shard_map/all_to_all | solution.py:125
  557.2 12.2 %all-to-all-done.1 = bf16[32,8,1024]{2,1,0:T(8,128)(2,1)S(1)} async-done(((bf16[32,8,1024]{2,1,0:T(8,128)(2,1)}), bf16[32,8,1024]{2,1,0:T(8,128)(2,1)S(1)}, u32[]{:S(2)}, u32[]{:S(2)}) %all-to-all-start.1) | async-done | bytes 524320 | tf_op jit(solution)/shard_map/all_to_all | solution.py:125
  569.4 3.5 convolution_multiply_fusion
  572.9 21.8 %select_reduce_fusion.1 = f32[256,64]{1,0:T(8,128)S(1)} fusion(f32[256,2048]{1,0:T(8,128)S(1)} %convolution_multiply_fusion, s32[256,64]{1,0:T(8,128)S(1)} %subtract_bitcast_fusion), kind=kLoop, calls=%fused_computation.26 | loop fusion | flops 100646912 | bytes 2228224 | tf_op jit(solution)/shard_map/reduce_sum | solution.py:135
  594.8 14.1 %all_to_all.19 = f32[32,1,512]{2,1,0:T(1,128)S(1)} all-to-all(f32[32,1,512]{2,1,0:T(1,128)S(1)} %reshape.125), channel_id=1, replica_groups=mesh['dp'=32,'tensor'=4] {'dp'}, dimensions={0} | all-to-all | bytes 131072 | tf_op jit(solution)/shard_map/all_to_all | solution.py:139
  (117 shorter events, 42.6 us)
Async XLA Ops:
  6.5 438.6 %copy-start = (bf16[1024,1024]{1,0:T(8,128)(2,1)S(1)}, bf16[1024,1024]{1,0:T(8,128)(2,1)}, u32[]{:S(2)}) copy-start(bf16[1024,1024]{1,0:T(8,128)(2,1)} %param.23) | copy-start | bytes 6291460
  6.5 50.9 %all-gather.4.cloned.1.call-start = ((), (), s32[]{:S(2)}) async-start(), calls=%async_computation.6 | async-start | bytes 5242880 | tf_op jit(solution)/shard_map/all_gather | solution.py:41
  7.3 137.0 %all-gather.6.cloned.1.call-start = ((), (), s32[]{:S(2)}) async-start(), calls=%async_computation.7 | async-start | bytes 4325376 | tf_op jit(solution)/shard_map/all_gather | solution.py:47
  8.0 385.8 %reduce-scatter.4.cloned.1.call-start = ((), (), s32[]{:S(2)}) async-start(), calls=%async_computation.8 | async-start | bytes 10485760 | tf_op jit(solution)/shard_map/reduce_scatter | solution.py:88
  57.4 3.7 copy-start.10
  57.4 4.1 copy-start.12
  144.3 4.7 copy-start.11
  149.0 2.4 copy-start.5
  317.9 0.7 copy-start.6
  317.9 0.7 copy-start.7
  317.9 75.9 %copy-start.3 = (bf16[512,1024]{1,0:T(8,128)(2,1)S(1)}, bf16[512,1024]{1,0:T(8,128)(2,1)}, u32[]{:S(2)}) copy-start(bf16[512,1024]{1,0:T(8,128)(2,1)} %param.15) | copy-start | bytes 3145732
  317.9 127.2 %all-gather.8.cloned.1.call-start = ((), (), s32[]{:S(2)}) async-start(), calls=%async_computation.9 | async-start | bytes 5242880 | tf_op jit(solution)/shard_map/all_gather | solution.py:99
  393.9 2.2 copy-start.1
  396.1 49.1 %copy-start.13 = (f32[1024]{0:T(1024)S(1)}, f32[1024]{0:T(1024)}, u32[]{:S(2)}) copy-start(f32[1024]{0:T(1024)} %param.22) | copy-start | bytes 12292
  398.2 122.6 %reduce-scatter.6.cloned.1.call-start = ((), (), s32[]{:S(2)}) async-start(), calls=%async_computation.10 | async-start | bytes 5242880 | tf_op jit(solution)/shard_map/reduce_scatter | solution.py:106
  473.7 47.1 %copy-start.2 = (bf16[512,1024]{1,0:T(8,128)(2,1)S(1)}, bf16[512,1024]{1,0:T(8,128)(2,1)}, u32[]{:S(2)}) copy-start(bf16[512,1024]{1,0:T(8,128)(2,1)} %add_convert_fusion.1) | copy-start | bytes 3145732
  473.7 51.8 %copy-start.8 = (s32[8,64]{1,0:T(8,128)S(1)}, s32[8,64]{1,0:T(8,128)}, u32[]{:S(2)}) copy-start(s32[8,64]{1,0:T(8,128)} %param.27) | copy-start | bytes 6148
  473.7 70.2 %reduce-scatter.8.cloned.1.call-start = ((), (), s32[]{:S(2)}) async-start(), calls=%async_computation.11 | async-start | bytes 163840 | tf_op jit(solution)/shard_map/reduce_scatter | solution.py:118
  474.1 61.6 %copy-start.9 = (s32[1,32]{1,0:T(1,128)S(1)}, s32[1,32]{1,0:T(1,128)}, u32[]{:S(2)}) copy-start(s32[1,32]{1,0:T(1,128)} %param.25) | copy-start | bytes 388
  520.8 3.4 copy-start.4
  526.3 19.4 %all-to-all-start = ((s32[32,1,512]{2,1,0:T(1,128)}), s32[32,1,512]{2,1,0:T(1,128)S(1)}, u32[]{:S(2)}, u32[]{:S(2)}) async-start(s32[32,1,512]{2,1,0:T(1,128)} %reshape.123), calls=%async_computation | async-start | bytes 131072 | tf_op jit(solution)/shard_map/all_to_all | solution.py:128
  546.6 22.8 %all-to-all-start.1 = ((bf16[32,8,1024]{2,1,0:T(8,128)(2,1)}), bf16[32,8,1024]{2,1,0:T(8,128)(2,1)S(1)}, u32[]{:S(2)}, u32[]{:S(2)}) async-start(bf16[32,8,1024]{2,1,0:T(8,128)(2,1)} %broadcast_in_dim.53), calls=%async_computation.4 | async-start | bytes 1048576 | tf_op jit(solution)/shard_map/all_to_all | solution.py:125
Sparse Core Ops, SparseCore 0:
  9.0 48.3 all-gather.3
  60.5 83.7 all-gather.5
  318.1 75.7 reduce-scatter.3
  398.3 46.8 all-gather.7
  473.8 46.8 reduce-scatter.5
  525.7 18.1 reduce-scatter.7

commit v2 on v1

--- a/solution.py
+++ b/solution.py
@@ -44,10 +44,14 @@
     )
     keys = project(whole, w_attn[1])
     values = project(whole, w_attn[2])
-    every_prompt = lax.all_gather(prompts, "dp", axis=0, tiled=True)
-    flat = every_prompt.reshape(-1, every_prompt.shape[2])
-    prompt_key = project(flat, w_attn[1])
-    prompt_value = project(flat, w_attn[2])
+    n_dp = lax.axis_size("dp")
+    own_prompt = prompts.reshape(-1, prompts.shape[2])
+    own_kv = jnp.concatenate([project(own_prompt, w_attn[1]), project(own_prompt, w_attn[2])], axis=1)
+    every_kv = lax.all_to_all(
+        jnp.broadcast_to(own_kv[None], (n_dp,) + own_kv.shape), "dp", 0, 0, tiled=True
+    ).reshape(-1, 2 * columns)
+    prompt_key = every_kv[:, :columns]
+    prompt_value = every_kv[:, columns:]
     prompt_len = prompts.shape[1]
     prompt_rows = prompt_key.shape[0]
     lens = lengths[0]
@@ -86,11 +90,11 @@
     )
     my_start = lax.axis_index("tensor") * shard_rows
     attn_part = lax.psum_scatter(
-        jnp.dot(context, w_out, preferred_element_type=jnp.float32),
+        jnp.dot(context, w_out, preferred_element_type=jnp.float32).astype(jnp.bfloat16),
         "tensor",
         scatter_dimension=0,
         tiled=True,
-    )
+    ).astype(jnp.float32)
     normed_rows = layer_norm(
         tokens.astype(jnp.float32) + attn_part, norm_gain[0], norm_bias[0]
     ).astype(jnp.bfloat16)
@@ -121,7 +125,6 @@
     pooled = pooled_sums / my_lens[:, None].astype(jnp.float32)
     square = jnp.mean(pooled * pooled, axis=1, keepdims=True)
     embedding = (pooled * lax.rsqrt(square + 1e-06)).astype(jnp.bfloat16)
-    n_dp = lax.axis_size("dp")
     asked_vectors = lax.all_to_all(
         jnp.broadcast_to(embedding[None], (n_dp,) + embedding.shape), "dp", 0, 0, tiled=True
     ).reshape(-1, embedding.shape[1])

time: 629 us -> 537 us (0.85)
  waiting for transfers between devices: 316 us -> 216 us
  starting transfers between devices: 19 us -> 29.9 us
    all_gather x1 -> x0, waiting for transfers between devices: 78.2 us -> none  [shards(): every_prompt = lax.all_gather(prompts, 'dp', axis=0, tiled=True)]
    all_to_all x0 -> x1, waiting for transfers between devices: none -> 29 us  [shards(): lax.all_to_all(jnp.broadcast_to(own_kv[None], (n_dp,) + own_kv.shape), 'd...]
    reduce_scatter x1, waiting for transfers between devices: 75.2 us -> 47 us  [shards(): lax.psum_scatter(jnp.dot(context, w_out, preferred_element_type=jnp.float...]
    all_gather x1, waiting for transfers between devices: 47.5 us -> 24.8 us  [shards(): whole = lax.all_gather(tokens, 'tensor', axis=0, tiled=True)]
    all_to_all x0 -> x1, starting transfers between devices: none -> 10.9 us  [shards(): lax.all_to_all(jnp.broadcast_to(own_kv[None], (n_dp,) + own_kv.shape), 'd...]
  transfers between devices with their start and end apart: 8 -> 8, of which waited for: 7 -> 8; matrix products, arithmetic and copies ran while one was open for 2% -> 2% of each run, Pallas kernels for 0% -> 0%
where the time goes in v2:
time: 537 us; the launch traced here: 526 us
  waiting for transfers between devices  216 us (40%)
  matrix products  174 us (32%)
  other arithmetic  48.1 us (9%)
  starting transfers between devices  29.9 us (6%)
  local copies, waits for them, and re-layouts  27.4 us (5%)
  blocking collectives  14.1 us (3%)
  between operations  13.8 us (3%)
    dot_general x4, matrix products, attend(): jnp.einsum('hqk,khe->qhe', probs, all_values, preferred_element_type=jnp....  64.8 us
    sub x4, matrix products, attend(): weights = jnp.exp(logits - top)  58 us
    reduce_scatter x1, waiting for transfers between devices, shards(): lax.psum_scatter(jnp.dot(context, w_out, preferred_element_type=jnp.float...  47 us
    all_gather x1, waiting for transfers between devices, shards(): lax.all_gather(normed_rows, 'tensor', axis=0, tiled=True)  46.9 us
    reduce_scatter x1, waiting for transfers between devices, shards(): lax.psum_scatter(jnp.dot(expanded, w_down, preferred_element_type=jnp.flo...  46.7 us
    all_to_all x1, waiting for transfers between devices, shards(): lax.all_to_all(jnp.broadcast_to(own_kv[None], (n_dp,) + own_kv.shape), 'd...  29 us
    dot_general x1, matrix products, shards(): jnp.dot(expanded, w_down, preferred_element_type=jnp.float32)  28.5 us
    all_gather x1, waiting for transfers between devices, shards(): whole = lax.all_gather(tokens, 'tensor', axis=0, tiled=True)  24.8 us
  transfers between devices with their start and end apart: 8, of which 8 were waited for; matrix products, arithmetic and copies ran while one was open for 2% of the time, Pallas kernels for 0%

profile of v2, /device:TPU:0, one launch (start us, length us, event | category | flops | bytes accessed | tf_op | source)
XLA Modules:
  0.0 526.0 jit_solution(133726603630260348)
XLA Ops:
  11.5 10.9 %all-to-all-start.1 = ((bf16[32,64,512]{2,1,0:T(8,128)(2,1)}), bf16[32,64,512]{2,1,0:T(8,128)(2,1)}, u32[]{:S(2)}, u32[]{:S(2)}) async-start(bf16[32,64,512]{2,1,0:T(8,128)(2,1)} %broadcast_in_dim.55), calls=%async_computation.1 | async-start | bytes 4194304 | tf_op jit(solution)/shard_map/all_to_all | solution.py:50
  23.0 29.0 %all-to-all-done.1 = bf16[32,64,512]{2,1,0:T(8,128)(2,1)} async-done(((bf16[32,64,512]{2,1,0:T(8,128)(2,1)}), bf16[32,64,512]{2,1,0:T(8,128)(2,1)}, u32[]{:S(2)}, u32[]{:S(2)}) %all-to-all-start.1) | async-done | bytes 2097184 | tf_op jit(solution)/shard_map/all_to_all | solution.py:50
  52.1 2.7 fusion.99
  54.8 24.8 %all-gather.3.cloned.1.call-done = bf16[2048,1024]{1,0:T(8,128)(2,1)} async-done(((bf16[512,1024]{1,0:T(8,128)(2,1)}), bf16[2048,1024]{1,0:T(8,128)(2,1)}) %all-gather.3.cloned.1.call-update) | async-done | bytes 4194320 | tf_op jit(solution)/shard_map/all_gather | solution.py:41
  79.6 3.7 convolution_convert_fusion.2
  83.3 2.4 convolution_convert_fusion.1
  85.7 2.3 pad_maximum_fusion
  88.0 4.1 copy.24
  92.2 4.1 copy.25
  96.3 4.6 fusion.48
  100.9 148.0 %while.11 = (s32[]{:T(128)}, bf16[4,512,256]{2,1,0:T(8,128)(2,1)}, s32[4]{0:T(128)S(1)}, s32[2048]{0:T(1024)S(1)}, s32[2048]{0:T(1024)S(1)}, /*index=5*/bf16[204...) while((s32[]{:T(128)}, bf16[4,512,256]{2,1,0:T(8,128)(2,1)}, ...), condition=%wide.region_6.7_spmd.clone, body=%wide.region_3.6_spmd.clone.sunk | while | flops 3284297728 | bytes 19714248 | solution.py:88
  106.4 14.5 %fusion.134 = f32[4,512]{1,0:T(4,128)S(1)} fusion(pred[512,4096]{1,0:T(8,128)(4,1)} %pad_add_fusion.2, bf16[512,4,64]{0,2,1:T(8,128)(2,1)S(1)} %bitcast.74, bf16[4096,4,64]{0,2,1:T(8,128)(2,1)} %get-tuple-element.204), kind=kOutput, calls=%fused_computation.131.clone.1 | convolution fusion | flops 1098911744 | bytes 4464640 | tf_op jit(solution)/shard_map/while/body/eval_jaxpr/sub | solution.py:82
  120.9 16.2 %fusion.135 = bf16[4,512,64]{1,2,0:T(8,128)(2,1)S(1)} fusion(bf16[4096,4,64]{0,2,1:T(8,128)(2,1)} %get-tuple-element.205, f32[4,512]{1,0:T(4,128)S(1)} %fusion.134, pred[512,4096]{1,0:T(8,128)(4,1)} %pad_add_fusion.2, bf16[512,4,64]{0,2,1:T(8,128)(2,1)S(1)} %bitcast.75, bf16[4096,4,64]{0,2,1:T(8,128)(2,1)} %get-tuple-element.204), kind=kOutput, calls=%fused_computation.13.clone.1 | convolution fusion | flops 2181175296 | bytes 6823936 | tf_op jit(solution)/shard_map/while/body/eval_jaxpr/hqk,khe->qhe/dot_general | solution.py:85
  143.3 14.5 %fusion.134 = f32[4,512]{1,0:T(4,128)S(1)} fusion(pred[512,4096]{1,0:T(8,128)(4,1)} %pad_add_fusion.2, bf16[512,4,64]{0,2,1:T(8,128)(2,1)S(1)} %bitcast.74, bf16[4096,4,64]{0,2,1:T(8,128)(2,1)} %get-tuple-element.204), kind=kOutput, calls=%fused_computation.131.clone.1 | convolution fusion | flops 1098911744 | bytes 4464640 | tf_op jit(solution)/shard_map/while/body/eval_jaxpr/sub | solution.py:82
  157.8 16.2 %fusion.135 = bf16[4,512,64]{1,2,0:T(8,128)(2,1)S(1)} fusion(bf16[4096,4,64]{0,2,1:T(8,128)(2,1)} %get-tuple-element.205, f32[4,512]{1,0:T(4,128)S(1)} %fusion.134, pred[512,4096]{1,0:T(8,128)(4,1)} %pad_add_fusion.2, bf16[512,4,64]{0,2,1:T(8,128)(2,1)S(1)} %bitcast.75, bf16[4096,4,64]{0,2,1:T(8,128)(2,1)} %get-tuple-element.204), kind=kOutput, calls=%fused_computation.13.clone.1 | convolution fusion | flops 2181175296 | bytes 6823936 | tf_op jit(solution)/shard_map/while/body/eval_jaxpr/hqk,khe->qhe/dot_general | solution.py:85
  180.2 14.5 %fusion.134 = f32[4,512]{1,0:T(4,128)S(1)} fusion(pred[512,4096]{1,0:T(8,128)(4,1)} %pad_add_fusion.2, bf16[512,4,64]{0,2,1:T(8,128)(2,1)S(1)} %bitcast.74, bf16[4096,4,64]{0,2,1:T(8,128)(2,1)} %get-tuple-element.204), kind=kOutput, calls=%fused_computation.131.clone.1 | convolution fusion | flops 1098911744 | bytes 4464640 | tf_op jit(solution)/shard_map/while/body/eval_jaxpr/sub | solution.py:82
  194.7 16.2 %fusion.135 = bf16[4,512,64]{1,2,0:T(8,128)(2,1)S(1)} fusion(bf16[4096,4,64]{0,2,1:T(8,128)(2,1)} %get-tuple-element.205, f32[4,512]{1,0:T(4,128)S(1)} %fusion.134, pred[512,4096]{1,0:T(8,128)(4,1)} %pad_add_fusion.2, bf16[512,4,64]{0,2,1:T(8,128)(2,1)S(1)} %bitcast.75, bf16[4096,4,64]{0,2,1:T(8,128)(2,1)} %get-tuple-element.204), kind=kOutput, calls=%fused_computation.13.clone.1 | convolution fusion | flops 2181175296 | bytes 6823936 | tf_op jit(solution)/shard_map/while/body/eval_jaxpr/hqk,khe->qhe/dot_general | solution.py:85
  217.1 14.5 %fusion.134 = f32[4,512]{1,0:T(4,128)S(1)} fusion(pred[512,4096]{1,0:T(8,128)(4,1)} %pad_add_fusion.2, bf16[512,4,64]{0,2,1:T(8,128)(2,1)S(1)} %bitcast.74, bf16[4096,4,64]{0,2,1:T(8,128)(2,1)} %get-tuple-element.204), kind=kOutput, calls=%fused_computation.131.clone.1 | convolution fusion | flops 1098911744 | bytes 4464640 | tf_op jit(solution)/shard_map/while/body/eval_jaxpr/sub | solution.py:82
  231.6 16.2 %fusion.135 = bf16[4,512,64]{1,2,0:T(8,128)(2,1)S(1)} fusion(bf16[4096,4,64]{0,2,1:T(8,128)(2,1)} %get-tuple-element.205, f32[4,512]{1,0:T(4,128)S(1)} %fusion.134, pred[512,4096]{1,0:T(8,128)(4,1)} %pad_add_fusion.2, bf16[512,4,64]{0,2,1:T(8,128)(2,1)S(1)} %bitcast.75, bf16[4096,4,64]{0,2,1:T(8,128)(2,1)} %get-tuple-element.204), kind=kOutput, calls=%fused_computation.13.clone.1 | convolution fusion | flops 2181175296 | bytes 6823936 | tf_op jit(solution)/shard_map/while/body/eval_jaxpr/hqk,khe->qhe/dot_general | solution.py:85
  248.9 4.5 convolution_convert_fusion
  254.2 47.0 %reduce-scatter.4.cloned.1.call-done = bf16[512,1024]{1,0:T(8,128)(2,1)} async-done(((bf16[2048,1024]{1,0:T(8,128)(2,1)}), bf16[512,1024]{1,0:T(8,128)(2,1)}) %reduce-scatter.4.cloned.1.call-update) | async-done | bytes 1048592 | tf_op jit(solution)/shard_map/reduce_scatter | solution.py:92
  302.9 1.7 multiply_reduce_fusion.1
  306.3 46.9 %all-gather.5.cloned.1.call-done = bf16[2048,1024]{1,0:T(8,128)(2,1)} async-done(((bf16[512,1024]{1,0:T(8,128)(2,1)}), bf16[2048,1024]{1,0:T(8,128)(2,1)}) %all-gather.5.cloned.1.call-update) | async-done | bytes 4194320 | tf_op jit(solution)/shard_map/all_gather | solution.py:103
  353.3 28.5 %fusion.43 = bf16[2048,1024]{1,0:T(8,128)(2,1)} fusion(bf16[1024,1024]{1,0:T(8,128)(2,1)S(1)} %copy-done, f32[1024]{0:T(1024)S(1)} %copy-done.13, bf16[2048,1024]{1,0:T(8,128)(2,1)} %all-gather.5.cloned.1.call-done, bf16[1024,1024]{1,0:T(8,128)(2,1)} %param.21), kind=kOutput, calls=%fused_computation.48 | convolution fusion | flops 8730443776 | bytes 12587008 | tf_op jit(solution)/shard_map/dot_general | solution.py:111
  382.2 46.7 %reduce-scatter.6.cloned.1.call-done = bf16[512,1024]{1,0:T(8,128)(2,1)} async-done(((bf16[2048,1024]{1,0:T(8,128)(2,1)}), bf16[512,1024]{1,0:T(8,128)(2,1)}) %reduce-scatter.6.cloned.1.call-update) | async-done | bytes 1048592 | tf_op jit(solution)/shard_map/reduce_scatter | solution.py:110
  434.4 9.4 %all-to-all-start = ((s32[32,1,512]{2,1,0:T(1,128)}), s32[32,1,512]{2,1,0:T(1,128)S(1)}, u32[]{:S(2)}, u32[]{:S(2)}) async-start(s32[32,1,512]{2,1,0:T(1,128)} %reshape.128), calls=%async_computation | async-start | bytes 131072 | tf_op jit(solution)/shard_map/all_to_all | solution.py:131
  443.9 8.0 %reduce-scatter.8.cloned.1.call-done = f32[8,1024]{1,0:T(8,128)} async-done(((f32[32,1024]{1,0:T(8,128)}), f32[8,1024]{1,0:T(8,128)}) %reduce-scatter.8.cloned.1.call-update) | async-done | bytes 32784 | tf_op jit(solution)/shard_map/reduce_scatter | solution.py:122
  454.7 9.2 %all-to-all-start.2 = ((bf16[32,8,1024]{2,1,0:T(8,128)(2,1)}), bf16[32,8,1024]{2,1,0:T(8,128)(2,1)S(1)}, u32[]{:S(2)}, u32[]{:S(2)}) async-start(bf16[32,8,1024]{2,1,0:T(8,128)(2,1)} %broadcast_in_dim.56), calls=%async_computation.5 | async-start | bytes 1048576 | tf_op jit(solution)/shard_map/all_to_all | solution.py:128
  465.3 12.2 %all-to-all-done.2 = bf16[32,8,1024]{2,1,0:T(8,128)(2,1)S(1)} async-done(((bf16[32,8,1024]{2,1,0:T(8,128)(2,1)}), bf16[32,8,1024]{2,1,0:T(8,128)(2,1)S(1)}, u32[]{:S(2)}, u32[]{:S(2)}) %all-to-all-start.2) | async-done | bytes 524320 | tf_op jit(solution)/shard_map/all_to_all | solution.py:128
  477.5 3.5 convolution_multiply_fusion
  481.0 21.8 %select_reduce_fusion.1 = f32[256,64]{1,0:T(8,128)S(1)} fusion(f32[256,2048]{1,0:T(8,128)S(1)} %convolution_multiply_fusion, s32[256,64]{1,0:T(8,128)S(1)} %subtract_bitcast_fusion), kind=kLoop, calls=%fused_computation.26 | loop fusion | flops 100646912 | bytes 2228224 | tf_op jit(solution)/shard_map/reduce_sum | solution.py:138
  502.9 14.1 %all_to_all.24 = f32[32,1,512]{2,1,0:T(1,128)S(1)} all-to-all(f32[32,1,512]{2,1,0:T(1,128)S(1)} %reshape.130), channel_id=1, replica_groups=mesh['dp'=32,'tensor'=4] {'dp'}, dimensions={0} | all-to-all | bytes 131072 | tf_op jit(solution)/shard_map/all_to_all | solution.py:142
  (118 shorter events, 44.0 us)
Async XLA Ops:
  6.5 346.7 %copy-start = (bf16[1024,1024]{1,0:T(8,128)(2,1)S(1)}, bf16[1024,1024]{1,0:T(8,128)(2,1)}, u32[]{:S(2)}) copy-start(bf16[1024,1024]{1,0:T(8,128)(2,1)} %param.23) | copy-start | bytes 6291460
  6.5 73.0 %all-gather.3.cloned.1.call-start = ((), (), s32[]{:S(2)}) async-start(), calls=%async_computation.7 | async-start | bytes 5242880 | tf_op jit(solution)/shard_map/all_gather | solution.py:41
  7.3 15.2 %copy-start.10 = (s32[1,32]{1,0:T(1,128)S(1)}, s32[1,32]{1,0:T(1,128)}, u32[]{:S(2)}) copy-start(s32[1,32]{1,0:T(1,128)} %param.25) | copy-start | bytes 388
  7.3 15.6 %copy-start.9 = (s32[32]{0:T(128)S(1)}, s32[32]{0:T(128)}, u32[]{:S(2)}) copy-start(s32[32]{0:T(128)} %param.26) | copy-start | bytes 388
  11.5 40.5 %all-to-all-start.1 = ((bf16[32,64,512]{2,1,0:T(8,128)(2,1)}), bf16[32,64,512]{2,1,0:T(8,128)(2,1)}, u32[]{:S(2)}, u32[]{:S(2)}) async-start(bf16[32,64,512]{2,1,0:T(8,128)(2,1)} %broadcast_in_dim.55), calls=%async_computation.1 | async-start | bytes 4194304 | tf_op jit(solution)/shard_map/all_to_all | solution.py:50
  22.4 278.8 %reduce-scatter.4.cloned.1.call-start = ((), (), s32[]{:S(2)}) async-start(), calls=%async_computation.8 | async-start | bytes 5242880 | tf_op jit(solution)/shard_map/reduce_scatter | solution.py:92
  79.6 3.7 copy-start.12
  83.3 2.4 copy-start.5
  253.5 0.7 copy-start.6
  253.5 0.7 copy-start.7
  253.5 47.8 %copy-start.1 = (bf16[512,1024]{1,0:T(8,128)(2,1)S(1)}, bf16[512,1024]{1,0:T(8,128)(2,1)}, u32[]{:S(2)}) copy-start(bf16[512,1024]{1,0:T(8,128)(2,1)} %param.15) | copy-start | bytes 3145732
  253.5 99.8 %all-gather.5.cloned.1.call-start = ((), (), s32[]{:S(2)}) async-start(), calls=%async_computation.9 | async-start | bytes 5242880 | tf_op jit(solution)/shard_map/all_gather | solution.py:103
  254.2 99.1 %copy-start.13 = (f32[1024]{0:T(1024)S(1)}, f32[1024]{0:T(1024)}, u32[]{:S(2)}) copy-start(f32[1024]{0:T(1024)} %param.22) | copy-start | bytes 12292
  301.2 3.4 copy-start.3
  306.3 122.6 %reduce-scatter.6.cloned.1.call-start = ((), (), s32[]{:S(2)}) async-start(), calls=%async_computation.10 | async-start | bytes 5242880 | tf_op jit(solution)/shard_map/reduce_scatter | solution.py:110
  381.8 47.1 %copy-start.2 = (bf16[512,1024]{1,0:T(8,128)(2,1)S(1)}, bf16[512,1024]{1,0:T(8,128)(2,1)}, u32[]{:S(2)}) copy-start(bf16[512,1024]{1,0:T(8,128)(2,1)} %add_convert_fusion.1) | copy-start | bytes 3145732
  381.8 51.8 %copy-start.8 = (s32[8,64]{1,0:T(8,128)S(1)}, s32[8,64]{1,0:T(8,128)}, u32[]{:S(2)}) copy-start(s32[8,64]{1,0:T(8,128)} %param.27) | copy-start | bytes 6148
  381.8 70.1 %reduce-scatter.8.cloned.1.call-start = ((), (), s32[]{:S(2)}) async-start(), calls=%async_computation.11 | async-start | bytes 163840 | tf_op jit(solution)/shard_map/reduce_scatter | solution.py:122
  382.2 61.6 %copy-start.11 = (s32[1,32]{1,0:T(1,128)S(1)}, s32[1,32]{1,0:T(1,128)}, u32[]{:S(2)}) copy-start(s32[1,32]{1,0:T(1,128)} %param.25) | copy-start | bytes 388
  428.9 3.4 copy-start.4
  434.4 19.4 %all-to-all-start = ((s32[32,1,512]{2,1,0:T(1,128)}), s32[32,1,512]{2,1,0:T(1,128)S(1)}, u32[]{:S(2)}, u32[]{:S(2)}) async-start(s32[32,1,512]{2,1,0:T(1,128)} %reshape.128), calls=%async_computation | async-start | bytes 131072 | tf_op jit(solution)/shard_map/all_to_all | solution.py:131
  454.7 22.8 %all-to-all-start.2 = ((bf16[32,8,1024]{2,1,0:T(8,128)(2,1)}), bf16[32,8,1024]{2,1,0:T(8,128)(2,1)S(1)}, u32[]{:S(2)}, u32[]{:S(2)}) async-start(bf16[32,8,1024]{2,1,0:T(8,128)(2,1)} %broadcast_in_dim.56), calls=%async_computation.5 | async-start | bytes 1048576 | tf_op jit(solution)/shard_map/all_to_all | solution.py:128
Sparse Core Ops, SparseCore 0:
  9.0 70.5 all-gather.2
  253.6 47.5 reduce-scatter.3
  306.4 46.8 all-gather.4
  381.9 46.8 reduce-scatter.5
  433.8 18.0 reduce-scatter.7

commit v3 on v2

--- a/solution.py
+++ b/solution.py
@@ -61,10 +61,13 @@
     position = jnp.arange(tok_dev, dtype=jnp.int32)
     seg = jnp.sum((position[:, None] >= ends[None, :]).astype(jnp.int32), axis=1)
     tok_group = jnp.sum(jnp.where(seg[:, None] == text_ids[None, :], groups[None, :], 0), axis=1)
-    key_group = jnp.arange(prompt_rows, dtype=jnp.int32) // prompt_len
-    all_keys = jnp.concatenate([keys, prompt_key], axis=0).reshape(-1, heads_here, HEAD_DIM)
-    all_values = jnp.concatenate([values, prompt_value], axis=0).reshape(-1, heads_here, HEAD_DIM)
-    block = min(512, tok_dev)
+    groups_all = prompt_rows // prompt_len
+    group_ids = jnp.arange(groups_all, dtype=jnp.int32)
+    starts = ends - lens
+    prompt_k4 = prompt_key.reshape(groups_all, prompt_len, heads_here, HEAD_DIM)
+    prompt_v4 = prompt_value.reshape(groups_all, prompt_len, heads_here, HEAD_DIM)
+    block = min(256, tok_dev)
+    window = min(tok_dev, -(-(block + 2 * (512 - 1)) // 128) * 128)
 
     def attend(number):
         start = number * block
@@ -73,16 +76,31 @@
         )
         seg_block = lax.dynamic_slice_in_dim(seg, start, block, 0)
         group_block = lax.dynamic_slice_in_dim(tok_group, start, block, 0)
-        allowed = jnp.concatenate(
-            [seg_block[:, None] == seg[None, :], group_block[:, None] == key_group[None, :]], axis=1
+        first = jnp.clip(starts[seg_block[0]], 0, tok_dev - window)
+        k_win = lax.dynamic_slice_in_dim(keys, first, window, 0).reshape(window, heads_here, HEAD_DIM)
+        v_win = lax.dynamic_slice_in_dim(values, first, window, 0).reshape(
+            window, heads_here, HEAD_DIM
         )
-        logits = jnp.einsum("qhe,khe->hqk", q_block, all_keys, preferred_element_type=jnp.float32)
-        logits = jnp.where(allowed[None], logits, jnp.float32(-1e30))
-        top = jnp.max(logits, axis=2, keepdims=True)
-        weights = jnp.exp(logits - top)
-        total = jnp.sum(weights, axis=2, keepdims=True)
-        probs = (weights / total).astype(jnp.bfloat16)
-        mixed = jnp.einsum("hqk,khe->qhe", probs, all_values, preferred_element_type=jnp.float32)
+        seg_win = lax.dynamic_slice_in_dim(seg, first, window, 0)
+        same = seg_block[:, None] == seg_win[None, :]
+        mine = group_ids[:, None] == group_block[None, :]
+        text_logits = jnp.einsum("qhe,khe->hqk", q_block, k_win, preferred_element_type=jnp.float32)
+        text_logits = jnp.where(same[None], text_logits, jnp.float32(-1e30))
+        every = jnp.einsum("qhe,gphe->hgqp", q_block, prompt_k4, preferred_element_type=jnp.float32)
+        prompt_logits = jnp.sum(jnp.where(mine[None, :, :, None], every, jnp.float32(0.0)), axis=1)
+        top = jnp.maximum(
+            jnp.max(text_logits, axis=2, keepdims=True), jnp.max(prompt_logits, axis=2, keepdims=True)
+        )
+        text_w = jnp.exp(text_logits - top)
+        prompt_w = jnp.exp(prompt_logits - top)
+        total = jnp.sum(text_w, axis=2, keepdims=True) + jnp.sum(prompt_w, axis=2, keepdims=True)
+        text_p = (text_w / total).astype(jnp.bfloat16)
+        prompt_p = (prompt_w / total).astype(jnp.bfloat16)
+        spread = jnp.where(mine[None, :, :, None], prompt_p[:, None], jnp.bfloat16(0))
+        mixed = jnp.einsum("hqk,khe->qhe", text_p, v_win, preferred_element_type=jnp.float32)
+        mixed = mixed + jnp.einsum(
+            "hgqp,gphe->qhe", spread, prompt_v4, preferred_element_type=jnp.float32
+        )
         return mixed.astype(jnp.bfloat16).reshape(block, columns)
 
     context = lax.map(attend, jnp.arange(tok_dev // block, dtype=jnp.int32)).reshape(

time: 537 us -> 622 us (1.16); the launches traced: 526 us -> 619 us
  local copies, waits for them, and re-layouts: 27.4 us -> 98.4 us
  other arithmetic: 48.1 us -> 79.2 us
  loops' own time: 3.05 us -> 28.4 us
  matrix products: 174 us -> 154 us
  waiting for transfers between devices: 216 us -> 202 us
    sub x4 -> x0, matrix products: 58 us -> none  [attend(): weights = jnp.exp(logits - top)]
    dynamic_slice x0 -> x40, local copies, waits for them, and re-layouts: none -> 51.2 us  [the longest x16 36.7 us: attend(): lax.dynamic_slice_in_dim(keys, first, window, 0)]
    reduce_sum x0 -> x24, other arithmetic: none -> 40.5 us  [the longest x8 31.7 us: attend(): jnp.sum(text_w, axis=2, keepdims=True)]
    another operation x1, loops' own time: 3.05 us -> 28.4 us  [shards(): lax.map(attend, jnp.arange(tok_dev // block, dtype=jnp.int32))]
    while x0 -> x8, matrix products: none -> 22.5 us
    dot_general x4 -> x24, matrix products: 64.8 us -> 80.5 us  [the longest x8 34.8 us: attend(): jnp.einsum('qhe,khe->hqk', q_block, k_win, preferred_element_type=jnp.flo...]
    all_gather x1, waiting for transfers between devices: 24.8 us -> 10.7 us  [shards(): whole = lax.all_gather(tokens, 'tensor', axis=0, tiled=True)]
    concatenate x2 -> x0, local copies, waits for them, and re-layouts: 8.26 us -> none  [the longest x1 4.14 us: shards(): jnp.concatenate([values, prompt_value], axis=0)]
  transfers between devices with their start and end apart: 8 -> 8, of which waited for: 8 -> 7; matrix products, arithmetic and copies ran while one was open for 2% -> 4% of each run, Pallas kernels for 0% -> 0%
where the time goes in v3:
time: 622 us; the launch traced here: 619 us
  waiting for transfers between devices  202 us (32%)
  matrix products  154 us (25%)
  local copies, waits for them, and re-layouts  98.4 us (16%)
  other arithmetic  79.2 us (13%)
  starting transfers between devices  29.9 us (5%)
  loops' own time  28.4 us (5%)
  blocking collectives  14.1 us (2%)
  between operations  13.4 us (2%)
    reduce_scatter x1, waiting for transfers between devices, shards(): lax.psum_scatter(jnp.dot(context, w_out, preferred_element_type=jnp.float...  47.7 us
    all_gather x1, waiting for transfers between devices, shards(): lax.all_gather(normed_rows, 'tensor', axis=0, tiled=True)  46.9 us
    reduce_scatter x1, waiting for transfers between devices, shards(): lax.psum_scatter(jnp.dot(expanded, w_down, preferred_element_type=jnp.flo...  46.6 us
    dynamic_slice x16, local copies, waits for them, and re-layouts, attend(): lax.dynamic_slice_in_dim(keys, first, window, 0)  36.7 us
    dot_general x8, matrix products, attend(): jnp.einsum('qhe,khe->hqk', q_block, k_win, preferred_element_type=jnp.flo...  34.8 us
    dot_general x8, matrix products, attend(): jnp.einsum('hqk,khe->qhe', text_p, v_win, preferred_element_type=jnp.floa...  32.8 us
    reduce_sum x8, other arithmetic, attend(): jnp.sum(text_w, axis=2, keepdims=True)  31.7 us
    all_to_all x1, waiting for transfers between devices, shards(): lax.all_to_all(jnp.broadcast_to(own_kv[None], (n_dp,) + own_kv.shape), 'd...  29 us
  transfers between devices with their start and end apart: 8, of which 7 were waited for; matrix products, arithmetic and copies ran while one was open for 4% of the time, Pallas kernels for 0%

profile of v3, /device:TPU:0, one launch (start us, length us, event | category | flops | bytes accessed | tf_op | source)
XLA Modules:
  0.0 619.4 jit_solution(9526944083609288161)
XLA Ops:
  11.5 10.9 %all-to-all-start.1 = ((bf16[32,64,512]{2,1,0:T(8,128)(2,1)}), bf16[32,64,512]{2,1,0:T(8,128)(2,1)}, u32[]{:S(2)}, u32[]{:S(2)}) async-start(bf16[32,64,512]{2,1,0:T(8,128)(2,1)} %broadcast_in_dim.90), calls=%async_computation.1 | async-start | bytes 4194304 | tf_op jit(solution)/shard_map/all_to_all | solution.py:50
  23.0 29.0 %all-to-all-done.1 = bf16[32,64,512]{2,1,0:T(8,128)(2,1)} async-done(((bf16[32,64,512]{2,1,0:T(8,128)(2,1)}), bf16[32,64,512]{2,1,0:T(8,128)(2,1)}, u32[]{:S(2)}, u32[]{:S(2)}) %all-to-all-start.1) | async-done | bytes 2097184 | tf_op jit(solution)/shard_map/all_to_all | solution.py:50
  54.7 4.5 reshape.209
  64.5 4.3 copy.42
  68.8 10.7 %all-gather.3.cloned.1.call-done = bf16[2048,1024]{1,0:T(8,128)(2,1)} async-done(((bf16[512,1024]{1,0:T(8,128)(2,1)}), bf16[2048,1024]{1,0:T(8,128)(2,1)}) %all-gather.3.cloned.1.call-update) | async-done | bytes 4194320 | tf_op jit(solution)/shard_map/all_gather | solution.py:41
  79.5 4.7 convolution_convert_fusion.2
  88.8 251.7 %while.11 = (s32[]{:T(128)}, bf16[8,256,256]{2,1,0:T(8,128)(2,1)}, s32[8]{0:T(128)S(1)}, s32[2048]{0:T(1024)S(1)}, s32[32]{0:T(128)S(1)}, /*index=5*/bf16[2048,2...) while((s32[]{:T(128)}, bf16[8,256,256]{2,1,0:T(8,128)(2,1)}, ...), condition=%wide.region_9.10_spmd.clone, body=%wide.region_3.9_spmd.clone.sunk | while | flops 891295744 | bytes 50050420 | solution.py:106
  104.1 4.4 select_reduce_fusion.7
  115.3 4.1 fusion.127
  135.6 4.4 select_reduce_fusion.7
  167.1 4.4 select_reduce_fusion.7
  178.3 4.1 fusion.127
  198.5 4.4 select_reduce_fusion.7
  209.7 4.1 fusion.127
  230.0 4.4 select_reduce_fusion.7
  241.2 4.1 fusion.127
  261.4 4.4 select_reduce_fusion.7
  272.6 4.1 fusion.127
  292.9 4.4 select_reduce_fusion.7
  304.1 4.1 fusion.127
  324.4 4.4 select_reduce_fusion.7
  340.4 4.6 convolution_convert_fusion
  345.2 47.7 %reduce-scatter.4.cloned.1.call-done = bf16[512,1024]{1,0:T(8,128)(2,1)} async-done(((bf16[2048,1024]{1,0:T(8,128)(2,1)}), bf16[512,1024]{1,0:T(8,128)(2,1)}) %reduce-scatter.4.cloned.1.call-update) | async-done | bytes 1048592 | tf_op jit(solution)/shard_map/reduce_scatter | solution.py:110
  399.1 46.9 %all-gather.5.cloned.1.call-done = bf16[2048,1024]{1,0:T(8,128)(2,1)} async-done(((bf16[512,1024]{1,0:T(8,128)(2,1)}), bf16[2048,1024]{1,0:T(8,128)(2,1)}) %all-gather.5.cloned.1.call-update) | async-done | bytes 4194320 | tf_op jit(solution)/shard_map/all_gather | solution.py:121
  446.0 28.5 %fusion.30 = bf16[2048,1024]{1,0:T(8,128)(2,1)} fusion(bf16[1024,1024]{1,0:T(8,128)(2,1)S(1)} %copy-done, f32[1024]{0:T(1024)S(1)} %copy-done.12, bf16[2048,1024]{1,0:T(8,128)(2,1)} %all-gather.5.cloned.1.call-done, bf16[1024,1024]{1,0:T(8,128)(2,1)} %param.21), kind=kOutput, calls=%fused_computation.49 | convolution fusion | flops 8730443776 | bytes 12587008 | tf_op jit(solution)/shard_map/dot_general | solution.py:129
  475.0 46.6 %reduce-scatter.6.cloned.1.call-done = bf16[512,1024]{1,0:T(8,128)(2,1)} async-done(((bf16[2048,1024]{1,0:T(8,128)(2,1)}), bf16[512,1024]{1,0:T(8,128)(2,1)}) %reduce-scatter.6.cloned.1.call-update) | async-done | bytes 1048592 | tf_op jit(solution)/shard_map/reduce_scatter | solution.py:128
  528.3 9.4 %all-to-all-start = ((s32[32,1,512]{2,1,0:T(1,128)}), s32[32,1,512]{2,1,0:T(1,128)S(1)}, u32[]{:S(2)}, u32[]{:S(2)}) async-start(s32[32,1,512]{2,1,0:T(1,128)} %reshape.212), calls=%async_computation | async-start | bytes 131072 | tf_op jit(solution)/shard_map/all_to_all | solution.py:149
  537.8 8.1 %reduce-scatter.8.cloned.1.call-done = f32[8,1024]{1,0:T(8,128)} async-done(((f32[32,1024]{1,0:T(8,128)}), f32[8,1024]{1,0:T(8,128)}) %reduce-scatter.8.cloned.1.call-update) | async-done | bytes 32784 | tf_op jit(solution)/shard_map/reduce_scatter | solution.py:140
  548.5 9.2 %all-to-all-start.2 = ((bf16[32,8,1024]{2,1,0:T(8,128)(2,1)}), bf16[32,8,1024]{2,1,0:T(8,128)(2,1)S(1)}, u32[]{:S(2)}, u32[]{:S(2)}) async-start(bf16[32,8,1024]{2,1,0:T(8,128)(2,1)} %broadcast_in_dim.91), calls=%async_computation.5 | async-start | bytes 1048576 | tf_op jit(solution)/shard_map/all_to_all | solution.py:146
  559.2 12.2 %all-to-all-done.2 = bf16[32,8,1024]{2,1,0:T(8,128)(2,1)S(1)} async-done(((bf16[32,8,1024]{2,1,0:T(8,128)(2,1)}), bf16[32,8,1024]{2,1,0:T(8,128)(2,1)S(1)}, u32[]{:S(2)}, u32[]{:S(2)}) %all-to-all-start.2) | async-done | bytes 524320 | tf_op jit(solution)/shard_map/all_to_all | solution.py:146
  574.8 21.8 %select_reduce_fusion.2 = f32[256,64]{1,0:T(8,128)S(1)} fusion(f32[256,2048]{1,0:T(8,128)S(1)} %convolution_multiply_fusion, s32[256,64]{1,0:T(8,128)S(1)} %subtract_bitcast_fusion), kind=kLoop, calls=%fused_computation.27 | loop fusion | flops 100646912 | bytes 2228224 | tf_op jit(solution)/shard_map/reduce_sum | solution.py:156
  596.8 14.1 %all_to_all.24 = f32[32,1,512]{2,1,0:T(1,128)S(1)} all-to-all(f32[32,1,512]{2,1,0:T(1,128)S(1)} %reshape.214), channel_id=1, replica_groups=mesh['dp'=32,'tensor'=4] {'dp'}, dimensions={0} | all-to-all | bytes 131072 | tf_op jit(solution)/shard_map/all_to_all | solution.py:160
  (292 shorter events, 205.0 us)
Async XLA Ops:
  6.5 439.5 %copy-start = (bf16[1024,1024]{1,0:T(8,128)(2,1)S(1)}, bf16[1024,1024]{1,0:T(8,128)(2,1)}, u32[]{:S(2)}) copy-start(bf16[1024,1024]{1,0:T(8,128)(2,1)} %param.23) | copy-start | bytes 6291460
  6.5 15.9 %copy-start.8 = (s32[1,32]{1,0:T(1,128)S(1)}, s32[1,32]{1,0:T(1,128)}, u32[]{:S(2)}) copy-start(s32[1,32]{1,0:T(1,128)} %param.25) | copy-start | bytes 388
  6.5 16.3 %copy-start.7 = (s32[32]{0:T(128)S(1)}, s32[32]{0:T(128)}, u32[]{:S(2)}) copy-start(s32[32]{0:T(128)} %param.26) | copy-start | bytes 388
  6.5 73.0 %all-gather.3.cloned.1.call-start = ((), (), s32[]{:S(2)}) async-start(), calls=%async_computation.7 | async-start | bytes 5242880 | tf_op jit(solution)/shard_map/all_gather | solution.py:41
  11.5 40.5 %all-to-all-start.1 = ((bf16[32,64,512]{2,1,0:T(8,128)(2,1)}), bf16[32,64,512]{2,1,0:T(8,128)(2,1)}, u32[]{:S(2)}, u32[]{:S(2)}) async-start(bf16[32,64,512]{2,1,0:T(8,128)(2,1)} %broadcast_in_dim.90), calls=%async_computation.1 | async-start | bytes 4194304 | tf_op jit(solution)/shard_map/all_to_all | solution.py:50
  22.4 370.5 %reduce-scatter.4.cloned.1.call-start = ((), (), s32[]{:S(2)}) async-start(), calls=%async_computation.8 | async-start | bytes 5242880 | tf_op jit(solution)/shard_map/reduce_scatter | solution.py:110
  79.5 4.7 copy-start.10
  79.5 4.7 copy-start.11
  108.5 4.1 copy-start.3
  140.0 4.1 copy-start.3
  171.5 4.1 copy-start.3
  202.9 4.1 copy-start.3
  234.4 4.1 copy-start.3
  265.8 4.1 copy-start.3
  297.3 4.1 copy-start.3
  328.8 4.1 copy-start.3
  340.4 4.7 copy-start.4
  340.4 4.7 copy-start.5
  340.4 52.4 %copy-start.1 = (bf16[512,1024]{1,0:T(8,128)(2,1)S(1)}, bf16[512,1024]{1,0:T(8,128)(2,1)}, u32[]{:S(2)}) copy-start(bf16[512,1024]{1,0:T(8,128)(2,1)} %param.15) | copy-start | bytes 3145732
  345.1 101.0 %copy-start.12 = (f32[1024]{0:T(1024)S(1)}, f32[1024]{0:T(1024)}, u32[]{:S(2)}) copy-start(f32[1024]{0:T(1024)} %param.22) | copy-start | bytes 12292
  345.1 100.9 %all-gather.5.cloned.1.call-start = ((), (), s32[]{:S(2)}) async-start(), calls=%async_computation.9 | async-start | bytes 5242880 | tf_op jit(solution)/shard_map/all_gather | solution.py:121
  399.0 122.6 %copy-start.2 = (bf16[512,1024]{1,0:T(8,128)(2,1)S(1)}, bf16[512,1024]{1,0:T(8,128)(2,1)}, u32[]{:S(2)}) copy-start(bf16[512,1024]{1,0:T(8,128)(2,1)} %add_convert_fusion.1) | copy-start | bytes 3145732
  399.1 122.6 %reduce-scatter.6.cloned.1.call-start = ((), (), s32[]{:S(2)}) async-start(), calls=%async_computation.10 | async-start | bytes 5242880 | tf_op jit(solution)/shard_map/reduce_scatter | solution.py:128
  474.6 53.0 %copy-start.6 = (s32[8,64]{1,0:T(8,128)S(1)}, s32[8,64]{1,0:T(8,128)}, u32[]{:S(2)}) copy-start(s32[8,64]{1,0:T(8,128)} %param.27) | copy-start | bytes 6148
  474.6 63.1 %copy-start.9 = (s32[1,32]{1,0:T(1,128)S(1)}, s32[1,32]{1,0:T(1,128)}, u32[]{:S(2)}) copy-start(s32[1,32]{1,0:T(1,128)} %param.25) | copy-start | bytes 388
  474.6 71.3 %reduce-scatter.8.cloned.1.call-start = ((), (), s32[]{:S(2)}) async-start(), calls=%async_computation.11 | async-start | bytes 163840 | tf_op jit(solution)/shard_map/reduce_scatter | solution.py:140
  528.3 19.4 %all-to-all-start = ((s32[32,1,512]{2,1,0:T(1,128)}), s32[32,1,512]{2,1,0:T(1,128)S(1)}, u32[]{:S(2)}, u32[]{:S(2)}) async-start(s32[32,1,512]{2,1,0:T(1,128)} %reshape.212), calls=%async_computation | async-start | bytes 131072 | tf_op jit(solution)/shard_map/all_to_all | solution.py:149
  548.5 22.8 %all-to-all-start.2 = ((bf16[32,8,1024]{2,1,0:T(8,128)(2,1)}), bf16[32,8,1024]{2,1,0:T(8,128)(2,1)S(1)}, u32[]{:S(2)}, u32[]{:S(2)}) async-start(bf16[32,8,1024]{2,1,0:T(8,128)(2,1)} %broadcast_in_dim.91), calls=%async_computation.5 | async-start | bytes 1048576 | tf_op jit(solution)/shard_map/all_to_all | solution.py:146
Sparse Core Ops, SparseCore 0:
  9.0 70.4 all-gather.2
  345.2 47.6 reduce-scatter.3
  399.2 46.8 all-gather.4
  474.7 46.8 reduce-scatter.5
  527.6 18.1 reduce-scatter.7

commit v4 on v2

--- a/solution.py
+++ b/solution.py
@@ -2,9 +2,73 @@
 import jax.numpy as jnp
 from jax import lax
 from jax.sharding import PartitionSpec as P
+import functools
+from jax.experimental import pallas as pl
+from jax.experimental.pallas import tpu as pltpu
+
 
 D = 1024
 HEAD_DIM = 64
+
+
+def attention_kernel(first_ref, q_ref, k_ref, v_ref, pk_ref, pv_ref, segq_ref, segw_ref, grpq_ref, kgrp_ref, o_ref, *, window):
+    b = pl.program_id(1)
+    f = pl.multiple_of(first_ref[b], 128)
+    q = q_ref[0]
+    kw = k_ref[0, pl.ds(f, window), :]
+    vw = v_ref[0, pl.ds(f, window), :]
+    nt = (((1,), (1,)), ((), ()))
+    lt = lax.dot_general(q, kw, nt, preferred_element_type=jnp.float32)
+    lt = jnp.where(segq_ref[...] == segw_ref[0], lt, jnp.float32(-1e30))
+    lp = lax.dot_general(q, pk_ref[0], nt, preferred_element_type=jnp.float32)
+    lp = jnp.where(grpq_ref[...] == kgrp_ref[...], lp, jnp.float32(-1e30))
+    top = jnp.maximum(jnp.max(lt, axis=1, keepdims=True), jnp.max(lp, axis=1, keepdims=True))
+    wt = jnp.exp(lt - top)
+    wp = jnp.exp(lp - top)
+    total = jnp.sum(wt, axis=1, keepdims=True) + jnp.sum(wp, axis=1, keepdims=True)
+    pt = (wt / total).astype(jnp.bfloat16)
+    pp = (wp / total).astype(jnp.bfloat16)
+    out = jnp.dot(pt, vw, preferred_element_type=jnp.float32) + jnp.dot(
+        pp, pv_ref[0], preferred_element_type=jnp.float32)
+    o_ref[0] = out.astype(jnp.bfloat16)
+
+def attention(query, keys, values, prompt_key, prompt_value, seg, tok_group, starts, prompt_len, head_dim, interpret=False):
+    tok, cols = query.shape
+    heads = cols // head_dim
+    block = 256
+    window = 1408
+    nb = tok // block
+    prow = prompt_key.shape[0]
+    def by_head(x):
+        return x.reshape(x.shape[0], heads, head_dim).transpose(1, 0, 2)
+    first = jnp.clip((starts[seg[::block]] // 128) * 128, 0, tok - window).astype(jnp.int32)
+    segw = jnp.take(seg, first[:, None] + jnp.arange(window, dtype=jnp.int32)[None, :], axis=0).reshape(nb, 1, window)
+    segq = seg.reshape(tok, 1)
+    grpq = tok_group.reshape(tok, 1)
+    kgrp = (jnp.arange(prow, dtype=jnp.int32) // prompt_len).reshape(1, prow)
+    grid_spec = pltpu.PrefetchScalarGridSpec(
+        num_scalar_prefetch=1,
+        grid=(heads, nb),
+        in_specs=[
+            pl.BlockSpec((1, block, head_dim), lambda h, b, fr: (h, b, 0)),
+            pl.BlockSpec((1, tok, head_dim), lambda h, b, fr: (h, 0, 0)),
+            pl.BlockSpec((1, tok, head_dim), lambda h, b, fr: (h, 0, 0)),
+            pl.BlockSpec((1, prow, head_dim), lambda h, b, fr: (h, 0, 0)),
+            pl.BlockSpec((1, prow, head_dim), lambda h, b, fr: (h, 0, 0)),
+            pl.BlockSpec((block, 1), lambda h, b, fr: (b, 0)),
+            pl.BlockSpec((1, 1, window), lambda h, b, fr: (b, 0, 0)),
+            pl.BlockSpec((block, 1), lambda h, b, fr: (b, 0)),
+            pl.BlockSpec((1, prow), lambda h, b, fr: (0, 0)),
+        ],
+        out_specs=pl.BlockSpec((1, block, head_dim), lambda h, b, fr: (h, b, 0)),
+    )
+    out = pl.pallas_call(
+        functools.partial(attention_kernel, window=window),
+        grid_spec=grid_spec,
+        out_shape=jax.ShapeDtypeStruct((heads, tok, head_dim), jnp.bfloat16),
+        interpret=interpret,
+    )(first, by_head(query), by_head(keys), by_head(values), by_head(prompt_key), by_head(prompt_value), segq, segw, grpq, kgrp)
+    return out.transpose(1, 0, 2).reshape(tok, cols)
 
 
 def layer_norm(values, gain, bias):
@@ -61,32 +125,9 @@
     position = jnp.arange(tok_dev, dtype=jnp.int32)
     seg = jnp.sum((position[:, None] >= ends[None, :]).astype(jnp.int32), axis=1)
     tok_group = jnp.sum(jnp.where(seg[:, None] == text_ids[None, :], groups[None, :], 0), axis=1)
-    key_group = jnp.arange(prompt_rows, dtype=jnp.int32) // prompt_len
-    all_keys = jnp.concatenate([keys, prompt_key], axis=0).reshape(-1, heads_here, HEAD_DIM)
-    all_values = jnp.concatenate([values, prompt_value], axis=0).reshape(-1, heads_here, HEAD_DIM)
-    block = min(512, tok_dev)
-
-    def attend(number):
-        start = number * block
-        q_block = lax.dynamic_slice_in_dim(query, start, block, 0).reshape(
-            block, heads_here, HEAD_DIM
-        )
-        seg_block = lax.dynamic_slice_in_dim(seg, start, block, 0)
-        group_block = lax.dynamic_slice_in_dim(tok_group, start, block, 0)
-        allowed = jnp.concatenate(
-            [seg_block[:, None] == seg[None, :], group_block[:, None] == key_group[None, :]], axis=1
-        )
-        logits = jnp.einsum("qhe,khe->hqk", q_block, all_keys, preferred_element_type=jnp.float32)
-        logits = jnp.where(allowed[None], logits, jnp.float32(-1e30))
-        top = jnp.max(logits, axis=2, keepdims=True)
-        weights = jnp.exp(logits - top)
-        total = jnp.sum(weights, axis=2, keepdims=True)
-        probs = (weights / total).astype(jnp.bfloat16)
-        mixed = jnp.einsum("hqk,khe->qhe", probs, all_values, preferred_element_type=jnp.float32)
-        return mixed.astype(jnp.bfloat16).reshape(block, columns)
-
-    context = lax.map(attend, jnp.arange(tok_dev // block, dtype=jnp.int32)).reshape(
-        tok_dev, columns
+    starts = ends - lens
+    context = attention(
+        query, keys, values, prompt_key, prompt_value, seg, tok_group, starts, prompt_len, HEAD_DIM
     )
     my_start = lax.axis_index("tensor") * shard_rows
     attn_part = lax.psum_scatter(

time: 537 us -> 463 us (0.86); the launches traced: 526 us -> 462 us
  matrix products: 174 us -> 51 us
  Pallas kernels: 0 us -> 67.8 us
  local copies, waits for them, and re-layouts: 27.4 us -> 88.2 us
  waiting for transfers between devices: 216 us -> 161 us
  other arithmetic: 48.1 us -> 36.3 us
    pallas_call x0 -> x1, Pallas kernels: none -> 67.8 us  [attention(): pl.pallas_call(functools.partial(attention_kernel, window=window), grid_s...]
    dot_general x4 -> x0, matrix products: 64.8 us -> none  [attend(): jnp.einsum('hqk,khe->qhe', probs, all_values, preferred_element_type=jnp....]
    gather x0 -> x2, local copies, waits for them, and re-layouts: none -> 63.1 us  [the longest x1 62.4 us: attention(): jnp.take(seg, first[:, None] + jnp.arange(window, dtype=jnp.int32)[None,...]
    sub x4 -> x0, matrix products: 58 us -> none  [attend(): weights = jnp.exp(logits - top)]
    all_to_all x1, waiting for transfers between devices: 29 us -> 0.01 us  [shards(): lax.all_to_all(jnp.broadcast_to(own_kv[None], (n_dp,) + own_kv.shape), 'd...]
    all_gather x1, waiting for transfers between devices: 24.8 us -> 0.01 us  [shards(): whole = lax.all_gather(tokens, 'tensor', axis=0, tiled=True)]
    reshape x0 -> x7, local copies, waits for them, and re-layouts: none -> 11.8 us  [the longest x5 9.02 us: by_head(): return x.reshape(x.shape[0], heads, head_dim).transpose(1, 0, 2)]
    concatenate x2 -> x0, local copies, waits for them, and re-layouts: 8.26 us -> none  [the longest x1 4.14 us: shards(): jnp.concatenate([values, prompt_value], axis=0)]
  transfers between devices with their start and end apart: 8 -> 8, of which waited for: 8 -> 5; matrix products, arithmetic and copies ran while one was open for 2% -> 19% of each run, Pallas kernels for 0% -> 0%
where the time goes in v4:
time: 463 us; the launch traced here: 462 us
  waiting for transfers between devices  161 us (35%)
  local copies, waits for them, and re-layouts  88.2 us (19%)
  Pallas kernels  67.8 us (15%)
  matrix products  51 us (11%)
  other arithmetic  36.3 us (8%)
  starting transfers between devices  30 us (6%)
  blocking collectives  14.1 us (3%)
  between operations  13.4 us (3%)
    pallas_call x1, Pallas kernels, attention(): pl.pallas_call(functools.partial(attention_kernel, window=window), grid_s...  67.8 us
    gather x1, local copies, waits for them, and re-layouts, attention(): jnp.take(seg, first[:, None] + jnp.arange(window, dtype=jnp.int32)[None,...  62.4 us
    all_gather x1, waiting for transfers between devices, shards(): lax.all_gather(normed_rows, 'tensor', axis=0, tiled=True)  46.8 us
    reduce_scatter x1, waiting for transfers between devices, shards(): lax.psum_scatter(jnp.dot(expanded, w_down, preferred_element_type=jnp.flo...  46.7 us
    reduce_scatter x1, waiting for transfers between devices, shards(): lax.psum_scatter(jnp.dot(context, w_out, preferred_element_type=jnp.float...  46.2 us
    dot_general x1, matrix products, shards(): jnp.dot(expanded, w_down, preferred_element_type=jnp.float32)  28.5 us
    reduce_sum x1, other arithmetic, shards(): jnp.sum(jnp.where(local_rows[:, :, None] == row_ids[None, None, :], table...  21.8 us
    all_to_all x1, blocking collectives, shards(): returned = lax.all_to_all(picked, 'dp', 0, 0, tiled=True)  14.1 us
  transfers between devices with their start and end apart: 8, of which 5 were waited for; matrix products, arithmetic and copies ran while one was open for 19% of the time, Pallas kernels for 0%

profile of v4, /device:TPU:0, one launch (start us, length us, event | category | flops | bytes accessed | tf_op | source)
XLA Modules:
  0.0 461.6 jit_solution(10694559882967663534)
XLA Ops:
  9.9 1.6 broadcast_in_dim.36
  11.5 10.9 %all-to-all-start.1 = ((bf16[32,64,512]{2,1,0:T(8,128)(2,1)}), bf16[32,64,512]{2,1,0:T(8,128)(2,1)}, u32[]{:S(2)}, u32[]{:S(2)}) async-start(bf16[32,64,512]{2,1,0:T(8,128)(2,1)} %broadcast_in_dim.36), calls=%async_computation.1 | async-start | bytes 4194304 | tf_op jit(solution)/shard_map/all_to_all | solution.py:114
  23.8 62.4 %gather_fusion.1 = s32[11264]{0:T(1024)S(1)} fusion(s32[2048]{0:T(1024)S(1)} %convert_reduce_fusion, s32[11264]{0:T(1024)S(1)} %broadcast_clamp_fusion), kind=kCustom, calls=%fused_computation.1 | custom fusion | bytes 135168 | tf_op jit(solution)/shard_map/jit(_take)/gather | solution.py:45
  90.5 3.0 fusion.67
  93.5 1.5 copy.40
  95.0 1.8 copy.41
  98.3 1.8 copy.43
  100.0 3.6 convolution_convert_fusion.1
  103.6 1.8 copy.39
  105.5 3.6 fusion.17
  109.1 1.8 copy.37
  110.9 3.6 convolution_convert_fusion.2
  114.5 1.8 copy.38
  116.3 67.8 %shard_map.127 = bf16[4,2048,64]{2,1,0:T(8,128)(2,1)} custom-call(s32[8]{0:T(128)} %copy-done.7, bf16[4,2048,64]{2,1,0:T(8,128)(2,1)} %bitcast.64, bf16[4,2048,64]{2,1,0:T(8,128)(2,1)} %bitcast.65, bf16[4,2048,64]{2,1,0:T(8,128)(2,1)} %bitcast.63, bf16[4,2048,64]{2,1,0:T(8,128)(2,1)} %bitcast.61, bf16[4,2048,64]{2,1,0:T(8,128)(2,1)} %bitcast.62, ...), custom_call_target="tpu_custom_call" | custom-call | tf_op jit(solution)/shard_map/pallas_call | solution.py:65
  184.1 1.9 copy.46
  186.0 4.3 convolution_convert_fusion
  191.0 46.2 %reduce-scatter.4.cloned.1.call-done = bf16[512,1024]{1,0:T(8,128)(2,1)} async-done(((bf16[2048,1024]{1,0:T(8,128)(2,1)}), bf16[512,1024]{1,0:T(8,128)(2,1)}) %reduce-scatter.4.cloned.1.call-update) | async-done | bytes 1048592 | tf_op jit(solution)/shard_map/reduce_scatter | solution.py:133
  237.2 1.7 fusion.19
  238.9 1.7 multiply_reduce_fusion.1
  240.7 1.6 add_convert_fusion.1
  242.5 46.8 %all-gather.5.cloned.1.call-done = bf16[2048,1024]{1,0:T(8,128)(2,1)} async-done(((bf16[512,1024]{1,0:T(8,128)(2,1)}), bf16[2048,1024]{1,0:T(8,128)(2,1)}) %all-gather.5.cloned.1.call-update) | async-done | bytes 4194320 | tf_op jit(solution)/shard_map/all_gather | solution.py:144
  289.3 28.5 %fusion.12 = bf16[2048,1024]{1,0:T(8,128)(2,1)} fusion(bf16[1024,1024]{1,0:T(8,128)(2,1)S(1)} %copy-done, f32[1024]{0:T(1024)S(1)} %copy-done.11, bf16[2048,1024]{1,0:T(8,128)(2,1)} %all-gather.5.cloned.1.call-done, bf16[1024,1024]{1,0:T(8,128)(2,1)} %param.19), kind=kOutput, calls=%fused_computation.24 | convolution fusion | flops 8730443776 | bytes 12587008 | tf_op jit(solution)/shard_map/dot_general | solution.py:152
  318.2 46.7 %reduce-scatter.6.cloned.1.call-done = bf16[512,1024]{1,0:T(8,128)(2,1)} async-done(((bf16[2048,1024]{1,0:T(8,128)(2,1)}), bf16[512,1024]{1,0:T(8,128)(2,1)}) %reduce-scatter.6.cloned.1.call-update) | async-done | bytes 1048592 | tf_op jit(solution)/shard_map/reduce_scatter | solution.py:151
  364.9 1.7 fusion.21
  366.6 1.7 multiply_reduce_fusion
  370.5 9.4 %all-to-all-start = ((s32[32,1,512]{2,1,0:T(1,128)}), s32[32,1,512]{2,1,0:T(1,128)S(1)}, u32[]{:S(2)}, u32[]{:S(2)}) async-start(s32[32,1,512]{2,1,0:T(1,128)} %reshape.309), calls=%async_computation | async-start | bytes 131072 | tf_op jit(solution)/shard_map/all_to_all | solution.py:172
  380.0 8.1 %reduce-scatter.8.cloned.1.call-done = f32[8,1024]{1,0:T(8,128)} async-done(((f32[32,1024]{1,0:T(8,128)}), f32[8,1024]{1,0:T(8,128)}) %reduce-scatter.8.cloned.1.call-update) | async-done | bytes 32784 | tf_op jit(solution)/shard_map/reduce_scatter | solution.py:163
  390.7 9.2 %all-to-all-start.2 = ((bf16[32,8,1024]{2,1,0:T(8,128)(2,1)}), bf16[32,8,1024]{2,1,0:T(8,128)(2,1)S(1)}, u32[]{:S(2)}, u32[]{:S(2)}) async-start(bf16[32,8,1024]{2,1,0:T(8,128)(2,1)} %broadcast_in_dim.40), calls=%async_computation.5 | async-start | bytes 1048576 | tf_op jit(solution)/shard_map/all_to_all | solution.py:169
  401.4 12.2 %all-to-all-done.2 = bf16[32,8,1024]{2,1,0:T(8,128)(2,1)S(1)} async-done(((bf16[32,8,1024]{2,1,0:T(8,128)(2,1)}), bf16[32,8,1024]{2,1,0:T(8,128)(2,1)S(1)}, u32[]{:S(2)}, u32[]{:S(2)}) %all-to-all-start.2) | async-done | bytes 524320 | tf_op jit(solution)/shard_map/all_to_all | solution.py:169
  413.5 3.5 convolution_multiply_fusion
  417.0 21.8 %select_reduce_fusion = f32[256,64]{1,0:T(8,128)S(1)} fusion(f32[256,2048]{1,0:T(8,128)S(1)} %convolution_multiply_fusion, s32[256,64]{1,0:T(8,128)S(1)} %subtract_bitcast_fusion), kind=kLoop, calls=%fused_computation.2 | loop fusion | flops 100646912 | bytes 2228224 | tf_op jit(solution)/shard_map/reduce_sum | solution.py:179
  439.0 14.1 %all_to_all.24 = f32[32,1,512]{2,1,0:T(1,128)S(1)} all-to-all(f32[32,1,512]{2,1,0:T(1,128)S(1)} %reshape.311), channel_id=1, replica_groups=mesh['dp'=32,'tensor'=4] {'dp'}, dimensions={0} | all-to-all | bytes 131072 | tf_op jit(solution)/shard_map/all_to_all | solution.py:183
  (83 shorter events, 20.2 us)
Async XLA Ops:
  6.5 282.8 %copy-start = (bf16[1024,1024]{1,0:T(8,128)(2,1)S(1)}, bf16[1024,1024]{1,0:T(8,128)(2,1)}, u32[]{:S(2)}) copy-start(bf16[1024,1024]{1,0:T(8,128)(2,1)} %param.21) | copy-start | bytes 6291460
  6.5 93.5 %all-gather.3.cloned.1.call-start = ((), (), s32[]{:S(2)}) async-start(), calls=%async_computation.7 | async-start | bytes 5242880 | tf_op jit(solution)/shard_map/all_gather | solution.py:105
  7.3 15.2 %copy-start.10 = (s32[1,32]{1,0:T(1,128)S(1)}, s32[1,32]{1,0:T(1,128)}, u32[]{:S(2)}) copy-start(s32[1,32]{1,0:T(1,128)} %param.23) | copy-start | bytes 388
  11.5 78.9 %all-to-all-start.1 = ((bf16[32,64,512]{2,1,0:T(8,128)(2,1)}), bf16[32,64,512]{2,1,0:T(8,128)(2,1)}, u32[]{:S(2)}, u32[]{:S(2)}) async-start(bf16[32,64,512]{2,1,0:T(8,128)(2,1)} %broadcast_in_dim.36), calls=%async_computation.1 | async-start | bytes 4194304 | tf_op jit(solution)/shard_map/all_to_all | solution.py:114
  22.4 214.8 %reduce-scatter.4.cloned.1.call-start = ((), (), s32[]{:S(2)}) async-start(), calls=%async_computation.8 | async-start | bytes 5242880 | tf_op jit(solution)/shard_map/reduce_scatter | solution.py:133
  23.6 66.1 %copy-start.7 = (s32[8]{0:T(128)}, s32[8]{0:T(128)S(1)}, u32[]{:S(2)}) copy-start(s32[8]{0:T(128)S(1)} %multiply_clamp_fusion.first_ref) | copy-start | bytes 100
  23.7 62.4 %copy-start.9 = (s32[32]{0:T(128)S(1)}, s32[32]{0:T(128)}, u32[]{:S(2)}) copy-start(s32[32]{0:T(128)} %param.24) | copy-start | bytes 388
  190.3 0.7 copy-start.5
  190.3 0.7 copy-start.6
  190.3 47.0 %copy-start.1 = (bf16[512,1024]{1,0:T(8,128)(2,1)S(1)}, bf16[512,1024]{1,0:T(8,128)(2,1)}, u32[]{:S(2)}) copy-start(bf16[512,1024]{1,0:T(8,128)(2,1)} %param.13) | copy-start | bytes 3145732
  190.3 99.0 %all-gather.5.cloned.1.call-start = ((), (), s32[]{:S(2)}) async-start(), calls=%async_computation.9 | async-start | bytes 5242880 | tf_op jit(solution)/shard_map/all_gather | solution.py:144
  191.0 98.3 %copy-start.11 = (f32[1024]{0:T(1024)S(1)}, f32[1024]{0:T(1024)}, u32[]{:S(2)}) copy-start(f32[1024]{0:T(1024)} %param.20) | copy-start | bytes 12292
  237.2 3.4 copy-start.3
  242.3 122.6 %reduce-scatter.6.cloned.1.call-start = ((), (), s32[]{:S(2)}) async-start(), calls=%async_computation.10 | async-start | bytes 5242880 | tf_op jit(solution)/shard_map/reduce_scatter | solution.py:151
  317.9 47.1 %copy-start.2 = (bf16[512,1024]{1,0:T(8,128)(2,1)S(1)}, bf16[512,1024]{1,0:T(8,128)(2,1)}, u32[]{:S(2)}) copy-start(bf16[512,1024]{1,0:T(8,128)(2,1)} %add_convert_fusion.1) | copy-start | bytes 3145732
  317.9 51.8 %copy-start.8 = (s32[8,64]{1,0:T(8,128)S(1)}, s32[8,64]{1,0:T(8,128)}, u32[]{:S(2)}) copy-start(s32[8,64]{1,0:T(8,128)} %param.25) | copy-start | bytes 6148
  317.9 70.2 %reduce-scatter.8.cloned.1.call-start = ((), (), s32[]{:S(2)}) async-start(), calls=%async_computation.11 | async-start | bytes 163840 | tf_op jit(solution)/shard_map/reduce_scatter | solution.py:163
  364.9 3.4 copy-start.4
  370.5 19.4 %all-to-all-start = ((s32[32,1,512]{2,1,0:T(1,128)}), s32[32,1,512]{2,1,0:T(1,128)S(1)}, u32[]{:S(2)}, u32[]{:S(2)}) async-start(s32[32,1,512]{2,1,0:T(1,128)} %reshape.309), calls=%async_computation | async-start | bytes 131072 | tf_op jit(solution)/shard_map/all_to_all | solution.py:172
  390.7 22.8 %all-to-all-start.2 = ((bf16[32,8,1024]{2,1,0:T(8,128)(2,1)}), bf16[32,8,1024]{2,1,0:T(8,128)(2,1)S(1)}, u32[]{:S(2)}, u32[]{:S(2)}) async-start(bf16[32,8,1024]{2,1,0:T(8,128)(2,1)} %broadcast_in_dim.40), calls=%async_computation.5 | async-start | bytes 1048576 | tf_op jit(solution)/shard_map/all_to_all | solution.py:169
Sparse Core Ops, SparseCore 0:
  9.0 70.4 all-gather.2
  190.4 46.7 reduce-scatter.3
  242.4 46.8 all-gather.4
  318.0 46.8 reduce-scatter.5
  369.8 18.1 reduce-scatter.7

commit v5 on v4

--- a/solution.py
+++ b/solution.py
@@ -32,7 +32,7 @@
         pp, pv_ref[0], preferred_element_type=jnp.float32)
     o_ref[0] = out.astype(jnp.bfloat16)
 
-def attention(query, keys, values, prompt_key, prompt_value, seg, tok_group, starts, prompt_len, head_dim, interpret=False):
+def attention(query, keys, values, prompt_key, prompt_value, seg, tok_group, ends, starts, prompt_len, head_dim, interpret=False):
     tok, cols = query.shape
     heads = cols // head_dim
     block = 256
@@ -42,7 +42,8 @@
     def by_head(x):
         return x.reshape(x.shape[0], heads, head_dim).transpose(1, 0, 2)
     first = jnp.clip((starts[seg[::block]] // 128) * 128, 0, tok - window).astype(jnp.int32)
-    segw = jnp.take(seg, first[:, None] + jnp.arange(window, dtype=jnp.int32)[None, :], axis=0).reshape(nb, 1, window)
+    at = first[:, None] + jnp.arange(window, dtype=jnp.int32)[None, :]
+    segw = jnp.sum((at[:, :, None] >= ends[None, None, :]).astype(jnp.int32), axis=2).reshape(nb, 1, window)
     segq = seg.reshape(tok, 1)
     grpq = tok_group.reshape(tok, 1)
     kgrp = (jnp.arange(prow, dtype=jnp.int32) // prompt_len).reshape(1, prow)
@@ -127,7 +128,7 @@
     tok_group = jnp.sum(jnp.where(seg[:, None] == text_ids[None, :], groups[None, :], 0), axis=1)
     starts = ends - lens
     context = attention(
-        query, keys, values, prompt_key, prompt_value, seg, tok_group, starts, prompt_len, HEAD_DIM
+        query, keys, values, prompt_key, prompt_value, seg, tok_group, ends, starts, prompt_len, HEAD_DIM
     )
     my_start = lax.axis_index("tensor") * shard_rows
     attn_part = lax.psum_scatter(
@@ -136,6 +137,10 @@
         scatter_dimension=0,
         tiled=True,
     ).astype(jnp.float32)
+    asked_rows = lax.all_to_all(
+        jnp.broadcast_to(candidates[None], (n_dp,) + candidates.shape), "dp", 0, 0, tiled=True
+    ).reshape(-1, candidates.shape[1])
+    asked_rows, attn_part = lax.optimization_barrier((asked_rows, attn_part))
     normed_rows = layer_norm(
         tokens.astype(jnp.float32) + attn_part, norm_gain[0], norm_bias[0]
     ).astype(jnp.bfloat16)
@@ -169,9 +174,6 @@
     asked_vectors = lax.all_to_all(
         jnp.broadcast_to(embedding[None], (n_dp,) + embedding.shape), "dp", 0, 0, tiled=True
     ).reshape(-1, embedding.shape[1])
-    asked_rows = lax.all_to_all(
-        jnp.broadcast_to(candidates[None], (n_dp,) + candidates.shape), "dp", 0, 0, tiled=True
-    ).reshape(-1, candidates.shape[1])
     held = index_rows.shape[0]
     local_rows = asked_rows - lax.axis_index("dp") * held
     table = jnp.dot(asked_vectors, index_rows.T, preferred_element_type=jnp.float32) * D ** (-0.5)

time: 463 us -> 442 us (0.955)
  local copies, waits for them, and re-layouts: 88.2 us -> 26.5 us
  waiting for transfers between devices: 161 us -> 203 us
    gather x1 -> x0, local copies, waits for them, and re-layouts: 62.4 us -> none  [attention(): jnp.take(seg, first[:, None] + jnp.arange(window, dtype=jnp.int32)[None,...]
    all_to_all x1, waiting for transfers between devices: 0.01 us -> 23.9 us  [shards(): lax.all_to_all(jnp.broadcast_to(own_kv[None], (n_dp,) + own_kv.shape), 'd...]
    reduce_scatter x1, waiting for transfers between devices: 46.2 us -> 24.9 us  [shards(): lax.psum_scatter(jnp.dot(context, w_out, preferred_element_type=jnp.float...]
    all_gather x1, waiting for transfers between devices: 0.01 us -> 17.9 us  [shards(): whole = lax.all_gather(tokens, 'tensor', axis=0, tiled=True)]
    reduce_scatter x1, waiting for transfers between devices: 8.1 us -> 18.1 us  [shards(): lax.psum_scatter(partial_sums, 'tensor', scatter_dimension=0, tiled=True)]
    all_to_all x1, waiting for transfers between devices: 0.03 us -> 9.91 us  [shards(): lax.all_to_all(jnp.broadcast_to(candidates[None], (n_dp,) + candidates.sh...]
  transfers between devices with their start and end apart: 8 -> 8, of which waited for: 5 -> 8; matrix products, arithmetic and copies ran while one was open for 19% -> 5% of each run, Pallas kernels for 0% -> 0%
where the time goes in v5:
time: 442 us; the launch traced here: 441 us
  waiting for transfers between devices  203 us (46%)
  Pallas kernels  67.8 us (15%)
  matrix products  51 us (12%)
  other arithmetic  34.6 us (8%)
  starting transfers between devices  31.3 us (7%)
  local copies, waits for them, and re-layouts  26.5 us (6%)
  blocking collectives  13.8 us (3%)
  between operations  13.4 us (3%)
    pallas_call x1, Pallas kernels, attention(): pl.pallas_call(functools.partial(attention_kernel, window=window), grid_s...  67.8 us
    all_gather x1, waiting for transfers between devices, shards(): lax.all_gather(normed_rows, 'tensor', axis=0, tiled=True)  47 us
    reduce_scatter x1, waiting for transfers between devices, shards(): lax.psum_scatter(jnp.dot(expanded, w_down, preferred_element_type=jnp.flo...  46.7 us
    dot_general x1, matrix products, shards(): jnp.dot(expanded, w_down, preferred_element_type=jnp.float32)  28.5 us
    reduce_scatter x1, waiting for transfers between devices, shards(): lax.psum_scatter(jnp.dot(context, w_out, preferred_element_type=jnp.float...  24.9 us
    all_to_all x1, waiting for transfers between devices, shards(): lax.all_to_all(jnp.broadcast_to(own_kv[None], (n_dp,) + own_kv.shape), 'd...  23.9 us
    reduce_sum x1, other arithmetic, shards(): jnp.sum(jnp.where(local_rows[:, :, None] == row_ids[None, None, :], table...  21.8 us
    reduce_scatter x1, waiting for transfers between devices, shards(): lax.psum_scatter(partial_sums, 'tensor', scatter_dimension=0, tiled=True)  18.1 us
  transfers between devices with their start and end apart: 8, of which 8 were waited for; matrix products, arithmetic and copies ran while one was open for 5% of the time, Pallas kernels for 0%

profile of v5, /device:TPU:0, one launch (start us, length us, event | category | flops | bytes accessed | tf_op | source)
XLA Modules:
  0.0 441.2 jit_solution(14880794275758461511)
XLA Ops:
  10.0 1.6 broadcast_in_dim.30
  11.5 10.9 %all-to-all-start.1 = ((bf16[32,64,512]{2,1,0:T(8,128)(2,1)}), bf16[32,64,512]{2,1,0:T(8,128)(2,1)}, u32[]{:S(2)}, u32[]{:S(2)}) async-start(bf16[32,64,512]{2,1,0:T(8,128)(2,1)} %broadcast_in_dim.30), calls=%async_computation.1 | async-start | bytes 4194304 | tf_op jit(solution)/shard_map/all_to_all | solution.py:115
  28.2 23.9 %all-to-all-done.1 = bf16[32,64,512]{2,1,0:T(8,128)(2,1)} async-done(((bf16[32,64,512]{2,1,0:T(8,128)(2,1)}), bf16[32,64,512]{2,1,0:T(8,128)(2,1)}, u32[]{:S(2)}, u32[]{:S(2)}) %all-to-all-start.1) | async-done | bytes 2097184 | tf_op jit(solution)/shard_map/all_to_all | solution.py:115
  52.0 3.0 fusion.66
  55.1 1.5 copy.40
  56.6 1.8 copy.41
  59.9 1.8 copy.43
  61.7 17.9 %all-gather.3.cloned.1.call-done = bf16[2048,1024]{1,0:T(8,128)(2,1)} async-done(((bf16[512,1024]{1,0:T(8,128)(2,1)}), bf16[2048,1024]{1,0:T(8,128)(2,1)}) %all-gather.3.cloned.1.call-update) | async-done | bytes 4194320 | tf_op jit(solution)/shard_map/all_gather | solution.py:106
  79.6 3.6 convolution_convert_fusion.1
  83.2 1.8 copy.39
  85.0 3.6 fusion.17
  88.6 1.8 copy.37
  90.4 3.6 convolution_convert_fusion.2
  94.0 1.8 copy.38
  95.8 67.8 %shard_map.127 = bf16[4,2048,64]{2,1,0:T(8,128)(2,1)} custom-call(s32[8]{0:T(128)} %copy-done.7, bf16[4,2048,64]{2,1,0:T(8,128)(2,1)} %bitcast.59, bf16[4,2048,64]{2,1,0:T(8,128)(2,1)} %bitcast.60, bf16[4,2048,64]{2,1,0:T(8,128)(2,1)} %bitcast.58, bf16[4,2048,64]{2,1,0:T(8,128)(2,1)} %bitcast.56, bf16[4,2048,64]{2,1,0:T(8,128)(2,1)} %bitcast.57, ...), custom_call_target="tpu_custom_call" | custom-call | tf_op jit(solution)/shard_map/pallas_call | solution.py:66
  163.6 1.9 copy.46
  165.5 4.3 convolution_convert_fusion
  171.2 10.7 %all-to-all-start = ((s32[32,1,512]{2,1,0:T(1,128)}), s32[32,1,512]{2,1,0:T(1,128)S(1)}, u32[]{:S(2)}, u32[]{:S(2)}) async-start(s32[32,1,512]{2,1,0:T(1,128)} %reshape.219), calls=%async_computation | async-start | bytes 131072 | tf_op jit(solution)/shard_map/all_to_all | solution.py:140
  182.0 9.9 %all-to-all-done = s32[32,1,512]{2,1,0:T(1,128)S(1)} async-done(((s32[32,1,512]{2,1,0:T(1,128)}), s32[32,1,512]{2,1,0:T(1,128)S(1)}, u32[]{:S(2)}, u32[]{:S(2)}) %all-to-all-start) | async-done | bytes 65568 | tf_op jit(solution)/shard_map/all_to_all | solution.py:140
  193.3 24.9 %reduce-scatter.4.cloned.1.call-done = bf16[512,1024]{1,0:T(8,128)(2,1)} async-done(((bf16[2048,1024]{1,0:T(8,128)(2,1)}), bf16[512,1024]{1,0:T(8,128)(2,1)}) %reduce-scatter.4.cloned.1.call-update) | async-done | bytes 1048592 | tf_op jit(solution)/shard_map/reduce_scatter | solution.py:134
  220.5 1.6 add_convert_fusion.1
  222.2 47.0 %all-gather.5.cloned.1.call-done = bf16[2048,1024]{1,0:T(8,128)(2,1)} async-done(((bf16[512,1024]{1,0:T(8,128)(2,1)}), bf16[2048,1024]{1,0:T(8,128)(2,1)}) %all-gather.5.cloned.1.call-update) | async-done | bytes 4194320 | tf_op jit(solution)/shard_map/all_gather | solution.py:149
  269.2 28.5 %fusion.12 = bf16[2048,1024]{1,0:T(8,128)(2,1)} fusion(bf16[1024,1024]{1,0:T(8,128)(2,1)S(1)} %copy-done, f32[1024]{0:T(1024)S(1)} %copy-done.10, bf16[2048,1024]{1,0:T(8,128)(2,1)} %all-gather.5.cloned.1.call-done, bf16[1024,1024]{1,0:T(8,128)(2,1)} %param.19), kind=kOutput, calls=%fused_computation.23 | convolution fusion | flops 8730443776 | bytes 12587008 | tf_op jit(solution)/shard_map/dot_general | solution.py:157
  298.1 46.7 %reduce-scatter.6.cloned.1.call-done = bf16[512,1024]{1,0:T(8,128)(2,1)} async-done(((bf16[2048,1024]{1,0:T(8,128)(2,1)}), bf16[512,1024]{1,0:T(8,128)(2,1)}) %reduce-scatter.6.cloned.1.call-update) | async-done | bytes 1048592 | tf_op jit(solution)/shard_map/reduce_scatter | solution.py:156
  344.8 1.7 fusion.19
  346.4 1.7 multiply_reduce_fusion
  349.6 18.1 %reduce-scatter.8.cloned.1.call-done = f32[8,1024]{1,0:T(8,128)} async-done(((f32[32,1024]{1,0:T(8,128)}), f32[8,1024]{1,0:T(8,128)}) %reduce-scatter.8.cloned.1.call-update) | async-done | bytes 32784 | tf_op jit(solution)/shard_map/reduce_scatter | solution.py:168
  370.4 9.4 %all-to-all-start.2 = ((bf16[32,8,1024]{2,1,0:T(8,128)(2,1)}), bf16[32,8,1024]{2,1,0:T(8,128)(2,1)S(1)}, u32[]{:S(2)}, u32[]{:S(2)}) async-start(bf16[32,8,1024]{2,1,0:T(8,128)(2,1)} %broadcast_in_dim.33), calls=%async_computation.5 | async-start | bytes 1048576 | tf_op jit(solution)/shard_map/all_to_all | solution.py:174
  379.8 13.7 %all-to-all-done.2 = bf16[32,8,1024]{2,1,0:T(8,128)(2,1)S(1)} async-done(((bf16[32,8,1024]{2,1,0:T(8,128)(2,1)}), bf16[32,8,1024]{2,1,0:T(8,128)(2,1)S(1)}, u32[]{:S(2)}, u32[]{:S(2)}) %all-to-all-start.2) | async-done | bytes 524320 | tf_op jit(solution)/shard_map/all_to_all | solution.py:174
  393.5 3.5 convolution_multiply_fusion
  397.0 21.8 %select_reduce_fusion = f32[256,64]{1,0:T(8,128)S(1)} fusion(f32[256,2048]{1,0:T(8,128)S(1)} %convolution_multiply_fusion, s32[256,64]{1,0:T(8,128)S(1)} %broadcast_subtract_fusion), kind=kLoop, calls=%fused_computation.1 | loop fusion | flops 100646912 | bytes 2228224 | tf_op jit(solution)/shard_map/reduce_sum | solution.py:181
  418.9 13.8 %all_to_all.24 = f32[32,1,512]{2,1,0:T(1,128)S(1)} all-to-all(f32[32,1,512]{2,1,0:T(1,128)S(1)} %reshape.221), channel_id=1, replica_groups=mesh['dp'=32,'tensor'=4] {'dp'}, dimensions={0} | all-to-all | bytes 131072 | tf_op jit(solution)/shard_map/all_to_all | solution.py:185
  (80 shorter events, 22.4 us)
Async XLA Ops:
  6.5 262.6 %copy-start = (bf16[1024,1024]{1,0:T(8,128)(2,1)S(1)}, bf16[1024,1024]{1,0:T(8,128)(2,1)}, u32[]{:S(2)}) copy-start(bf16[1024,1024]{1,0:T(8,128)(2,1)} %param.21) | copy-start | bytes 6291460
  6.5 73.0 %all-gather.3.cloned.1.call-start = ((), (), s32[]{:S(2)}) async-start(), calls=%async_computation.7 | async-start | bytes 5242880 | tf_op jit(solution)/shard_map/all_gather | solution.py:106
  7.3 15.2 %copy-start.9 = (s32[1,32]{1,0:T(1,128)S(1)}, s32[1,32]{1,0:T(1,128)}, u32[]{:S(2)}) copy-start(s32[1,32]{1,0:T(1,128)} %param.23) | copy-start | bytes 388
  8.6 16.1 %copy-start.8 = (s32[32]{0:T(128)S(1)}, s32[32]{0:T(128)}, u32[]{:S(2)}) copy-start(s32[32]{0:T(128)} %param.24) | copy-start | bytes 388
  11.5 40.5 %all-to-all-start.1 = ((bf16[32,64,512]{2,1,0:T(8,128)(2,1)}), bf16[32,64,512]{2,1,0:T(8,128)(2,1)}, u32[]{:S(2)}, u32[]{:S(2)}) async-start(bf16[32,64,512]{2,1,0:T(8,128)(2,1)} %broadcast_in_dim.30), calls=%async_computation.1 | async-start | bytes 4194304 | tf_op jit(solution)/shard_map/all_to_all | solution.py:115
  22.4 195.8 %reduce-scatter.4.cloned.1.call-start = ((), (), s32[]{:S(2)}) async-start(), calls=%async_computation.8 | async-start | bytes 5242880 | tf_op jit(solution)/shard_map/reduce_scatter | solution.py:134
  23.6 32.9 %copy-start.7 = (s32[8]{0:T(128)}, s32[8]{0:T(128)S(1)}, u32[]{:S(2)}) copy-start(s32[8]{0:T(128)S(1)} %multiply_clamp_fusion.first_ref) | copy-start | bytes 100
  169.8 0.7 copy-start.6
  169.8 12.2 %copy-start.4 = (f32[2,1024]{1,0:T(2,128)S(1)}, f32[2,1024]{1,0:T(2,128)}, u32[]{:S(2)}) copy-start(f32[2,1024]{1,0:T(2,128)} %param.17) | copy-start | bytes 24580
  169.8 12.2 %copy-start.5 = (f32[2,1024]{1,0:T(2,128)S(1)}, f32[2,1024]{1,0:T(2,128)}, u32[]{:S(2)}) copy-start(f32[2,1024]{1,0:T(2,128)} %param.18) | copy-start | bytes 24580
  169.8 49.9 %copy-start.2 = (bf16[512,1024]{1,0:T(8,128)(2,1)S(1)}, bf16[512,1024]{1,0:T(8,128)(2,1)}, u32[]{:S(2)}) copy-start(bf16[512,1024]{1,0:T(8,128)(2,1)} %param.13) | copy-start | bytes 3145732
  171.2 20.7 %all-to-all-start = ((s32[32,1,512]{2,1,0:T(1,128)}), s32[32,1,512]{2,1,0:T(1,128)S(1)}, u32[]{:S(2)}, u32[]{:S(2)}) async-start(s32[32,1,512]{2,1,0:T(1,128)} %reshape.219), calls=%async_computation | async-start | bytes 131072 | tf_op jit(solution)/shard_map/all_to_all | solution.py:140
  181.9 87.3 %all-gather.5.cloned.1.call-start = ((), (), s32[]{:S(2)}) async-start(), calls=%async_computation.9 | async-start | bytes 5242880 | tf_op jit(solution)/shard_map/all_gather | solution.py:149
  220.0 49.1 %copy-start.10 = (f32[1024]{0:T(1024)S(1)}, f32[1024]{0:T(1024)}, u32[]{:S(2)}) copy-start(f32[1024]{0:T(1024)} %param.20) | copy-start | bytes 12292
  222.2 122.6 %reduce-scatter.6.cloned.1.call-start = ((), (), s32[]{:S(2)}) async-start(), calls=%async_computation.10 | async-start | bytes 5242880 | tf_op jit(solution)/shard_map/reduce_scatter | solution.py:156
  297.7 47.1 %copy-start.1 = (bf16[512,1024]{1,0:T(8,128)(2,1)S(1)}, bf16[512,1024]{1,0:T(8,128)(2,1)}, u32[]{:S(2)}) copy-start(bf16[512,1024]{1,0:T(8,128)(2,1)} %add_convert_fusion.1) | copy-start | bytes 3145732
  297.7 70.0 %reduce-scatter.8.cloned.1.call-start = ((), (), s32[]{:S(2)}) async-start(), calls=%async_computation.11 | async-start | bytes 163840 | tf_op jit(solution)/shard_map/reduce_scatter | solution.py:168
  344.8 3.4 copy-start.3
  370.4 23.1 %all-to-all-start.2 = ((bf16[32,8,1024]{2,1,0:T(8,128)(2,1)}), bf16[32,8,1024]{2,1,0:T(8,128)(2,1)S(1)}, u32[]{:S(2)}, u32[]{:S(2)}) async-start(bf16[32,8,1024]{2,1,0:T(8,128)(2,1)} %broadcast_in_dim.33), calls=%async_computation.5 | async-start | bytes 1048576 | tf_op jit(solution)/shard_map/all_to_all | solution.py:174
Sparse Core Ops, SparseCore 0:
  9.0 70.5 all-gather.2
  169.9 48.2 reduce-scatter.3
  222.3 46.8 all-gather.4
  297.8 46.8 reduce-scatter.5
  349.7 18.0 reduce-scatter.7

commit v6 on v5

--- a/solution.py
+++ b/solution.py
@@ -32,7 +32,7 @@
         pp, pv_ref[0], preferred_element_type=jnp.float32)
     o_ref[0] = out.astype(jnp.bfloat16)
 
-def attention(query, keys, values, prompt_key, prompt_value, seg, tok_group, ends, starts, prompt_len, head_dim, interpret=False):
+def attention(query, keys, values, prompt_key, prompt_value, seg, tok_group, ends, starts, prompt_len, head_dim, parity=0, halves=1, interpret=False):
     tok, cols = query.shape
     heads = cols // head_dim
     block = 256
@@ -47,18 +47,20 @@
     segq = seg.reshape(tok, 1)
     grpq = tok_group.reshape(tok, 1)
     kgrp = (jnp.arange(prow, dtype=jnp.int32) // prompt_len).reshape(1, prow)
+    first = first[parity::halves]
+    segw = segw[parity::halves]
     grid_spec = pltpu.PrefetchScalarGridSpec(
         num_scalar_prefetch=1,
-        grid=(heads, nb),
+        grid=(heads, nb // halves),
         in_specs=[
-            pl.BlockSpec((1, block, head_dim), lambda h, b, fr: (h, b, 0)),
+            pl.BlockSpec((1, block, head_dim), lambda h, b, fr: (h, halves * b + parity, 0)),
             pl.BlockSpec((1, tok, head_dim), lambda h, b, fr: (h, 0, 0)),
             pl.BlockSpec((1, tok, head_dim), lambda h, b, fr: (h, 0, 0)),
             pl.BlockSpec((1, prow, head_dim), lambda h, b, fr: (h, 0, 0)),
             pl.BlockSpec((1, prow, head_dim), lambda h, b, fr: (h, 0, 0)),
-            pl.BlockSpec((block, 1), lambda h, b, fr: (b, 0)),
+            pl.BlockSpec((block, 1), lambda h, b, fr: (halves * b + parity, 0)),
             pl.BlockSpec((1, 1, window), lambda h, b, fr: (b, 0, 0)),
-            pl.BlockSpec((block, 1), lambda h, b, fr: (b, 0)),
+            pl.BlockSpec((block, 1), lambda h, b, fr: (halves * b + parity, 0)),
             pl.BlockSpec((1, prow), lambda h, b, fr: (0, 0)),
         ],
         out_specs=pl.BlockSpec((1, block, head_dim), lambda h, b, fr: (h, b, 0)),
@@ -66,10 +68,10 @@
     out = pl.pallas_call(
         functools.partial(attention_kernel, window=window),
         grid_spec=grid_spec,
-        out_shape=jax.ShapeDtypeStruct((heads, tok, head_dim), jnp.bfloat16),
+        out_shape=jax.ShapeDtypeStruct((heads, tok // halves, head_dim), jnp.bfloat16),
         interpret=interpret,
     )(first, by_head(query), by_head(keys), by_head(values), by_head(prompt_key), by_head(prompt_value), segq, segw, grpq, kgrp)
-    return out.transpose(1, 0, 2).reshape(tok, cols)
+    return out.transpose(1, 0, 2).reshape(tok // halves, cols)
 
 
 def layer_norm(values, gain, bias):
@@ -127,16 +129,21 @@
     seg = jnp.sum((position[:, None] >= ends[None, :]).astype(jnp.int32), axis=1)
     tok_group = jnp.sum(jnp.where(seg[:, None] == text_ids[None, :], groups[None, :], 0), axis=1)
     starts = ends - lens
-    context = attention(
-        query, keys, values, prompt_key, prompt_value, seg, tok_group, ends, starts, prompt_len, HEAD_DIM
-    )
     my_start = lax.axis_index("tensor") * shard_rows
-    attn_part = lax.psum_scatter(
-        jnp.dot(context, w_out, preferred_element_type=jnp.float32).astype(jnp.bfloat16),
-        "tensor",
-        scatter_dimension=0,
-        tiled=True,
-    ).astype(jnp.float32)
+
+    def attend_half(parity):
+        context = attention(
+            query, keys, values, prompt_key, prompt_value, seg, tok_group, ends, starts, prompt_len,
+            HEAD_DIM, parity=parity, halves=2,
+        )
+        return lax.psum_scatter(
+            jnp.dot(context, w_out, preferred_element_type=jnp.float32).astype(jnp.bfloat16),
+            "tensor",
+            scatter_dimension=0,
+            tiled=True,
+        ).astype(jnp.float32)
+
+    attn_part = jnp.concatenate([attend_half(0), attend_half(1)], axis=0)
     asked_rows = lax.all_to_all(
         jnp.broadcast_to(candidates[None], (n_dp,) + candidates.shape), "dp", 0, 0, tiled=True
     ).reshape(-1, candidates.shape[1])
@@ -144,21 +151,28 @@
     normed_rows = layer_norm(
         tokens.astype(jnp.float32) + attn_part, norm_gain[0], norm_bias[0]
     ).astype(jnp.bfloat16)
-    expanded = jax.nn.gelu(
-        jnp.dot(
-            lax.all_gather(normed_rows, "tensor", axis=0, tiled=True),
-            w_in,
-            preferred_element_type=jnp.float32,
-        )
-        + b_in,
-        approximate=False,
-    ).astype(jnp.bfloat16)
-    reduced = lax.psum_scatter(
-        jnp.dot(expanded, w_down, preferred_element_type=jnp.float32).astype(jnp.bfloat16),
-        "tensor",
-        scatter_dimension=0,
-        tiled=True,
-    ).astype(jnp.float32)
+    half_rows = shard_rows // 2
+
+    def feed_half(rows):
+        expanded = jax.nn.gelu(
+            jnp.dot(
+                lax.all_gather(rows, "tensor", axis=0, tiled=True),
+                w_in,
+                preferred_element_type=jnp.float32,
+            )
+            + b_in,
+            approximate=False,
+        ).astype(jnp.bfloat16)
+        return lax.psum_scatter(
+            jnp.dot(expanded, w_down, preferred_element_type=jnp.float32).astype(jnp.bfloat16),
+            "tensor",
+            scatter_dimension=0,
+            tiled=True,
+        ).astype(jnp.float32)
+
+    reduced = jnp.concatenate(
+        [feed_half(normed_rows[:half_rows]), feed_half(normed_rows[half_rows:])], axis=0
+    )
     output = layer_norm(
         normed_rows.astype(jnp.float32) + reduced, norm_gain[1], norm_bias[1]
     ).astype(jnp.bfloat16)

time: 442 us -> 435 us (0.984)
  waiting for transfers between devices: 203 us -> 185 us
    reduce_scatter x2 -> x4, waiting for transfers between devices: 71.6 us -> 56 us  [the longest x2 47.6 us: feed_half(): lax.psum_scatter(jnp.dot(expanded, w_down, preferred_element_type=jnp.flo...]
    pallas_call x1 -> x2, Pallas kernels: 67.8 us -> 71.6 us  [attention(): pl.pallas_call(functools.partial(attention_kernel, window=window), grid_s...]
    dot_general x2 -> x4, matrix products: 32.8 us -> 36.5 us  [the longest x2 31.1 us: feed_half(): jnp.dot(expanded, w_down, preferred_element_type=jnp.float32)]
    all_gather x1 -> x2, waiting for transfers between devices: 47 us -> 45 us  [feed_half(): lax.all_gather(rows, 'tensor', axis=0, tiled=True)]
  transfers between devices with their start and end apart: 8 -> 11, of which waited for: 8 -> 10; matrix products, arithmetic and copies ran while one was open for 5% -> 14% of each run, Pallas kernels for 0% -> 8%
where the time goes in v6:
time: 435 us; the launch traced here: 434 us
  waiting for transfers between devices  185 us (43%)
  Pallas kernels  71.6 us (16%)
  matrix products  54.8 us (13%)
  other arithmetic  33.5 us (8%)
  starting transfers between devices  31.6 us (7%)
  local copies, waits for them, and re-layouts  30.1 us (7%)
  between operations  13.9 us (3%)
  blocking collectives  13.8 us (3%)
    pallas_call x2, Pallas kernels, attention(): pl.pallas_call(functools.partial(attention_kernel, window=window), grid_s...  71.6 us
    reduce_scatter x2, waiting for transfers between devices, feed_half(): lax.psum_scatter(jnp.dot(expanded, w_down, preferred_element_type=jnp.flo...  47.6 us
    all_gather x2, waiting for transfers between devices, feed_half(): lax.all_gather(rows, 'tensor', axis=0, tiled=True)  45 us
    dot_general x2, matrix products, feed_half(): jnp.dot(expanded, w_down, preferred_element_type=jnp.float32)  31.1 us
    all_to_all x1, waiting for transfers between devices, shards(): lax.all_to_all(jnp.broadcast_to(own_kv[None], (n_dp,) + own_kv.shape), 'd...  23.3 us
    reduce_sum x1, other arithmetic, shards(): jnp.sum(jnp.where(local_rows[:, :, None] == row_ids[None, None, :], table...  21.8 us
    reduce_scatter x1, waiting for transfers between devices, shards(): lax.psum_scatter(partial_sums, 'tensor', scatter_dimension=0, tiled=True)  18.1 us
    all_gather x1, waiting for transfers between devices, shards(): whole = lax.all_gather(tokens, 'tensor', axis=0, tiled=True)  17.9 us
  transfers between devices with their start and end apart: 11, of which 10 were waited for; matrix products, arithmetic and copies ran while one was open for 14% of the time, Pallas kernels for 8%

profile of v6, /device:TPU:0, one launch (start us, length us, event | category | flops | bytes accessed | tf_op | source)
XLA Modules:
  0.0 434.4 jit_solution(15425638896170588336)
XLA Ops:
  11.5 10.9 %all-to-all-start.1 = ((bf16[32,64,512]{2,1,0:T(8,128)(2,1)}), bf16[32,64,512]{2,1,0:T(8,128)(2,1)}, u32[]{:S(2)}, u32[]{:S(2)}) async-start(bf16[32,64,512]{2,1,0:T(8,128)(2,1)} %broadcast_in_dim.30), calls=%async_computation.1 | async-start | bytes 4194304 | tf_op jit(solution)/shard_map/all_to_all | solution.py:117
  28.8 23.3 %all-to-all-done.1 = bf16[32,64,512]{2,1,0:T(8,128)(2,1)} async-done(((bf16[32,64,512]{2,1,0:T(8,128)(2,1)}), bf16[32,64,512]{2,1,0:T(8,128)(2,1)}, u32[]{:S(2)}, u32[]{:S(2)}) %all-to-all-start.1) | async-done | bytes 2097184 | tf_op jit(solution)/shard_map/all_to_all | solution.py:117
  52.0 3.0 fusion.114
  56.6 1.8 copy.49
  59.9 1.8 copy.47
  61.7 17.9 %all-gather.4.cloned.1.call-done = bf16[2048,1024]{1,0:T(8,128)(2,1)} async-done(((bf16[512,1024]{1,0:T(8,128)(2,1)}), bf16[2048,1024]{1,0:T(8,128)(2,1)}) %all-gather.4.cloned.1.call-update) | async-done | bytes 4194320 | tf_op jit(solution)/shard_map/all_gather | solution.py:108
  79.6 3.6 convolution_convert_fusion
  83.2 1.8 copy.45
  85.0 3.6 convolution_convert_fusion.1
  88.6 1.8 copy.44
  90.4 3.6 fusion.20
  94.0 1.8 copy.43
  95.7 35.9 %shard_map.128 = bf16[4,1024,64]{2,1,0:T(8,128)(2,1)} custom-call(s32[4]{0:T(128)} %slice.59.first_ref, bf16[4,2048,64]{2,1,0:T(8,128)(2,1)} %bitcast.71, bf16[4,2048,64]{2,1,0:T(8,128)(2,1)} %bitcast.69, bf16[4,2048,64]{2,1,0:T(8,128)(2,1)} %bitcast.67, bf16[4,2048,64]{2,1,0:T(8,128)(2,1)} %bitcast.65, bf16[4,2048,64]{2,1,0:T(8,128)(2,1)} %bitcast.63, ...), custom_call_target="tpu_custom_call" | custom-call | tf_op jit(solution)/shard_map/pallas_call | solution.py:68
  133.2 2.1 convolution_convert_fusion.2
  136.1 35.7 %shard_map.127 = bf16[4,1024,64]{2,1,0:T(8,128)(2,1)} custom-call(s32[4]{0:T(128)} %slice.52.first_ref, bf16[4,2048,64]{2,1,0:T(8,128)(2,1)} %bitcast.72, bf16[4,2048,64]{2,1,0:T(8,128)(2,1)} %bitcast.70, bf16[4,2048,64]{2,1,0:T(8,128)(2,1)} %bitcast.68, bf16[4,2048,64]{2,1,0:T(8,128)(2,1)} %bitcast.66, bf16[4,2048,64]{2,1,0:T(8,128)(2,1)} %bitcast.64, ...), custom_call_target="tpu_custom_call" | custom-call | tf_op jit(solution)/shard_map/pallas_call | solution.py:68
  171.9 2.4 copy.52
  174.2 3.3 convolution_convert_fusion.3
  178.3 10.7 %all-to-all-start = ((s32[32,1,512]{2,1,0:T(1,128)}), s32[32,1,512]{2,1,0:T(1,128)S(1)}, u32[]{:S(2)}, u32[]{:S(2)}) async-start(s32[32,1,512]{2,1,0:T(1,128)} %reshape.232), calls=%async_computation | async-start | bytes 131072 | tf_op jit(solution)/shard_map/all_to_all | solution.py:147
  189.1 9.9 %all-to-all-done = s32[32,1,512]{2,1,0:T(1,128)S(1)} async-done(((s32[32,1,512]{2,1,0:T(1,128)}), s32[32,1,512]{2,1,0:T(1,128)S(1)}, u32[]{:S(2)}, u32[]{:S(2)}) %all-to-all-start) | async-done | bytes 65568 | tf_op jit(solution)/shard_map/all_to_all | solution.py:147
  200.5 8.5 %reduce-scatter.6.cloned.1.call-done = bf16[256,1024]{1,0:T(8,128)(2,1)} async-done(((bf16[1024,1024]{1,0:T(8,128)(2,1)}), bf16[256,1024]{1,0:T(8,128)(2,1)}) %reduce-scatter.6.cloned.1.call-update) | async-done | bytes 524304 | tf_op jit(solution)/shard_map/reduce_scatter | solution.py:139
  213.5 29.2 %all-gather.6.cloned.1.call-done = bf16[1024,1024]{1,0:T(8,128)(2,1)} async-done(((bf16[256,1024]{1,0:T(8,128)(2,1)}), bf16[1024,1024]{1,0:T(8,128)(2,1)}) %all-gather.6.cloned.1.call-update) | async-done | bytes 2097168 | tf_op jit(solution)/shard_map/all_gather | solution.py:159
  242.8 15.5 %fusion.31 = bf16[1024,1024]{1,0:T(8,128)(2,1)} fusion(bf16[1024,1024]{1,0:T(8,128)(2,1)S(1)} %copy-done, f32[1024]{0:T(1024)S(1)} %copy-done.11, bf16[1024,1024]{1,0:T(8,128)(2,1)} %all-gather.6.cloned.1.call-done, bf16[1024,1024]{1,0:T(8,128)(2,1)} %param.19), kind=kOutput, calls=%fused_computation.60 | convolution fusion | flops 4365221888 | bytes 8392704 | tf_op jit(solution)/shard_map/dot_general | solution.py:167
  258.6 15.7 %all-gather.8.cloned.1.call-done = bf16[1024,1024]{1,0:T(8,128)(2,1)} async-done(((bf16[256,1024]{1,0:T(8,128)(2,1)}), bf16[1024,1024]{1,0:T(8,128)(2,1)}) %all-gather.8.cloned.1.call-update) | async-done | bytes 2097168 | tf_op jit(solution)/shard_map/all_gather | solution.py:159
  274.3 15.6 %fusion.34 = bf16[1024,1024]{1,0:T(8,128)(2,1)} fusion(bf16[1024,1024]{1,0:T(8,128)(2,1)S(1)} %copy-done, f32[1024]{0:T(1024)S(1)} %copy-done.11, bf16[1024,1024]{1,0:T(8,128)(2,1)} %all-gather.8.cloned.1.call-done, bf16[1024,1024]{1,0:T(8,128)(2,1)} %param.19), kind=kOutput, calls=%fused_computation.61 | convolution fusion | flops 4365221888 | bytes 8392704 | tf_op jit(solution)/shard_map/dot_general | solution.py:167
  290.1 16.0 %reduce-scatter.10.cloned.1.call-done = bf16[256,1024]{1,0:T(8,128)(2,1)} async-done(((bf16[1024,1024]{1,0:T(8,128)(2,1)}), bf16[256,1024]{1,0:T(8,128)(2,1)}) %reduce-scatter.10.cloned.1.call-update) | async-done | bytes 524304 | tf_op jit(solution)/shard_map/reduce_scatter | solution.py:166
  306.0 31.6 %reduce-scatter.12.cloned.1.call-done = bf16[256,1024]{1,0:T(8,128)(2,1)} async-done(((bf16[1024,1024]{1,0:T(8,128)(2,1)}), bf16[256,1024]{1,0:T(8,128)(2,1)}) %reduce-scatter.12.cloned.1.call-update) | async-done | bytes 524304 | tf_op jit(solution)/shard_map/reduce_scatter | solution.py:166
  342.5 18.1 %reduce-scatter.14.cloned.1.call-done = f32[8,1024]{1,0:T(8,128)} async-done(((f32[32,1024]{1,0:T(8,128)}), f32[8,1024]{1,0:T(8,128)}) %reduce-scatter.14.cloned.1.call-update) | async-done | bytes 32784 | tf_op jit(solution)/shard_map/reduce_scatter | solution.py:182
  363.2 9.4 %all-to-all-start.2 = ((bf16[32,8,1024]{2,1,0:T(8,128)(2,1)}), bf16[32,8,1024]{2,1,0:T(8,128)(2,1)S(1)}, u32[]{:S(2)}, u32[]{:S(2)}) async-start(bf16[32,8,1024]{2,1,0:T(8,128)(2,1)} %broadcast_in_dim.33), calls=%async_computation.7 | async-start | bytes 1048576 | tf_op jit(solution)/shard_map/all_to_all | solution.py:188
  372.6 13.6 %all-to-all-done.2 = bf16[32,8,1024]{2,1,0:T(8,128)(2,1)S(1)} async-done(((bf16[32,8,1024]{2,1,0:T(8,128)(2,1)}), bf16[32,8,1024]{2,1,0:T(8,128)(2,1)S(1)}, u32[]{:S(2)}, u32[]{:S(2)}) %all-to-all-start.2) | async-done | bytes 524320 | tf_op jit(solution)/shard_map/all_to_all | solution.py:188
  386.3 3.5 convolution_multiply_fusion
  389.8 21.8 %select_reduce_fusion = f32[256,64]{1,0:T(8,128)S(1)} fusion(f32[256,2048]{1,0:T(8,128)S(1)} %convolution_multiply_fusion, s32[256,64]{1,0:T(8,128)S(1)} %broadcast_subtract_fusion), kind=kLoop, calls=%fused_computation.1 | loop fusion | flops 100646912 | bytes 2228224 | tf_op jit(solution)/shard_map/reduce_sum | solution.py:195
  411.7 13.8 %all_to_all.24 = f32[32,1,512]{2,1,0:T(1,128)S(1)} all-to-all(f32[32,1,512]{2,1,0:T(1,128)S(1)} %reshape.234), channel_id=1, replica_groups=mesh['dp'=32,'tensor'=4] {'dp'}, dimensions={0} | all-to-all | bytes 131072 | tf_op jit(solution)/shard_map/all_to_all | solution.py:199
  (99 shorter events, 33.4 us)
Async XLA Ops:
  6.5 236.2 %copy-start = (bf16[1024,1024]{1,0:T(8,128)(2,1)S(1)}, bf16[1024,1024]{1,0:T(8,128)(2,1)}, u32[]{:S(2)}) copy-start(bf16[1024,1024]{1,0:T(8,128)(2,1)} %param.21) | copy-start | bytes 6291460
  6.5 73.0 %all-gather.4.cloned.1.call-start = ((), (), s32[]{:S(2)}) async-start(), calls=%async_computation.9 | async-start | bytes 5242880 | tf_op jit(solution)/shard_map/all_gather | solution.py:108
  7.3 15.2 %copy-start.10 = (s32[1,32]{1,0:T(1,128)S(1)}, s32[1,32]{1,0:T(1,128)}, u32[]{:S(2)}) copy-start(s32[1,32]{1,0:T(1,128)} %param.23) | copy-start | bytes 388
  8.6 16.1 %copy-start.9 = (s32[32]{0:T(128)S(1)}, s32[32]{0:T(128)}, u32[]{:S(2)}) copy-start(s32[32]{0:T(128)} %param.24) | copy-start | bytes 388
  11.5 40.5 %all-to-all-start.1 = ((bf16[32,64,512]{2,1,0:T(8,128)(2,1)}), bf16[32,64,512]{2,1,0:T(8,128)(2,1)}, u32[]{:S(2)}, u32[]{:S(2)}) async-start(bf16[32,64,512]{2,1,0:T(8,128)(2,1)} %broadcast_in_dim.30), calls=%async_computation.1 | async-start | bytes 4194304 | tf_op jit(solution)/shard_map/all_to_all | solution.py:117
  22.4 178.0 %reduce-scatter.8.cloned.1.call-start = ((), (), s32[]{:S(2)}) async-start(), calls=%async_computation.11 | async-start | bytes 2621440 | tf_op jit(solution)/shard_map/reduce_scatter | solution.py:139
  95.7 37.4 %copy-start.5 = (bf16[256,1024]{1,0:T(8,128)(2,1)S(1)}, bf16[256,1024]{1,0:T(8,128)(2,1)}, u32[]{:S(2)}) copy-start(bf16[256,1024]{1,0:T(8,128)(2,1)} %param.16) | copy-start | bytes 1572868
  135.3 73.6 %reduce-scatter.6.cloned.1.call-start = ((), (), s32[]{:S(2)}) async-start(), calls=%async_computation.10 | async-start | bytes 2621440 | tf_op jit(solution)/shard_map/reduce_scatter | solution.py:139
  171.8 5.7 %copy-start.8 = (s32[8,64]{1,0:T(8,128)S(1)}, s32[8,64]{1,0:T(8,128)}, u32[]{:S(2)}) copy-start(s32[8,64]{1,0:T(8,128)} %param.25) | copy-start | bytes 6148
  171.8 17.3 %copy-start.6 = (f32[2,1024]{1,0:T(2,128)S(1)}, f32[2,1024]{1,0:T(2,128)}, u32[]{:S(2)}) copy-start(f32[2,1024]{1,0:T(2,128)} %param.17) | copy-start | bytes 24580
  171.8 17.3 %copy-start.7 = (f32[2,1024]{1,0:T(2,128)S(1)}, f32[2,1024]{1,0:T(2,128)}, u32[]{:S(2)}) copy-start(f32[2,1024]{1,0:T(2,128)} %param.18) | copy-start | bytes 24580
  174.2 36.2 %copy-start.1 = (bf16[512,1024]{1,0:T(8,128)(2,1)S(1)}, bf16[512,1024]{1,0:T(8,128)(2,1)}, u32[]{:S(2)}) copy-start(bf16[512,1024]{1,0:T(8,128)(2,1)} %param.13) | copy-start | bytes 3145732
  178.3 20.7 %all-to-all-start = ((s32[32,1,512]{2,1,0:T(1,128)}), s32[32,1,512]{2,1,0:T(1,128)S(1)}, u32[]{:S(2)}, u32[]{:S(2)}) async-start(s32[32,1,512]{2,1,0:T(1,128)} %reshape.232), calls=%async_computation | async-start | bytes 131072 | tf_op jit(solution)/shard_map/all_to_all | solution.py:147
  189.0 53.7 %all-gather.6.cloned.1.call-start = ((), (), s32[]{:S(2)}) async-start(), calls=%async_computation.12 | async-start | bytes 2621440 | tf_op jit(solution)/shard_map/all_gather | solution.py:159
  208.9 2.4 copy-start.2
  211.3 31.5 %copy-start.11 = (f32[1024]{0:T(1024)S(1)}, f32[1024]{0:T(1024)}, u32[]{:S(2)}) copy-start(f32[1024]{0:T(1024)} %param.20) | copy-start | bytes 12292
  212.9 61.4 %all-gather.8.cloned.1.call-start = ((), (), s32[]{:S(2)}) async-start(), calls=%async_computation.14 | async-start | bytes 2621440 | tf_op jit(solution)/shard_map/all_gather | solution.py:159
  213.5 92.6 %reduce-scatter.10.cloned.1.call-start = ((), (), s32[]{:S(2)}) async-start(), calls=%async_computation.13 | async-start | bytes 2621440 | tf_op jit(solution)/shard_map/reduce_scatter | solution.py:166
  258.3 79.3 %reduce-scatter.12.cloned.1.call-start = ((), (), s32[]{:S(2)}) async-start(), calls=%async_computation.15 | async-start | bytes 2621440 | tf_op jit(solution)/shard_map/reduce_scatter | solution.py:166
  289.9 70.6 %reduce-scatter.14.cloned.1.call-start = ((), (), s32[]{:S(2)}) async-start(), calls=%async_computation.16 | async-start | bytes 163840 | tf_op jit(solution)/shard_map/reduce_scatter | solution.py:182
  337.6 3.4 copy-start.3
  337.6 3.4 copy-start.4
  363.2 23.1 %all-to-all-start.2 = ((bf16[32,8,1024]{2,1,0:T(8,128)(2,1)}), bf16[32,8,1024]{2,1,0:T(8,128)(2,1)S(1)}, u32[]{:S(2)}, u32[]{:S(2)}) async-start(bf16[32,8,1024]{2,1,0:T(8,128)(2,1)} %broadcast_in_dim.33), calls=%async_computation.7 | async-start | bytes 1048576 | tf_op jit(solution)/shard_map/all_to_all | solution.py:188
Sparse Core Ops, SparseCore 0:
  9.0 70.5 all-gather.3
  135.4 30.4 reduce-scatter.7
  177.7 31.1 reduce-scatter.5
  213.0 29.7 all-gather.5
  244.3 30.0 all-gather.7
  276.6 29.3 reduce-scatter.9
  308.4 29.1 reduce-scatter.11
  342.5 18.0 reduce-scatter.13

commit v7 on v6

--- a/solution.py
+++ b/solution.py
@@ -73,6 +73,45 @@
     )(first, by_head(query), by_head(keys), by_head(values), by_head(prompt_key), by_head(prompt_value), segq, segw, grpq, kgrp)
     return out.transpose(1, 0, 2).reshape(tok // halves, cols)
 
+CROSS = [(0, 2), (2, 0), (1, 3), (3, 1)]
+ONCHIP = [(0, 1), (1, 0), (2, 3), (3, 2)]
+
+
+def gather_tensor(x):
+    t = lax.axis_index("tensor")
+    upper = t // 2
+    core = t % 2
+    y = lax.ppermute(x, "tensor", CROSS)
+    low = jnp.where(upper == 0, x, y)
+    high = jnp.where(upper == 0, y, x)
+    pair = jnp.stack([low, high])
+    other = lax.ppermute(pair, "tensor", ONCHIP)
+    first = core == 0
+    return jnp.concatenate(
+        [
+            jnp.where(first, pair[0], other[0]),
+            jnp.where(first, other[0], pair[0]),
+            jnp.where(first, pair[1], other[1]),
+            jnp.where(first, other[1], pair[1]),
+        ],
+        axis=0,
+    )
+
+
+def scatter_tensor(part, link_dtype):
+    t = lax.axis_index("tensor")
+    upper = t // 2
+    core = t % 2
+    n = part.shape[0] // 4
+    blocks = part.reshape((2, 2, n) + part.shape[1:])
+    mine = lax.dynamic_index_in_dim(blocks, core, axis=1, keepdims=False)
+    theirs = lax.dynamic_index_in_dim(blocks, 1 - core, axis=1, keepdims=False)
+    got = lax.ppermute(theirs.astype(link_dtype), "tensor", ONCHIP)
+    chip_sum = mine.astype(jnp.float32) + got.astype(jnp.float32)
+    keep = lax.dynamic_index_in_dim(chip_sum, upper, axis=0, keepdims=False)
+    send = lax.dynamic_index_in_dim(chip_sum, 1 - upper, axis=0, keepdims=False)
+    return keep + lax.ppermute(send.astype(link_dtype), "tensor", CROSS).astype(jnp.float32)
+
 
 def layer_norm(values, gain, bias):
     mean = jnp.mean(values, axis=-1, keepdims=True)
@@ -105,7 +144,7 @@
     columns = w_attn.shape[2]
     heads_here = columns // HEAD_DIM
     scale = HEAD_DIM ** (-0.5)
-    whole = lax.all_gather(tokens, "tensor", axis=0, tiled=True)
+    whole = gather_tensor(tokens)
     query = (jnp.dot(whole, w_attn[0], preferred_element_type=jnp.float32) * scale).astype(
         jnp.bfloat16
     )
@@ -136,12 +175,7 @@
             query, keys, values, prompt_key, prompt_value, seg, tok_group, ends, starts, prompt_len,
             HEAD_DIM, parity=parity, halves=2,
         )
-        return lax.psum_scatter(
-            jnp.dot(context, w_out, preferred_element_type=jnp.float32).astype(jnp.bfloat16),
-            "tensor",
-            scatter_dimension=0,
-            tiled=True,
-        ).astype(jnp.float32)
+        return scatter_tensor(jnp.dot(context, w_out, preferred_element_type=jnp.float32), jnp.bfloat16)
 
     attn_part = jnp.concatenate([attend_half(0), attend_half(1)], axis=0)
     asked_rows = lax.all_to_all(
@@ -156,19 +190,14 @@
     def feed_half(rows):
         expanded = jax.nn.gelu(
             jnp.dot(
-                lax.all_gather(rows, "tensor", axis=0, tiled=True),
+                gather_tensor(rows),
                 w_in,
                 preferred_element_type=jnp.float32,
             )
             + b_in,
             approximate=False,
         ).astype(jnp.bfloat16)
-        return lax.psum_scatter(
-            jnp.dot(expanded, w_down, preferred_element_type=jnp.float32).astype(jnp.bfloat16),
-            "tensor",
-            scatter_dimension=0,
-            tiled=True,
-        ).astype(jnp.float32)
+        return scatter_tensor(jnp.dot(expanded, w_down, preferred_element_type=jnp.float32), jnp.bfloat16)
 
     reduced = jnp.concatenate(
         [feed_half(normed_rows[:half_rows]), feed_half(normed_rows[half_rows:])], axis=0

time: 435 us -> 449 us (1.032)
  waiting for transfers between devices: 185 us -> 123 us
  local copies, waits for them, and re-layouts: 30.1 us -> 62.8 us
  other arithmetic: 33.5 us -> 53.6 us
  matrix products: 54.8 us -> 65.1 us
  starting transfers between devices: 31.6 us -> 40.5 us
    ppermute x0 -> x14, waiting for transfers between devices: none -> 90.7 us  [the longest x3 54.9 us: gather_tensor(): y = lax.ppermute(x, 'tensor', CROSS)]
    all_gather x3 -> x0, waiting for transfers between devices: 62.9 us -> none  [the longest x2 45 us: feed_half(): lax.all_gather(rows, 'tensor', axis=0, tiled=True)]
    reduce_scatter x4 -> x0, waiting for transfers between devices: 56 us -> none  [the longest x2 47.6 us: feed_half(): lax.psum_scatter(jnp.dot(expanded, w_down, preferred_element_type=jnp.flo...]
    all_to_all x1, waiting for transfers between devices: 23.3 us -> 0.01 us  [shards(): lax.all_to_all(jnp.broadcast_to(own_kv[None], (n_dp,) + own_kv.shape), 'd...]
    add x0 -> x8, other arithmetic: none -> 12.8 us  [the longest x4 6.72 us: scatter_tensor(): chip_sum = mine.astype(jnp.float32) + got.astype(jnp.float32)]
    dot_general x0 -> x4, local copies, waits for them, and re-layouts: none -> 11.5 us  [attend_half(): jnp.dot(context, w_out, preferred_element_type=jnp.float32)]
    convert_element_type x0 -> x8, local copies, waits for them, and re-layouts: none -> 10.6 us  [the longest x4 6.99 us: scatter_tensor(): got = lax.ppermute(theirs.astype(link_dtype), 'tensor', ONCHIP)]
    ppermute x0 -> x14, starting transfers between devices: none -> 9.89 us  [the longest x4 4.24 us: scatter_tensor(): lax.ppermute(send.astype(link_dtype), 'tensor', CROSS).astype(jnp.float32)]
  transfers between devices with their start and end apart: 11 -> 18, of which waited for: 10 -> 10; matrix products, arithmetic and copies ran while one was open for 14% -> 20% of each run, Pallas kernels for 8% -> 0%
where the time goes in v7:
time: 449 us; the launch traced here: 445 us
  waiting for transfers between devices  123 us (27%)
  Pallas kernels  71.4 us (16%)
  matrix products  65.1 us (14%)
  local copies, waits for them, and re-layouts  62.8 us (14%)
  other arithmetic  53.6 us (12%)
  starting transfers between devices  40.5 us (9%)
  between operations  14.4 us (3%)
  blocking collectives  13.8 us (3%)
    pallas_call x2, Pallas kernels, attention(): pl.pallas_call(functools.partial(attention_kernel, window=window), grid_s...  71.4 us
    ppermute x3, waiting for transfers between devices, gather_tensor(): y = lax.ppermute(x, 'tensor', CROSS)  54.9 us
    ppermute x4, waiting for transfers between devices, scatter_tensor(): lax.ppermute(send.astype(link_dtype), 'tensor', CROSS).astype(jnp.float32)  35.8 us
    dot_general x2, matrix products, feed_half(): jnp.dot(expanded, w_down, preferred_element_type=jnp.float32)  32.8 us
    reduce_sum x1, other arithmetic, shards(): jnp.sum(jnp.where(local_rows[:, :, None] == row_ids[None, None, :], table...  21.8 us
    reduce_scatter x1, waiting for transfers between devices, shards(): lax.psum_scatter(partial_sums, 'tensor', scatter_dimension=0, tiled=True)  17.8 us
    dot_general x4, matrix products, project(): jnp.dot(block, weight, preferred_element_type=jnp.float32)  17.4 us
    reshape x5, local copies, waits for them, and re-layouts, by_head(): return x.reshape(x.shape[0], heads, head_dim).transpose(1, 0, 2)  13.9 us
  transfers between devices with their start and end apart: 18, of which 10 were waited for; matrix products, arithmetic and copies ran while one was open for 20% of the time, Pallas kernels for 0%

profile of v7, /device:TPU:0, one launch (start us, length us, event | category | flops | bytes accessed | tf_op | source)
XLA Modules:
  0.0 445.1 jit_solution(11105871510469792032)
XLA Ops:
  12.8 10.5 %all-to-all-start.1 = ((bf16[32,64,512]{2,1,0:T(8,128)(2,1)}), bf16[32,64,512]{2,1,0:T(8,128)(2,1)}, u32[]{:S(2)}, u32[]{:S(2)}) async-start(bf16[32,64,512]{2,1,0:T(8,128)(2,1)} %broadcast_in_dim.30), calls=%async_computation.1 | async-start | bytes 4194304 | tf_op jit(solution)/shard_map/all_to_all | solution.py:156
  24.5 29.4 %collective-permute-done = bf16[512,1024]{1,0:T(8,128)(2,1)} collective-permute-done((bf16[512,1024]{1,0:T(8,128)(2,1)}, bf16[512,1024]{1,0:T(8,128)(2,1)}, u32[]{:S(2)}, u32[]{:S(2)}) %collective-permute-start) | collective-permute-done | bytes 1048608 | tf_op jit(solution)/shard_map/ppermute | solution.py:84
  63.6 3.0 fusion.145
  66.6 2.8 copy.59
  69.4 2.7 copy.60
  79.9 7.3 %convolution_convert_fusion.1 = bf16[2048,256]{0,1:T(8,128)(2,1)} fusion(bf16[3,1024,256]{2,1,0:T(8,128)(2,1)S(1)} %copy-done.22, bf16[512,1024]{1,0:T(8,128)(2,1)S(1)} %get-tuple-element.15, bf16[512,1024]{1,0:T(8,128)(2,1)S(1)} %get-tuple-element.16, bf16[512,1024]{1,0:T(8,128)(2,1)S(1)} %get-tuple-element.10, bf16[512,1024]{1,0:T(8,128)(2,1)S(1)} %get-tuple-element.9), kind=kOutput, calls=%fused_computation.46 | convolution fusion | flops 1091043328 | bytes 5767168 | tf_op jit(solution)/shard_map/dot_general | solution.py:124
  87.3 7.4 %convolution_convert_fusion = bf16[2048,256]{0,1:T(8,128)(2,1)} fusion(bf16[3,1024,256]{2,1,0:T(8,128)(2,1)S(1)} %copy-done.22, bf16[512,1024]{1,0:T(8,128)(2,1)S(1)} %get-tuple-element.15, bf16[512,1024]{1,0:T(8,128)(2,1)S(1)} %get-tuple-element.16, bf16[512,1024]{1,0:T(8,128)(2,1)S(1)} %get-tuple-element.10, bf16[512,1024]{1,0:T(8,128)(2,1)S(1)} %get-tuple-element.9), kind=kOutput, calls=%fused_computation.45 | convolution fusion | flops 1091043328 | bytes 5767168 | tf_op jit(solution)/shard_map/dot_general | solution.py:124
  94.6 7.4 %fusion.20 = bf16[2048,256]{0,1:T(8,128)(2,1)} fusion(bf16[3,1024,256]{2,1,0:T(8,128)(2,1)S(1)} %copy-done.22, bf16[512,1024]{1,0:T(8,128)(2,1)S(1)} %get-tuple-element.15, bf16[512,1024]{1,0:T(8,128)(2,1)S(1)} %get-tuple-element.16, bf16[512,1024]{1,0:T(8,128)(2,1)S(1)} %get-tuple-element.10, bf16[512,1024]{1,0:T(8,128)(2,1)S(1)} %get-tuple-element.9), kind=kOutput, calls=%fused_computation.44 | convolution fusion | flops 1091567616 | bytes 5767168 | tf_op jit(solution)/shard_map/dot_general | solution.py:148
  104.8 2.8 copy.56
  107.5 2.9 copy.54
  110.5 35.7 %shard_map.127 = bf16[4,1024,64]{2,1,0:T(8,128)(2,1)} custom-call(s32[4]{0:T(128)} %slice.76.first_ref, bf16[4,2048,64]{2,1,0:T(8,128)(2,1)} %bitcast.157, bf16[4,2048,64]{2,1,0:T(8,128)(2,1)} %bitcast.153, bf16[4,2048,64]{2,1,0:T(8,128)(2,1)} %bitcast.155, bf16[4,2048,64]{2,1,0:T(8,128)(2,1)} %bitcast.151, bf16[4,2048,64]{2,1,0:T(8,128)(2,1)} %bitcast.149, ...), custom_call_target="tpu_custom_call" | custom-call | tf_op jit(solution)/shard_map/pallas_call | solution.py:68
  146.2 3.0 copy.73
  149.2 2.7 reshape.248
  151.9 35.7 %shard_map.128 = bf16[4,1024,64]{2,1,0:T(8,128)(2,1)} custom-call(s32[4]{0:T(128)} %slice.85.first_ref, bf16[4,2048,64]{2,1,0:T(8,128)(2,1)} %bitcast.158, bf16[4,2048,64]{2,1,0:T(8,128)(2,1)} %bitcast.154, bf16[4,2048,64]{2,1,0:T(8,128)(2,1)} %bitcast.156, bf16[4,2048,64]{2,1,0:T(8,128)(2,1)} %bitcast.152, bf16[4,2048,64]{2,1,0:T(8,128)(2,1)} %bitcast.150, ...), custom_call_target="tpu_custom_call" | custom-call | tf_op jit(solution)/shard_map/pallas_call | solution.py:68
  187.6 3.0 copy.74
  190.7 2.8 reshape.249
  202.8 10.4 %all-to-all-start = ((s32[32,1,512]{2,1,0:T(1,128)}), s32[32,1,512]{2,1,0:T(1,128)S(1)}, u32[]{:S(2)}, u32[]{:S(2)}) async-start(s32[32,1,512]{2,1,0:T(1,128)} %reshape.251), calls=%async_computation | async-start | bytes 131072 | tf_op jit(solution)/shard_map/all_to_all | solution.py:181
  224.6 7.2 %collective-permute-done.5 = bf16[256,1024]{1,0:T(8,128)(2,1)} collective-permute-done((bf16[256,1024]{1,0:T(8,128)(2,1)}, bf16[256,1024]{1,0:T(8,128)(2,1)}, u32[]{:S(2)}, u32[]{:S(2)}) %collective-permute-start.5) | collective-permute-done | bytes 524320 | tf_op jit(solution)/shard_map/ppermute | solution.py:113
  233.3 9.0 %collective-permute-done.3 = bf16[256,1024]{1,0:T(8,128)(2,1)} collective-permute-done((bf16[256,1024]{1,0:T(8,128)(2,1)}, bf16[256,1024]{1,0:T(8,128)(2,1)}, u32[]{:S(2)}, u32[]{:S(2)}) %collective-permute-start.3) | collective-permute-done | bytes 524320 | tf_op jit(solution)/shard_map/ppermute | solution.py:113
  247.0 12.3 %collective-permute-done.6 = bf16[256,1024]{1,0:T(8,128)(2,1)S(1)} collective-permute-done((bf16[256,1024]{1,0:T(8,128)(2,1)S(1)}, bf16[256,1024]{1,0:T(8,128)(2,1)S(1)}, u32[]{:S(2)}, u32[]{:S(2)}) %collective-permute-start.6) | collective-permute-done | bytes 524320 | tf_op jit(solution)/shard_map/ppermute | solution.py:84
  260.7 13.2 %collective-permute-done.10 = bf16[256,1024]{1,0:T(8,128)(2,1)S(1)} collective-permute-done((bf16[256,1024]{1,0:T(8,128)(2,1)S(1)}, bf16[256,1024]{1,0:T(8,128)(2,1)S(1)}, u32[]{:S(2)}, u32[]{:S(2)}) %collective-permute-start.10) | collective-permute-done | bytes 524320 | tf_op jit(solution)/shard_map/ppermute | solution.py:84
  277.3 16.4 %fusion.39 = f32[1024,1024]{1,0:T(8,128)} fusion(bf16[1024,1024]{1,0:T(8,128)(2,1)S(1)} %copy-done, f32[1024]{0:T(1024)S(1)} %copy-done.23, bf16[1024,1024]{1,0:T(8,128)(2,1)} %param.19, bf16[256,1024]{1,0:T(8,128)(2,1)} %get-tuple-element.31, bf16[256,1024]{1,0:T(8,128)(2,1)} %get-tuple-element.32, bf16[256,1024]{1,0:T(8,128)(2,1)} %get-tuple-element.20, ...), kind=kOutput, calls=%fused_computation.80 | convolution fusion | flops 4372561920 | bytes 10489856 | tf_op jit(solution)/shard_map/dot_general | solution.py:200
  297.2 2.9 broadcast_select_fusion.13
  300.1 16.4 %fusion.37 = f32[1024,1024]{1,0:T(8,128)} fusion(bf16[1024,1024]{1,0:T(8,128)(2,1)S(1)} %copy-done, f32[1024]{0:T(1024)S(1)} %copy-done.23, bf16[1024,1024]{1,0:T(8,128)(2,1)} %param.19, bf16[256,1024]{1,0:T(8,128)(2,1)} %get-tuple-element.34, bf16[256,1024]{1,0:T(8,128)(2,1)} %get-tuple-element.35, bf16[256,1024]{1,0:T(8,128)(2,1)} %get-tuple-element.26, ...), kind=kOutput, calls=%fused_computation.79 | convolution fusion | flops 4372561920 | bytes 10489856 | tf_op jit(solution)/shard_map/dot_general | solution.py:200
  327.7 10.4 %collective-permute-done.9 = bf16[256,1024]{1,0:T(8,128)(2,1)} collective-permute-done((bf16[256,1024]{1,0:T(8,128)(2,1)}, bf16[256,1024]{1,0:T(8,128)(2,1)}, u32[]{:S(2)}, u32[]{:S(2)}) %collective-permute-start.9) | collective-permute-done | bytes 524320 | tf_op jit(solution)/shard_map/ppermute | solution.py:113
  339.6 9.2 %collective-permute-done.13 = bf16[256,1024]{1,0:T(8,128)(2,1)} collective-permute-done((bf16[256,1024]{1,0:T(8,128)(2,1)}, bf16[256,1024]{1,0:T(8,128)(2,1)}, u32[]{:S(2)}, u32[]{:S(2)}) %collective-permute-start.13) | collective-permute-done | bytes 524320 | tf_op jit(solution)/shard_map/ppermute | solution.py:113
  352.6 17.8 %reduce-scatter.2.cloned.1.call-done = f32[8,1024]{1,0:T(8,128)} async-done(((f32[32,1024]{1,0:T(8,128)}), f32[8,1024]{1,0:T(8,128)}) %reduce-scatter.2.cloned.1.call-update) | async-done | bytes 32784 | tf_op jit(solution)/shard_map/reduce_scatter | solution.py:211
  373.1 9.7 %all-to-all-start.2 = ((bf16[32,8,1024]{2,1,0:T(8,128)(2,1)}), bf16[32,8,1024]{2,1,0:T(8,128)(2,1)S(1)}, u32[]{:S(2)}, u32[]{:S(2)}) async-start(bf16[32,8,1024]{2,1,0:T(8,128)(2,1)} %broadcast_in_dim.33), calls=%async_computation.3 | async-start | bytes 1048576 | tf_op jit(solution)/shard_map/all_to_all | solution.py:217
  382.8 13.6 %all-to-all-done.2 = bf16[32,8,1024]{2,1,0:T(8,128)(2,1)S(1)} async-done(((bf16[32,8,1024]{2,1,0:T(8,128)(2,1)}), bf16[32,8,1024]{2,1,0:T(8,128)(2,1)S(1)}, u32[]{:S(2)}, u32[]{:S(2)}) %all-to-all-start.2) | async-done | bytes 524320 | tf_op jit(solution)/shard_map/all_to_all | solution.py:217
  396.5 3.5 convolution_multiply_fusion
  400.0 21.8 %select_reduce_fusion = f32[256,64]{1,0:T(8,128)S(1)} fusion(f32[256,2048]{1,0:T(8,128)S(1)} %convolution_multiply_fusion, s32[256,64]{1,0:T(8,128)S(1)} %broadcast_subtract_fusion), kind=kLoop, calls=%fused_computation.1 | loop fusion | flops 100646912 | bytes 2228224 | tf_op jit(solution)/shard_map/reduce_sum | solution.py:224
  421.9 13.8 %all_to_all.24 = f32[32,1,512]{2,1,0:T(1,128)S(1)} all-to-all(f32[32,1,512]{2,1,0:T(1,128)S(1)} %reshape.253), channel_id=1, replica_groups=mesh['dp'=32,'tensor'=4] {'dp'}, dimensions={0} | all-to-all | bytes 131072 | tf_op jit(solution)/shard_map/all_to_all | solution.py:228
  (157 shorter events, 83.8 us)
Async XLA Ops:
  6.5 270.8 %copy-start = (bf16[1024,1024]{1,0:T(8,128)(2,1)S(1)}, bf16[1024,1024]{1,0:T(8,128)(2,1)}, u32[]{:S(2)}) copy-start(bf16[1024,1024]{1,0:T(8,128)(2,1)} %param.21) | copy-start | bytes 6291460
  6.5 47.3 %copy-start.1 = (bf16[512,1024]{1,0:T(8,128)(2,1)S(1)}, bf16[512,1024]{1,0:T(8,128)(2,1)}, u32[]{:S(2)}) copy-start(bf16[512,1024]{1,0:T(8,128)(2,1)} %param.13) | copy-start | bytes 3145732
  6.5 16.8 %copy-start.21 = (s32[1,32]{1,0:T(1,128)S(1)}, s32[1,32]{1,0:T(1,128)}, u32[]{:S(2)}) copy-start(s32[1,32]{1,0:T(1,128)} %param.23) | copy-start | bytes 388
  6.5 47.3 %collective-permute-start = (bf16[512,1024]{1,0:T(8,128)(2,1)}, bf16[512,1024]{1,0:T(8,128)(2,1)}, u32[]{:S(2)}, u32[]{:S(2)}) collective-permute-start(bf16[512,1024]{1,0:T(8,128)(2,1)} %param.13), channel_id=1, source_target_pairs={{0,2},{2,0},{1,3},{3,1},{4,6},{6,4},{5,7},{7,5},{8,10},{10,8},{9,1... | collective-permute-start | bytes 3145736 | tf_op jit(solution)/shard_map/ppermute | solution.py:84
  12.8 50.8 %all-to-all-start.1 = ((bf16[32,64,512]{2,1,0:T(8,128)(2,1)}), bf16[32,64,512]{2,1,0:T(8,128)(2,1)}, u32[]{:S(2)}, u32[]{:S(2)}) async-start(bf16[32,64,512]{2,1,0:T(8,128)(2,1)} %broadcast_in_dim.30), calls=%async_computation.1 | async-start | bytes 4194304 | tf_op jit(solution)/shard_map/all_to_all | solution.py:156
  24.4 35.0 %copy-start.20 = (s32[32]{0:T(128)S(1)}, s32[32]{0:T(128)}, u32[]{:S(2)}) copy-start(s32[32]{0:T(128)} %param.24) | copy-start | bytes 388
  57.8 19.5 %collective-permute-start.1 = (bf16[2,512,1024]{2,1,0:T(8,128)(2,1)}, bf16[2,512,1024]{2,1,0:T(8,128)(2,1)}, u32[]{:S(2)}, u32[]{:S(2)}) collective-permute-start(bf16[2,512,1024]{2,1,0:T(8,128)(2,1)} %pad_maximum_fusion.1), channel_id=1, source_target_pairs={{0,1},{1,0},{2,3},{3,2},{4,5},{5,4},{6,7},{7,6},{8,9},{9,8},{10,11... | collective-permute-start | bytes 6291464 | tf_op jit(solution)/shard_map/ppermute | solution.py:88
  77.2 2.7 copy-start.22
  193.4 4.8 %copy-start.15 = (bf16[256,1024]{1,0:T(8,128)(2,1)S(1)}, bf16[256,1024]{1,0:T(8,128)(2,1)}, u32[]{:S(2)}) copy-start(bf16[256,1024]{1,0:T(8,128)(2,1)} %param.16) | copy-start | bytes 1572868
  193.4 4.8 %copy-start.16 = (bf16[2,2,256,256]{3,2,1,0:T(8,128)(2,1)S(1)}, bf16[2,2,256,256]{3,2,1,0:T(8,128)(2,1)}, u32[]{:S(2)}) copy-start(bf16[2,2,256,256]{3,2,1,0:T(8,128)(2,1)} %reshape.248) | copy-start | bytes 1572868
  197.7 4.3 copy-start.19
  197.7 15.6 %collective-permute-start.4 = (bf16[2,256,1024]{2,1,0:T(8,128)(2,1)}, bf16[2,256,1024]{2,1,0:T(8,128)(2,1)}, u32[]{:S(2)}, u32[]{:S(2)}) collective-permute-start(bf16[2,256,1024]{2,1,0:T(8,128)(2,1)} %fusion.50), channel_id=1, source_target_pairs={{0,1},{1,0},{2,3},{3,2},{4,5},{5,4},{6,7},{7,6},{8,9},{9,8},{10,11... | collective-permute-start | bytes 3145736 | tf_op jit(solution)/shard_map/ppermute | solution.py:109
  202.0 15.6 %collective-permute-start.2 = (bf16[2,256,1024]{2,1,0:T(8,128)(2,1)}, bf16[2,256,1024]{2,1,0:T(8,128)(2,1)}, u32[]{:S(2)}, u32[]{:S(2)}) collective-permute-start(bf16[2,256,1024]{2,1,0:T(8,128)(2,1)} %fusion.49), channel_id=1, source_target_pairs={{0,1},{1,0},{2,3},{3,2},{4,5},{5,4},{6,7},{7,6},{8,9},{9,8},{10,11... | collective-permute-start | bytes 3145736 | tf_op jit(solution)/shard_map/ppermute | solution.py:109
  202.8 20.4 %all-to-all-start = ((s32[32,1,512]{2,1,0:T(1,128)}), s32[32,1,512]{2,1,0:T(1,128)S(1)}, u32[]{:S(2)}, u32[]{:S(2)}) async-start(s32[32,1,512]{2,1,0:T(1,128)} %reshape.251), calls=%async_computation | async-start | bytes 131072 | tf_op jit(solution)/shard_map/all_to_all | solution.py:181
  213.2 157.2 %reduce-scatter.2.cloned.1.call-start = ((), (), s32[]{:S(2)}) async-start(), calls=%async_computation.5 | async-start | bytes 163840 | tf_op jit(solution)/shard_map/reduce_scatter | solution.py:211
  213.3 4.3 copy-start.4
  215.7 3.6 copy-start.8
  215.7 6.3 %copy-start.17 = (f32[2,1024]{1,0:T(2,128)S(1)}, f32[2,1024]{1,0:T(2,128)}, u32[]{:S(2)}) copy-start(f32[2,1024]{1,0:T(2,128)} %param.17) | copy-start | bytes 24580
  215.7 6.3 %copy-start.18 = (f32[2,1024]{1,0:T(2,128)S(1)}, f32[2,1024]{1,0:T(2,128)}, u32[]{:S(2)}) copy-start(f32[2,1024]{1,0:T(2,128)} %param.18) | copy-start | bytes 24580
  216.6 15.2 %collective-permute-start.5 = (bf16[256,1024]{1,0:T(8,128)(2,1)}, bf16[256,1024]{1,0:T(8,128)(2,1)}, u32[]{:S(2)}, u32[]{:S(2)}) collective-permute-start(bf16[256,1024]{1,0:T(8,128)(2,1)} %fusion.56), channel_id=1, source_target_pairs={{0,2},{2,0},{1,3},{3,1},{4,6},{6,4},{5,7},{7,5},{8,10},{10,8},{9,1... | collective-permute-start | bytes 1572872 | tf_op jit(solution)/shard_map/ppermute | solution.py:113
  220.8 21.6 %collective-permute-start.3 = (bf16[256,1024]{1,0:T(8,128)(2,1)}, bf16[256,1024]{1,0:T(8,128)(2,1)}, u32[]{:S(2)}, u32[]{:S(2)}) collective-permute-start(bf16[256,1024]{1,0:T(8,128)(2,1)} %fusion.55), channel_id=1, source_target_pairs={{0,2},{2,0},{1,3},{3,1},{4,6},{6,4},{5,7},{7,5},{8,10},{10,8},{9,1... | collective-permute-start | bytes 1572872 | tf_op jit(solution)/shard_map/ppermute | solution.py:113
  245.9 13.4 %collective-permute-start.6 = (bf16[256,1024]{1,0:T(8,128)(2,1)S(1)}, bf16[256,1024]{1,0:T(8,128)(2,1)S(1)}, u32[]{:S(2)}, u32[]{:S(2)}) collective-permute-start(bf16[256,1024]{1,0:T(8,128)(2,1)S(1)} %slice.103), channel_id=1, source_target_pairs={{0,2},{2,0},{1,3},{3,1},{4,6},{6,4},{5,7},{7,5},{8,10},{10,8},{9,1... | collective-permute-start | bytes 1572872 | tf_op jit(solution)/shard_map/ppermute | solution.py:84
  259.5 16.4 %collective-permute-start.7 = (bf16[2,256,1024]{2,1,0:T(8,128)(2,1)S(1)}, bf16[2,256,1024]{2,1,0:T(8,128)(2,1)S(1)}, u32[]{:S(2)}, u32[]{:S(2)}) collective-permute-start(bf16[2,256,1024]{2,1,0:T(8,128)(2,1)S(1)} %pad_maximum_fusion.3), channel_id=1, source_target_pairs={{0,1},{1,0},{2,3},{3,2},{4,5},{5,4},{6,7},{7,6},{8,9},{9,8},{10,11... | collective-permute-start | bytes 3145736 | tf_op jit(solution)/shard_map/ppermute | solution.py:88
  259.6 17.8 %copy-start.23 = (f32[1024]{0:T(1024)S(1)}, f32[1024]{0:T(1024)}, u32[]{:S(2)}) copy-start(f32[1024]{0:T(1024)} %param.20) | copy-start | bytes 12292
  259.6 14.3 %collective-permute-start.10 = (bf16[256,1024]{1,0:T(8,128)(2,1)S(1)}, bf16[256,1024]{1,0:T(8,128)(2,1)S(1)}, u32[]{:S(2)}, u32[]{:S(2)}) collective-permute-start(bf16[256,1024]{1,0:T(8,128)(2,1)S(1)} %get-tuple-element.33), channel_id=1, source_target_pairs={{0,2},{2,0},{1,3},{3,1},{4,6},{6,4},{5,7},{7,5},{8,10},{10,8},{9,1... | collective-permute-start | bytes 1572872 | tf_op jit(solution)/shard_map/ppermute | solution.py:84
  275.9 21.3 %collective-permute-start.11 = (bf16[2,256,1024]{2,1,0:T(8,128)(2,1)}, bf16[2,256,1024]{2,1,0:T(8,128)(2,1)}, u32[]{:S(2)}, u32[]{:S(2)}) collective-permute-start(bf16[2,256,1024]{2,1,0:T(8,128)(2,1)} %pad_maximum_fusion.4), channel_id=1, source_target_pairs={{0,1},{1,0},{2,3},{3,2},{4,5},{5,4},{6,7},{7,6},{8,9},{9,8},{10,11... | collective-permute-start | bytes 3145736 | tf_op jit(solution)/shard_map/ppermute | solution.py:88
  296.5 22.1 %collective-permute-start.8 = (bf16[2,256,1024]{2,1,0:T(8,128)(2,1)}, bf16[2,256,1024]{2,1,0:T(8,128)(2,1)}, u32[]{:S(2)}, u32[]{:S(2)}) collective-permute-start(bf16[2,256,1024]{2,1,0:T(8,128)(2,1)} %fusion.51), channel_id=1, source_target_pairs={{0,1},{1,0},{2,3},{3,2},{4,5},{5,4},{6,7},{7,6},{8,9},{9,8},{10,11... | collective-permute-start | bytes 3145736 | tf_op jit(solution)/shard_map/ppermute | solution.py:109
  316.5 7.5 %copy-start.14 = (f32[1024,1024]{1,0:T(8,128)S(1)}, f32[1024,1024]{1,0:T(8,128)}, u32[]{:S(2)}) copy-start(f32[1024,1024]{1,0:T(8,128)} %fusion.37) | copy-start | bytes 12582916
  318.4 5.6 %collective-permute-start.12 = (bf16[2,256,1024]{2,1,0:T(8,128)(2,1)S(1)}, bf16[2,256,1024]{2,1,0:T(8,128)(2,1)S(1)}, u32[]{:S(2)}, u32[]{:S(2)}) collective-permute-start(bf16[2,256,1024]{2,1,0:T(8,128)(2,1)S(1)} %fusion.52), channel_id=1, source_target_pairs={{0,1},{1,0},{2,3},{3,2},{4,5},{5,4},{6,7},{7,6},{8,9},{9,8},{10,11... | collective-permute-start | bytes 3145736 | tf_op jit(solution)/shard_map/ppermute | solution.py:109
  323.0 15.1 %collective-permute-start.9 = (bf16[256,1024]{1,0:T(8,128)(2,1)}, bf16[256,1024]{1,0:T(8,128)(2,1)}, u32[]{:S(2)}, u32[]{:S(2)}) collective-permute-start(bf16[256,1024]{1,0:T(8,128)(2,1)} %fusion.57), channel_id=1, source_target_pairs={{0,2},{2,0},{1,3},{3,1},{4,6},{6,4},{5,7},{7,5},{8,10},{10,8},{9,1... | collective-permute-start | bytes 1572872 | tf_op jit(solution)/shard_map/ppermute | solution.py:113
  326.6 22.2 %collective-permute-start.13 = (bf16[256,1024]{1,0:T(8,128)(2,1)}, bf16[256,1024]{1,0:T(8,128)(2,1)}, u32[]{:S(2)}, u32[]{:S(2)}) collective-permute-start(bf16[256,1024]{1,0:T(8,128)(2,1)} %fusion.58), channel_id=1, source_target_pairs={{0,2},{2,0},{1,3},{3,1},{4,6},{6,4},{5,7},{7,5},{8,10},{10,8},{9,1... | collective-permute-start | bytes 1572872 | tf_op jit(solution)/shard_map/ppermute | solution.py:113
  373.1 23.4 %all-to-all-start.2 = ((bf16[32,8,1024]{2,1,0:T(8,128)(2,1)}), bf16[32,8,1024]{2,1,0:T(8,128)(2,1)S(1)}, u32[]{:S(2)}, u32[]{:S(2)}) async-start(bf16[32,8,1024]{2,1,0:T(8,128)(2,1)} %broadcast_in_dim.33), calls=%async_computation.3 | async-start | bytes 1048576 | tf_op jit(solution)/shard_map/all_to_all | solution.py:217
  (10 other events, 15.9 us)
Sparse Core Ops, SparseCore 0:
  352.7 17.7 reduce-scatter.1

commit v8 on v7

--- a/solution.py
+++ b/solution.py
@@ -144,7 +144,7 @@
     columns = w_attn.shape[2]
     heads_here = columns // HEAD_DIM
     scale = HEAD_DIM ** (-0.5)
-    whole = gather_tensor(tokens)
+    whole = lax.all_gather(tokens, "tensor", axis=0, tiled=True)
     query = (jnp.dot(whole, w_attn[0], preferred_element_type=jnp.float32) * scale).astype(
         jnp.bfloat16
     )
@@ -175,7 +175,12 @@
             query, keys, values, prompt_key, prompt_value, seg, tok_group, ends, starts, prompt_len,
             HEAD_DIM, parity=parity, halves=2,
         )
-        return scatter_tensor(jnp.dot(context, w_out, preferred_element_type=jnp.float32), jnp.bfloat16)
+        return lax.psum_scatter(
+            jnp.dot(context, w_out, preferred_element_type=jnp.float32).astype(jnp.bfloat16),
+            "tensor",
+            scatter_dimension=0,
+            tiled=True,
+        ).astype(jnp.float32)
 
     attn_part = jnp.concatenate([attend_half(0), attend_half(1)], axis=0)
     asked_rows = lax.all_to_all(

time: 449 us -> 433 us (0.964)
  local copies, waits for them, and re-layouts: 62.8 us -> 41.2 us
  waiting for transfers between devices: 123 us -> 139 us
  matrix products: 65.1 us -> 56.5 us
  other arithmetic: 53.6 us -> 48.9 us
    ppermute x3 -> x2, waiting for transfers between devices: 54.9 us -> 28.5 us  [gather_tensor(): y = lax.ppermute(x, 'tensor', CROSS)]
    all_to_all x1, waiting for transfers between devices: 0.01 us -> 23.3 us  [shards(): lax.all_to_all(jnp.broadcast_to(own_kv[None], (n_dp,) + own_kv.shape), 'd...]
    all_gather x0 -> x1, waiting for transfers between devices: none -> 17.9 us  [shards(): whole = lax.all_gather(tokens, 'tensor', axis=0, tiled=True)]
    ppermute x4 -> x2, waiting for transfers between devices: 35.8 us -> 18.4 us  [scatter_tensor(): lax.ppermute(send.astype(link_dtype), 'tensor', CROSS).astype(jnp.float32)]
    dot_general x4 -> x0, local copies, waits for them, and re-layouts: 11.5 us -> none  [attend_half(): jnp.dot(context, w_out, preferred_element_type=jnp.float32)]
    reduce_scatter x0 -> x2, starting transfers between devices: none -> 9.99 us  [attend_half(): lax.psum_scatter(jnp.dot(context, w_out, preferred_element_type=jnp.float...]
    all_to_all x1, waiting for transfers between devices: 1.19 us -> 9.91 us  [shards(): lax.all_to_all(jnp.broadcast_to(candidates[None], (n_dp,) + candidates.sh...]
    reduce_scatter x0 -> x2, waiting for transfers between devices: none -> 8.46 us  [attend_half(): lax.psum_scatter(jnp.dot(context, w_out, preferred_element_type=jnp.float...]
  transfers between devices with their start and end apart: 18 -> 15, of which waited for: 10 -> 10; matrix products, arithmetic and copies ran while one was open for 20% -> 19% of each run, Pallas kernels for 0% -> 8%
where the time goes in v8:
time: 433 us; the launch traced here: 429 us
  waiting for transfers between devices  139 us (32%)
  Pallas kernels  71.6 us (17%)
  matrix products  56.5 us (13%)
  other arithmetic  48.9 us (11%)
  starting transfers between devices  44.1 us (10%)
  local copies, waits for them, and re-layouts  41.2 us (10%)
  between operations  14 us (3%)
  blocking collectives  13.8 us (3%)
    pallas_call x2, Pallas kernels, attention(): pl.pallas_call(functools.partial(attention_kernel, window=window), grid_s...  71.6 us
    dot_general x2, matrix products, feed_half(): jnp.dot(expanded, w_down, preferred_element_type=jnp.float32)  32.8 us
    ppermute x2, waiting for transfers between devices, gather_tensor(): y = lax.ppermute(x, 'tensor', CROSS)  28.5 us
    all_to_all x1, waiting for transfers between devices, shards(): lax.all_to_all(jnp.broadcast_to(own_kv[None], (n_dp,) + own_kv.shape), 'd...  23.3 us
    reduce_sum x1, other arithmetic, shards(): jnp.sum(jnp.where(local_rows[:, :, None] == row_ids[None, None, :], table...  21.8 us
    ppermute x2, waiting for transfers between devices, scatter_tensor(): lax.ppermute(send.astype(link_dtype), 'tensor', CROSS).astype(jnp.float32)  18.4 us
    reduce_scatter x1, waiting for transfers between devices, shards(): lax.psum_scatter(partial_sums, 'tensor', scatter_dimension=0, tiled=True)  18.2 us
    all_gather x1, waiting for transfers between devices, shards(): whole = lax.all_gather(tokens, 'tensor', axis=0, tiled=True)  17.9 us
  transfers between devices with their start and end apart: 15, of which 10 were waited for; matrix products, arithmetic and copies ran while one was open for 19% of the time, Pallas kernels for 8%

profile of v8, /device:TPU:0, one launch (start us, length us, event | category | flops | bytes accessed | tf_op | source)
XLA Modules:
  0.0 429.1 jit_solution(4199473247567435408)
XLA Ops:
  11.5 10.9 %all-to-all-start.1 = ((bf16[32,64,512]{2,1,0:T(8,128)(2,1)}), bf16[32,64,512]{2,1,0:T(8,128)(2,1)}, u32[]{:S(2)}, u32[]{:S(2)}) async-start(bf16[32,64,512]{2,1,0:T(8,128)(2,1)} %broadcast_in_dim.30), calls=%async_computation.1 | async-start | bytes 4194304 | tf_op jit(solution)/shard_map/all_to_all | solution.py:156
  28.8 23.3 %all-to-all-done.1 = bf16[32,64,512]{2,1,0:T(8,128)(2,1)} async-done(((bf16[32,64,512]{2,1,0:T(8,128)(2,1)}), bf16[32,64,512]{2,1,0:T(8,128)(2,1)}, u32[]{:S(2)}, u32[]{:S(2)}) %all-to-all-start.1) | async-done | bytes 2097184 | tf_op jit(solution)/shard_map/all_to_all | solution.py:156
  52.0 3.0 fusion.137
  61.6 17.9 %all-gather.2.cloned.1.call-done = bf16[2048,1024]{1,0:T(8,128)(2,1)} async-done(((bf16[512,1024]{1,0:T(8,128)(2,1)}), bf16[2048,1024]{1,0:T(8,128)(2,1)}) %all-gather.2.cloned.1.call-update) | async-done | bytes 4194320 | tf_op jit(solution)/shard_map/all_gather | solution.py:147
  79.6 3.6 convolution_convert_fusion
  85.0 3.6 convolution_convert_fusion.1
  90.4 3.6 fusion.20
  95.7 35.8 %shard_map.128 = bf16[4,1024,64]{2,1,0:T(8,128)(2,1)} custom-call(s32[4]{0:T(128)} %slice.75.first_ref, bf16[4,2048,64]{2,1,0:T(8,128)(2,1)} %bitcast.123, bf16[4,2048,64]{2,1,0:T(8,128)(2,1)} %bitcast.121, bf16[4,2048,64]{2,1,0:T(8,128)(2,1)} %bitcast.119, bf16[4,2048,64]{2,1,0:T(8,128)(2,1)} %bitcast.117, bf16[4,2048,64]{2,1,0:T(8,128)(2,1)} %bitcast.115, ...), custom_call_target="tpu_custom_call" | custom-call | tf_op jit(solution)/shard_map/pallas_call | solution.py:68
  135.2 9.9 %reduce-scatter.4.cloned.1.call-start = ((), (), s32[]{:S(2)}) async-start(), calls=%async_computation.8 | async-start | bytes 2621440 | tf_op jit(solution)/shard_map/reduce_scatter | solution.py:178
  145.8 35.8 %shard_map.127 = bf16[4,1024,64]{2,1,0:T(8,128)(2,1)} custom-call(s32[4]{0:T(128)} %slice.68.first_ref, bf16[4,2048,64]{2,1,0:T(8,128)(2,1)} %bitcast.124, bf16[4,2048,64]{2,1,0:T(8,128)(2,1)} %bitcast.122, bf16[4,2048,64]{2,1,0:T(8,128)(2,1)} %bitcast.120, bf16[4,2048,64]{2,1,0:T(8,128)(2,1)} %bitcast.118, bf16[4,2048,64]{2,1,0:T(8,128)(2,1)} %bitcast.116, ...), custom_call_target="tpu_custom_call" | custom-call | tf_op jit(solution)/shard_map/pallas_call | solution.py:68
  181.6 2.4 copy.56
  183.9 3.3 convolution_convert_fusion.3
  188.1 10.6 %all-to-all-start = ((s32[32,1,512]{2,1,0:T(1,128)}), s32[32,1,512]{2,1,0:T(1,128)S(1)}, u32[]{:S(2)}, u32[]{:S(2)}) async-start(s32[32,1,512]{2,1,0:T(1,128)} %reshape.244), calls=%async_computation | async-start | bytes 131072 | tf_op jit(solution)/shard_map/all_to_all | solution.py:186
  198.8 9.9 %all-to-all-done = s32[32,1,512]{2,1,0:T(1,128)S(1)} async-done(((s32[32,1,512]{2,1,0:T(1,128)}), s32[32,1,512]{2,1,0:T(1,128)S(1)}, u32[]{:S(2)}, u32[]{:S(2)}) %all-to-all-start) | async-done | bytes 65568 | tf_op jit(solution)/shard_map/all_to_all | solution.py:186
  210.2 8.4 %reduce-scatter.4.cloned.1.call-done = bf16[256,1024]{1,0:T(8,128)(2,1)} async-done(((bf16[1024,1024]{1,0:T(8,128)(2,1)}), bf16[256,1024]{1,0:T(8,128)(2,1)}) %reduce-scatter.4.cloned.1.call-update) | async-done | bytes 524304 | tf_op jit(solution)/shard_map/reduce_scatter | solution.py:178
  222.4 14.1 %collective-permute-done = bf16[256,1024]{1,0:T(8,128)(2,1)} collective-permute-done((bf16[256,1024]{1,0:T(8,128)(2,1)}, bf16[256,1024]{1,0:T(8,128)(2,1)}, u32[]{:S(2)}, u32[]{:S(2)}) %collective-permute-start) | collective-permute-done | bytes 524320 | tf_op jit(solution)/shard_map/ppermute | solution.py:84
  240.7 14.4 %collective-permute-done.4 = bf16[256,1024]{1,0:T(8,128)(2,1)} collective-permute-done((bf16[256,1024]{1,0:T(8,128)(2,1)}, bf16[256,1024]{1,0:T(8,128)(2,1)}, u32[]{:S(2)}, u32[]{:S(2)}) %collective-permute-start.4) | collective-permute-done | bytes 524320 | tf_op jit(solution)/shard_map/ppermute | solution.py:84
  258.1 2.7 broadcast_select_fusion.11
  260.8 16.4 %fusion.39 = f32[1024,1024]{1,0:T(8,128)} fusion(bf16[1024,1024]{1,0:T(8,128)(2,1)S(1)} %copy-done, f32[1024]{0:T(1024)S(1)} %copy-done.18, bf16[1024,1024]{1,0:T(8,128)(2,1)} %param.19, bf16[256,1024]{1,0:T(8,128)(2,1)} %get-tuple-element.23, bf16[256,1024]{1,0:T(8,128)(2,1)} %get-tuple-element.24, bf16[256,1024]{1,0:T(8,128)(2,1)} %get-tuple-element.12, ...), kind=kOutput, calls=%fused_computation.73 | convolution fusion | flops 4372561920 | bytes 10489856 | tf_op jit(solution)/shard_map/dot_general | solution.py:205
  277.2 2.7 fusion.49
  280.4 2.9 broadcast_select_fusion.7
  283.3 16.4 %fusion.37 = f32[1024,1024]{1,0:T(8,128)} fusion(bf16[1024,1024]{1,0:T(8,128)(2,1)S(1)} %copy-done, f32[1024]{0:T(1024)S(1)} %copy-done.18, bf16[1024,1024]{1,0:T(8,128)(2,1)} %param.19, bf16[256,1024]{1,0:T(8,128)(2,1)} %get-tuple-element.26, bf16[256,1024]{1,0:T(8,128)(2,1)} %get-tuple-element.27, bf16[256,1024]{1,0:T(8,128)(2,1)} %get-tuple-element.18, ...), kind=kOutput, calls=%fused_computation.72 | convolution fusion | flops 4372561920 | bytes 10489856 | tf_op jit(solution)/shard_map/dot_general | solution.py:205
  299.7 2.7 fusion.50
  302.5 2.4 bitcast_add_fusion.1
  313.1 9.1 %collective-permute-done.3 = bf16[256,1024]{1,0:T(8,128)(2,1)} collective-permute-done((bf16[256,1024]{1,0:T(8,128)(2,1)}, bf16[256,1024]{1,0:T(8,128)(2,1)}, u32[]{:S(2)}, u32[]{:S(2)}) %collective-permute-start.3) | collective-permute-done | bytes 524320 | tf_op jit(solution)/shard_map/ppermute | solution.py:113
  323.7 9.2 %collective-permute-done.7 = bf16[256,1024]{1,0:T(8,128)(2,1)} collective-permute-done((bf16[256,1024]{1,0:T(8,128)(2,1)}, bf16[256,1024]{1,0:T(8,128)(2,1)}, u32[]{:S(2)}, u32[]{:S(2)}) %collective-permute-start.7) | collective-permute-done | bytes 524320 | tf_op jit(solution)/shard_map/ppermute | solution.py:113
  336.8 18.2 %reduce-scatter.8.cloned.1.call-done = f32[8,1024]{1,0:T(8,128)} async-done(((f32[32,1024]{1,0:T(8,128)}), f32[8,1024]{1,0:T(8,128)}) %reduce-scatter.8.cloned.1.call-update) | async-done | bytes 32784 | tf_op jit(solution)/shard_map/reduce_scatter | solution.py:216
  357.6 9.6 %all-to-all-start.2 = ((bf16[32,8,1024]{2,1,0:T(8,128)(2,1)}), bf16[32,8,1024]{2,1,0:T(8,128)(2,1)S(1)}, u32[]{:S(2)}, u32[]{:S(2)}) async-start(bf16[32,8,1024]{2,1,0:T(8,128)(2,1)} %broadcast_in_dim.33), calls=%async_computation.5 | async-start | bytes 1048576 | tf_op jit(solution)/shard_map/all_to_all | solution.py:222
  367.3 13.6 %all-to-all-done.2 = bf16[32,8,1024]{2,1,0:T(8,128)(2,1)S(1)} async-done(((bf16[32,8,1024]{2,1,0:T(8,128)(2,1)}), bf16[32,8,1024]{2,1,0:T(8,128)(2,1)S(1)}, u32[]{:S(2)}, u32[]{:S(2)}) %all-to-all-start.2) | async-done | bytes 524320 | tf_op jit(solution)/shard_map/all_to_all | solution.py:222
  380.9 3.5 convolution_multiply_fusion
  384.4 21.8 %select_reduce_fusion = f32[256,64]{1,0:T(8,128)S(1)} fusion(f32[256,2048]{1,0:T(8,128)S(1)} %convolution_multiply_fusion, s32[256,64]{1,0:T(8,128)S(1)} %broadcast_subtract_fusion), kind=kLoop, calls=%fused_computation.1 | loop fusion | flops 100646912 | bytes 2228224 | tf_op jit(solution)/shard_map/reduce_sum | solution.py:229
  406.4 13.8 %all_to_all.24 = f32[32,1,512]{2,1,0:T(1,128)S(1)} all-to-all(f32[32,1,512]{2,1,0:T(1,128)S(1)} %reshape.246), channel_id=1, replica_groups=mesh['dp'=32,'tensor'=4] {'dp'}, dimensions={0} | all-to-all | bytes 131072 | tf_op jit(solution)/shard_map/all_to_all | solution.py:233
  (131 shorter events, 59.4 us)
Async XLA Ops:
  6.5 254.2 %copy-start = (bf16[1024,1024]{1,0:T(8,128)(2,1)S(1)}, bf16[1024,1024]{1,0:T(8,128)(2,1)}, u32[]{:S(2)}) copy-start(bf16[1024,1024]{1,0:T(8,128)(2,1)} %param.21) | copy-start | bytes 6291460
  6.5 73.0 %all-gather.2.cloned.1.call-start = ((), (), s32[]{:S(2)}) async-start(), calls=%async_computation.7 | async-start | bytes 5242880 | tf_op jit(solution)/shard_map/all_gather | solution.py:147
  7.3 15.2 %copy-start.17 = (s32[1,32]{1,0:T(1,128)S(1)}, s32[1,32]{1,0:T(1,128)}, u32[]{:S(2)}) copy-start(s32[1,32]{1,0:T(1,128)} %param.23) | copy-start | bytes 388
  8.6 16.1 %copy-start.16 = (s32[32]{0:T(128)S(1)}, s32[32]{0:T(128)}, u32[]{:S(2)}) copy-start(s32[32]{0:T(128)} %param.24) | copy-start | bytes 388
  11.5 40.5 %all-to-all-start.1 = ((bf16[32,64,512]{2,1,0:T(8,128)(2,1)}), bf16[32,64,512]{2,1,0:T(8,128)(2,1)}, u32[]{:S(2)}, u32[]{:S(2)}) async-start(bf16[32,64,512]{2,1,0:T(8,128)(2,1)} %broadcast_in_dim.30), calls=%async_computation.1 | async-start | bytes 4194304 | tf_op jit(solution)/shard_map/all_to_all | solution.py:156
  22.4 187.7 %reduce-scatter.6.cloned.1.call-start = ((), (), s32[]{:S(2)}) async-start(), calls=%async_computation.9 | async-start | bytes 2621440 | tf_op jit(solution)/shard_map/reduce_scatter | solution.py:178
  95.7 37.4 %copy-start.12 = (bf16[256,1024]{1,0:T(8,128)(2,1)S(1)}, bf16[256,1024]{1,0:T(8,128)(2,1)}, u32[]{:S(2)}) copy-start(bf16[256,1024]{1,0:T(8,128)(2,1)} %param.16) | copy-start | bytes 1572868
  135.2 83.4 %reduce-scatter.4.cloned.1.call-start = ((), (), s32[]{:S(2)}) async-start(), calls=%async_computation.8 | async-start | bytes 2621440 | tf_op jit(solution)/shard_map/reduce_scatter | solution.py:178
  181.6 5.8 %copy-start.15 = (s32[8,64]{1,0:T(8,128)S(1)}, s32[8,64]{1,0:T(8,128)}, u32[]{:S(2)}) copy-start(s32[8,64]{1,0:T(8,128)} %param.25) | copy-start | bytes 6148
  181.6 17.2 %copy-start.13 = (f32[2,1024]{1,0:T(2,128)S(1)}, f32[2,1024]{1,0:T(2,128)}, u32[]{:S(2)}) copy-start(f32[2,1024]{1,0:T(2,128)} %param.17) | copy-start | bytes 24580
  181.6 17.2 %copy-start.14 = (f32[2,1024]{1,0:T(2,128)S(1)}, f32[2,1024]{1,0:T(2,128)}, u32[]{:S(2)}) copy-start(f32[2,1024]{1,0:T(2,128)} %param.18) | copy-start | bytes 24580
  183.9 36.2 %copy-start.1 = (bf16[512,1024]{1,0:T(8,128)(2,1)S(1)}, bf16[512,1024]{1,0:T(8,128)(2,1)}, u32[]{:S(2)}) copy-start(bf16[512,1024]{1,0:T(8,128)(2,1)} %param.13) | copy-start | bytes 3145732
  188.1 20.7 %all-to-all-start = ((s32[32,1,512]{2,1,0:T(1,128)}), s32[32,1,512]{2,1,0:T(1,128)S(1)}, u32[]{:S(2)}, u32[]{:S(2)}) async-start(s32[32,1,512]{2,1,0:T(1,128)} %reshape.244), calls=%async_computation | async-start | bytes 131072 | tf_op jit(solution)/shard_map/all_to_all | solution.py:186
  198.7 156.2 %reduce-scatter.8.cloned.1.call-start = ((), (), s32[]{:S(2)}) async-start(), calls=%async_computation.10 | async-start | bytes 163840 | tf_op jit(solution)/shard_map/reduce_scatter | solution.py:216
  218.6 2.4 copy-start.2
  222.3 14.3 %collective-permute-start = (bf16[256,1024]{1,0:T(8,128)(2,1)}, bf16[256,1024]{1,0:T(8,128)(2,1)}, u32[]{:S(2)}, u32[]{:S(2)}) collective-permute-start(bf16[256,1024]{1,0:T(8,128)(2,1)} %slice.91), channel_id=1, source_target_pairs={{0,2},{2,0},{1,3},{3,1},{4,6},{6,4},{5,7},{7,5},{8,10},{10,8},{9,1... | collective-permute-start | bytes 1572872 | tf_op jit(solution)/shard_map/ppermute | solution.py:84
  238.5 1.9 copy-start.9
  240.4 17.7 %collective-permute-start.1 = (bf16[2,256,1024]{2,1,0:T(8,128)(2,1)}, bf16[2,256,1024]{2,1,0:T(8,128)(2,1)}, u32[]{:S(2)}, u32[]{:S(2)}) collective-permute-start(bf16[2,256,1024]{2,1,0:T(8,128)(2,1)} %pad_maximum_fusion), channel_id=1, source_target_pairs={{0,1},{1,0},{2,3},{3,2},{4,5},{5,4},{6,7},{7,6},{8,9},{9,8},{10,11... | collective-permute-start | bytes 3145736 | tf_op jit(solution)/shard_map/ppermute | solution.py:88
  240.4 14.7 %collective-permute-start.4 = (bf16[256,1024]{1,0:T(8,128)(2,1)}, bf16[256,1024]{1,0:T(8,128)(2,1)}, u32[]{:S(2)}, u32[]{:S(2)}) collective-permute-start(bf16[256,1024]{1,0:T(8,128)(2,1)} %get-tuple-element.25), channel_id=1, source_target_pairs={{0,2},{2,0},{1,3},{3,1},{4,6},{6,4},{5,7},{7,5},{8,10},{10,8},{9,1... | collective-permute-start | bytes 1572872 | tf_op jit(solution)/shard_map/ppermute | solution.py:84
  240.7 17.4 %copy-start.8 = (bf16[256,1024]{1,0:T(8,128)(2,1)S(1)}, bf16[256,1024]{1,0:T(8,128)(2,1)}, u32[]{:S(2)}) copy-start(bf16[256,1024]{1,0:T(8,128)(2,1)} %copy-done.7) | copy-start | bytes 1572868
  240.7 17.4 %copy-start.10 = (bf16[256,1024]{1,0:T(8,128)(2,1)S(1)}, bf16[256,1024]{1,0:T(8,128)(2,1)}, u32[]{:S(2)}) copy-start(bf16[256,1024]{1,0:T(8,128)(2,1)} %copy-done.9) | copy-start | bytes 1572868
  240.7 20.1 %copy-start.18 = (f32[1024]{0:T(1024)S(1)}, f32[1024]{0:T(1024)}, u32[]{:S(2)}) copy-start(f32[1024]{0:T(1024)} %param.20) | copy-start | bytes 12292
  256.2 1.9 copy-start.6
  258.1 22.3 %collective-permute-start.5 = (bf16[2,256,1024]{2,1,0:T(8,128)(2,1)}, bf16[2,256,1024]{2,1,0:T(8,128)(2,1)}, u32[]{:S(2)}, u32[]{:S(2)}) collective-permute-start(bf16[2,256,1024]{2,1,0:T(8,128)(2,1)} %pad_maximum_fusion.1), channel_id=1, source_target_pairs={{0,1},{1,0},{2,3},{3,2},{4,5},{5,4},{6,7},{7,6},{8,9},{9,8},{10,11... | collective-permute-start | bytes 3145736 | tf_op jit(solution)/shard_map/ppermute | solution.py:88
  279.9 22.6 %collective-permute-start.2 = (bf16[2,256,1024]{2,1,0:T(8,128)(2,1)}, bf16[2,256,1024]{2,1,0:T(8,128)(2,1)}, u32[]{:S(2)}, u32[]{:S(2)}) collective-permute-start(bf16[2,256,1024]{2,1,0:T(8,128)(2,1)} %fusion.49), channel_id=1, source_target_pairs={{0,1},{1,0},{2,3},{3,2},{4,5},{5,4},{6,7},{7,6},{8,9},{9,8},{10,11... | collective-permute-start | bytes 3145736 | tf_op jit(solution)/shard_map/ppermute | solution.py:109
  302.5 4.9 %collective-permute-start.6 = (bf16[2,256,1024]{2,1,0:T(8,128)(2,1)}, bf16[2,256,1024]{2,1,0:T(8,128)(2,1)}, u32[]{:S(2)}, u32[]{:S(2)}) collective-permute-start(bf16[2,256,1024]{2,1,0:T(8,128)(2,1)} %fusion.50), channel_id=1, source_target_pairs={{0,1},{1,0},{2,3},{3,2},{4,5},{5,4},{6,7},{7,6},{8,9},{9,8},{10,11... | collective-permute-start | bytes 3145736 | tf_op jit(solution)/shard_map/ppermute | solution.py:109
  302.5 4.9 %copy-start.11 = (f32[1024,1024]{1,0:T(8,128)S(1)}, f32[1024,1024]{1,0:T(8,128)}, u32[]{:S(2)}) copy-start(f32[1024,1024]{1,0:T(8,128)} %fusion.37) | copy-start | bytes 12582916
  304.8 1.3 copy-start.3
  307.1 15.1 %collective-permute-start.3 = (bf16[256,1024]{1,0:T(8,128)(2,1)}, bf16[256,1024]{1,0:T(8,128)(2,1)}, u32[]{:S(2)}, u32[]{:S(2)}) collective-permute-start(bf16[256,1024]{1,0:T(8,128)(2,1)} %fusion.53), channel_id=1, source_target_pairs={{0,2},{2,0},{1,3},{3,1},{4,6},{6,4},{5,7},{7,5},{8,10},{10,8},{9,1... | collective-permute-start | bytes 1572872 | tf_op jit(solution)/shard_map/ppermute | solution.py:113
  309.1 1.3 copy-start.4
  311.3 21.7 %collective-permute-start.7 = (bf16[256,1024]{1,0:T(8,128)(2,1)}, bf16[256,1024]{1,0:T(8,128)(2,1)}, u32[]{:S(2)}, u32[]{:S(2)}) collective-permute-start(bf16[256,1024]{1,0:T(8,128)(2,1)} %fusion.54), channel_id=1, source_target_pairs={{0,2},{2,0},{1,3},{3,1},{4,6},{6,4},{5,7},{7,5},{8,10},{10,8},{9,1... | collective-permute-start | bytes 1572872 | tf_op jit(solution)/shard_map/ppermute | solution.py:113
  357.6 23.3 %all-to-all-start.2 = ((bf16[32,8,1024]{2,1,0:T(8,128)(2,1)}), bf16[32,8,1024]{2,1,0:T(8,128)(2,1)S(1)}, u32[]{:S(2)}, u32[]{:S(2)}) async-start(bf16[32,8,1024]{2,1,0:T(8,128)(2,1)} %broadcast_in_dim.33), calls=%async_computation.5 | async-start | bytes 1048576 | tf_op jit(solution)/shard_map/all_to_all | solution.py:222
  (2 other events, 1.6 us)
Sparse Core Ops, SparseCore 0:
  9.0 70.5 all-gather.1
  135.4 30.4 reduce-scatter.5
  187.4 31.1 reduce-scatter.3
  336.8 18.0 reduce-scatter.7
